TPU v7x, 512 devices: a whole 4x4x16 slice. The times are simulated.
512 devices in a mesh: wide: 64 (over x, z), narrow: 8 (over y, core).
Axes of the slice: x: 4, y: 4, z: 16, core: 2. Of those that a mesh axis runs over, the one named last changes fastest.
Arguments:
- tokens: bfloat16 [49152, 2048], P('wide', 'narrow'), may hold values from -6 to 6
- norm_gain: float32 [2048], replicated, may hold values from 0.1 to 1.9
- qkv_weight: bfloat16 [2048, 3, 2048], P('wide', None, 'narrow'), may hold values from -0.125 to 0.125
- out_weight: bfloat16 [2048, 2048], P('wide', 'narrow'), may hold values from -0.25 to 0.25
- cache_pool: bfloat16 [1536, 128, 2, 2048], P('wide', None, None, 'narrow'), may hold values from -400 to 400, as said below
- prefix_pool: bfloat16 [2048, 2, 2048], P('wide', None, 'narrow'), may hold values from -6 to 6
- page_table: int32 [64, 24], P('wide'), may hold values from 0 to 23, each once within a row
- cache_len: int32 [64], P('wide'), may hold values from 512 to 3072
- group_ids: int32 [64], P('wide'), may hold values from 0 to 7, as said below
- group_pages: int32 [16], replicated, may hold values from 0 to 15, each once
Outputs:
- branch_out: bfloat16 [49152, 2048], P('wide', 'narrow')
- new_pages: bfloat16 [49152, 2, 2048], P('wide', None, 'narrow')
Inputs may be any that keep to these rules, and one draw needn't show every extreme that they name: `page_table`: each row is a permutation of the 24 pages of that request. `group_ids`: each group has 8 requests. `group_pages`: a permutation of the prefix pool's pages. `cache_pool`: keys are stored already rotated.
All inputs are finite; a program needn't handle non-finite values.
Results may differ from a plain program's by a relative error of at most 0.0095.
The roundings to bfloat16 on the way count: a program that leaves them out, or rounds other values in their place, can miss the bound.
Values may be sent and summed in bfloat16 or wider, within the bound.
No kernel may reach another device: no remote copies, remote signals or barrier semaphores. Data moves between devices by JAX's collectives and lax.ppermute only.
A program may use at most 128 MiB of HBM per device.

v0:
```python
import jax
import jax.numpy as jnp
from jax import lax
from jax.sharding import PartitionSpec as P

HEAD_DIM = 64
ROT = 16
PAGE = 128
KB = 4
PPAGES = 2


NEGATIVE = -1e30


def rotary(vectors, positions):
    half_rot = ROT // 2
    frequency = 10000.0 ** (-(jnp.arange(half_rot, dtype=jnp.float32) * 2.0 / ROT))
    angles = positions.astype(jnp.float32)[:, None] * frequency[None, :]
    cos_part = jnp.concatenate([jnp.cos(angles), jnp.cos(angles)], axis=1)[:, None, :]
    sine_part = jnp.concatenate([jnp.sin(angles), jnp.sin(angles)], axis=1)[:, None, :]
    rotated_in = vectors[..., :ROT]
    turned = jnp.concatenate([-rotated_in[..., half_rot:], rotated_in[..., :half_rot]], axis=-1)
    return jnp.concatenate(
        [rotated_in * cos_part + turned * sine_part, vectors[..., ROT:]], axis=-1
    )


def attend(running, queries, keys, values, key_valid):
    row_max, weight_sum, weighted = running
    scores = jnp.einsum("qhd,khd->hqk", queries, keys, preferred_element_type=jnp.float32) * 0.125
    scores = jnp.where(key_valid[None], scores, NEGATIVE)
    new_max = jnp.maximum(row_max, jnp.max(scores, axis=2))
    expo = jnp.where(key_valid[None], jnp.exp(scores - new_max[:, :, None]), 0.0)
    factor = jnp.exp(row_max - new_max)
    weight_sum = weight_sum * factor + jnp.sum(expo, axis=2)
    update = jnp.einsum(
        "hqk,khd->qhd", expo.astype(jnp.bfloat16), values, preferred_element_type=jnp.float32
    )
    weighted = weighted * jnp.transpose(factor)[:, :, None] + update
    return (new_max, weight_sum, weighted)


def local(
    tokens,
    norm_gain,
    qkv_weight,
    out_weight,
    cache_pool,
    prefix_pool,
    page_table,
    cache_len,
    group_ids,
    group_pages,
):
    span_rows = tokens.shape[0]
    local_width = qkv_weight.shape[2]
    heads_here = local_width // HEAD_DIM
    gathered = lax.all_gather(tokens, "narrow", axis=1, tiled=True)
    widened = gathered.astype(jnp.float32)
    row_mean = jnp.mean(widened, axis=1, keepdims=True)
    centered = widened - row_mean
    variance = jnp.mean(centered * centered, axis=1, keepdims=True)
    normed = (centered * lax.rsqrt(variance + 1e-05) * norm_gain).astype(jnp.bfloat16)
    piece_rows = lax.all_gather(qkv_weight, "wide", axis=0, tiled=True)
    piece_count = piece_rows.shape[0]
    columns = normed
    projected = jnp.dot(
        columns,
        piece_rows.reshape(piece_count, 3 * local_width),
        preferred_element_type=jnp.float32,
    )
    projected = projected.reshape(span_rows, 3, heads_here, HEAD_DIM)
    length = cache_len[0]
    offset = jnp.arange(span_rows, dtype=jnp.int32)
    positions = PPAGES * PAGE + length + offset
    queries = rotary(projected[:, 0], positions).astype(jnp.bfloat16)
    keys = rotary(projected[:, 1], positions).astype(jnp.bfloat16)
    values = projected[:, 2].astype(jnp.bfloat16)
    new_pages = jnp.stack(
        [keys.reshape(span_rows, local_width), values.reshape(span_rows, local_width)], axis=1
    )
    initial = (
        jnp.full((heads_here, span_rows), NEGATIVE, jnp.float32),
        jnp.zeros((heads_here, span_rows), jnp.float32),
        jnp.zeros((span_rows, heads_here, HEAD_DIM), jnp.float32),
    )
    running = attend(initial, queries, keys, values, offset[:, None] >= offset[None, :])
    my_group = group_ids[0]
    prefix_whole = lax.all_gather(prefix_pool, "wide", axis=0, tiled=True)
    prefix_pages = prefix_whole.reshape(-1, PAGE, 2, heads_here, HEAD_DIM)
    chosen = lax.dynamic_slice_in_dim(group_pages, my_group * PPAGES, PPAGES)
    key_rows = jnp.take(prefix_pages, chosen, axis=0).reshape(
        PPAGES * PAGE, 2, heads_here, HEAD_DIM
    )
    running = attend(
        running,
        queries,
        key_rows[:, 0],
        key_rows[:, 1],
        jnp.ones((span_rows, PPAGES * PAGE), dtype=bool),
    )
    page_list = page_table[0]
    block_keys = KB * PAGE
    blocks = (length + block_keys - 1) // block_keys
    key_offset = jnp.arange(block_keys, dtype=jnp.int32)

    def cache_block(block_index, state_now):
        page_ids = lax.dynamic_slice_in_dim(page_list, block_index * KB, KB)
        key_rows = jnp.take(cache_pool, page_ids, axis=0).reshape(
            block_keys, 2, heads_here, HEAD_DIM
        )
        key_valid = jnp.broadcast_to(
            (block_index * block_keys + key_offset < length)[None, :], (span_rows, block_keys)
        )
        return attend(state_now, queries, key_rows[:, 0], key_rows[:, 1], key_valid)

    running = lax.fori_loop(0, blocks, cache_block, running)
    head_values = (
        (running[2] / jnp.transpose(running[1])[:, :, None])
        .astype(jnp.bfloat16)
        .reshape(span_rows, local_width)
    )
    all_heads = lax.all_gather(head_values, "narrow", axis=1, tiled=True)
    columns = all_heads
    branch_out = jnp.dot(
        columns,
        lax.all_gather(out_weight, "wide", axis=0, tiled=True),
        preferred_element_type=jnp.float32,
    )
    return (branch_out.astype(jnp.bfloat16), new_pages)


def solution(mesh):
    placed = (
        P("wide", "narrow"),
        P(),
        P("wide", None, "narrow"),
        P("wide", "narrow"),
        P("wide", None, None, "narrow"),
        P("wide", None, "narrow"),
        P("wide", None),
        P("wide"),
        P("wide"),
        P(),
    )
    return jax.shard_map(
        local,
        mesh=mesh,
        in_specs=placed,
        out_specs=(P("wide", "narrow"), P("wide", None, "narrow")),
        check_vma=False,
    )
```

profile of v0, /device:TPU:1, one launch (start us, length us, event | category | flops | bytes accessed | tf_op | source)
XLA Modules:
  0.0 524.0 jit_solution(7641525677525579463)
XLA Ops:
  13.4 134.0 %all-gather.10.cloned.1.call-done = bf16[2048,2,256]{2,1,0:T(2,128)(2,1)} async-done(((bf16[32,2,256]{2,1,0:T(2,128)(2,1)}), bf16[2048,2,256]{2,1,0:T(2,128)(2,1)}) %all-gather.10.cloned.1.call-update) | async-done | bytes 2097168 | tf_op jit(solution)/shard_map/all_gather | solution.py:90
  147.3 8.8 %reshape.131 = bf16[16,128,2,4,64]{4,3,2,1,0:T(4,128)(2,1)} reshape(bf16[2048,2,256]{2,1,0:T(2,128)(2,1)} %all-gather.10.cloned.1.call-done) | data formatting | bytes 4194304 | tf_op jit(solution)/shard_map/reshape | solution.py:91
  156.2 5.8 %copy.32 = bf16[16,128,2,4,64]{1,4,3,2,0:T(8,128)(2,1)S(1)} copy(bf16[16,128,2,4,64]{4,3,2,1,0:T(4,128)(2,1)} %reshape.131) | data formatting | bytes 4194304 | tf_op jit(solution)/shard_map/reshape | solution.py:91
  162.6 31.8 %all-gather.6.cloned.1.call-done = bf16[768,2048]{1,0:T(8,128)(2,1)} async-done(((bf16[768,256]{1,0:T(8,128)(2,1)}), bf16[768,2048]{1,0:T(8,128)(2,1)}) %all-gather.6.cloned.1.call-update) | async-done | bytes 3145744 | tf_op jit(solution)/shard_map/all_gather | solution.py:59
  194.4 2.5 convert_reduce_fusion
  197.0 2.8 fusion.27
  199.8 132.6 %all-gather.8.cloned.1.call-done = bf16[2048,3,256]{2,0,1:T(8,128)(2,1)} async-done(((bf16[32,3,256]{2,0,1:T(8,128)(2,1)}), bf16[2048,3,256]{2,0,1:T(8,128)(2,1)}) %all-gather.8.cloned.1.call-update) | async-done | bytes 3145744 | tf_op jit(solution)/shard_map/all_gather | solution.py:65
  332.4 4.7 copy.30
  337.1 4.6 fusion.34
  343.3 1.8 fusion.22
  345.1 2.3 fusion.26
  347.4 2.8 fusion.57
  351.5 21.3 %while.15 = (s32[]{:T(128)}, f32[4,768]{1,0:T(4,128)S(1)}, f32[4,768]{1,0:T(4,128)S(1)}, f32[768,4,64]{0,2,1:T(8,128)S(1)}, s32[]{:T(128)}, /*index=5*/s32[]{:T(...) while((s32[]{:T(128)}, f32[4,768]{1,0:T(4,128)S(1)}, ...), condition=%wide.region_9.10_spmd.clone, body=%wide.region_6.9_spmd.clone.sunk | while | flops 423767072 | bytes 25763612 | solution.py:118
  352.4 3.5 gather_fusion
  358.4 2.0 fusion.90
  360.3 1.7 fusion.91
  362.9 3.5 gather_fusion
  367.5 1.4 bitcast_reduce_fusion.2
  368.9 2.0 fusion.90
  370.9 1.7 fusion.91
  376.1 2.7 pad_maximum_fusion
  378.8 90.2 %all-gather.14.cloned.1.call-done = bf16[2048,256]{1,0:T(8,128)(2,1)} async-done(((bf16[32,256]{1,0:T(8,128)(2,1)}), bf16[2048,256]{1,0:T(8,128)(2,1)}) %all-gather.14.cloned.1.call-update) | async-done | bytes 1048592 | tf_op jit(solution)/shard_map/all_gather | solution.py:128
  469.0 44.6 %all-gather.12.cloned.1.call-done = bf16[768,2048]{0,1:T(8,128)(2,1)} async-done(((bf16[768,256]{0,1:T(8,128)(2,1)}), bf16[768,2048]{0,1:T(8,128)(2,1)}) %all-gather.12.cloned.1.call-update) | async-done | bytes 3145744 | tf_op jit(solution)/shard_map/all_gather | solution.py:124
  513.6 3.9 convolution_convert_fusion
  (71 shorter events, 16.7 us)
Async XLA Ops:
  7.2 140.2 %all-gather.10.cloned.1.call-start = ((), (), s32[]{:S(2)}) async-start(), calls=%async_computation.2 | async-start | bytes 2129920 | tf_op jit(solution)/shard_map/all_gather | solution.py:90
  7.9 186.5 %all-gather.6.cloned.1.call-start = ((), (), s32[]{:S(2)}) async-start(), calls=%async_computation | async-start | bytes 3538944 | tf_op jit(solution)/shard_map/all_gather | solution.py:59
  8.6 323.8 %all-gather.8.cloned.1.call-start = ((), (), s32[]{:S(2)}) async-start(), calls=%async_computation.1 | async-start | bytes 3194880 | tf_op jit(solution)/shard_map/all_gather | solution.py:65
  9.4 459.6 %all-gather.14.cloned.1.call-start = ((), (), s32[]{:S(2)}) async-start(), calls=%async_computation.4 | async-start | bytes 1064960 | tf_op jit(solution)/shard_map/all_gather | solution.py:128
  10.0 503.6 %all-gather.12.cloned.1.call-start = ((), (), s32[]{:S(2)}) async-start(), calls=%async_computation.3 | async-start | bytes 3538944 | tf_op jit(solution)/shard_map/all_gather | solution.py:124
  162.6 174.6 %copy-start.4 = (f32[2048]{0:T(1024)S(1)}, f32[2048]{0:T(1024)}, u32[]{:S(2)}) copy-start(f32[2048]{0:T(1024)} %param.13) | copy-start | bytes 24580
  194.4 142.7 %copy-start = (bf16[768,2048]{1,0:T(8,128)(2,1)S(1)}, bf16[768,2048]{1,0:T(8,128)(2,1)}, u32[]{:S(2)}) copy-start(bf16[768,2048]{1,0:T(8,128)(2,1)} %all-gather.6.cloned.1.call-done) | copy-start | bytes 9437188
  341.8 5.7 %copy-start.2 = (f32[768,3,4,64]{0,3,2,1:T(8,128)}, f32[768,3,4,64]{0,3,2,1:T(8,128)S(1)}, u32[]{:S(2)}) copy-start(f32[768,3,4,64]{0,3,2,1:T(8,128)S(1)} %fusion.34) | copy-start | bytes 7077892
  341.8 1.5 copy-start.1
  350.2 1.3 copy-start.3
Sparse Core Ops, SparseCore 0:
  10.9 136.3 all-gather.9
  149.5 44.9 all-gather.5
  197.4 134.9 all-gather.7
  335.2 133.7 all-gather.13
  471.5 42.0 all-gather.11
where the time goes:
time: 525 us; the launch traced here: 524 us
  waiting for transfers between devices  436 us (83%)
  local copies, waits for them, and re-layouts  32.3 us (6%)
  matrix products  20.6 us (4%)
  other arithmetic  19.5 us (4%)
  between operations  15.3 us (3%)
    all_gather x1, waiting for transfers between devices, local(): prefix_whole = lax.all_gather(prefix_pool, 'wide', axis=0, tiled=True)  134 us
    all_gather x1, waiting for transfers between devices, local(): piece_rows = lax.all_gather(qkv_weight, 'wide', axis=0, tiled=True)  133 us
    all_gather x1, waiting for transfers between devices, local(): lax.all_gather(out_weight, 'wide', axis=0, tiled=True)  90.2 us
    all_gather x1, waiting for transfers between devices, local(): all_heads = lax.all_gather(head_values, 'narrow', axis=1, tiled=True)  44.6 us
    all_gather x1, waiting for transfers between devices, local(): gathered = lax.all_gather(tokens, 'narrow', axis=1, tiled=True)  31.8 us
    reshape x2, local copies, waits for them, and re-layouts, local(): prefix_pages = prefix_whole.reshape(-1, PAGE, 2, heads_here, HEAD_DIM)  14.6 us
  transfers between devices with their start and end apart: 5, of which 5 were waited for; matrix products, arithmetic and copies ran while one was open for 13% of the time, Pallas kernels for 0%

commit v1 on v0

--- a/solution.py
+++ b/solution.py
@@ -1,7 +1,7 @@
 import jax
 import jax.numpy as jnp
 from jax import lax
-from jax.sharding import PartitionSpec as P
+from jax.sharding import Mesh, PartitionSpec as P
 
 HEAD_DIM = 64
 ROT = 16
@@ -62,7 +62,21 @@
     centered = widened - row_mean
     variance = jnp.mean(centered * centered, axis=1, keepdims=True)
     normed = (centered * lax.rsqrt(variance + 1e-05) * norm_gain).astype(jnp.bfloat16)
-    piece_rows = lax.all_gather(qkv_weight, "wide", axis=0, tiled=True)
+    shard_rows = qkv_weight.shape[0]
+    merged = jnp.concatenate(
+        [
+            qkv_weight.reshape(shard_rows, 3 * local_width),
+            out_weight,
+            prefix_pool.reshape(shard_rows, 2 * local_width),
+        ],
+        axis=1,
+    )
+    by_x = lax.all_gather(merged, "wx", axis=0, tiled=False)
+    by_xz = lax.all_gather(by_x, "wz", axis=0, tiled=False)
+    merged_whole = jnp.transpose(by_xz, (1, 0, 2, 3)).reshape(-1, merged.shape[1])
+    piece_rows = merged_whole[:, : 3 * local_width]
+    out_rows = merged_whole[:, 3 * local_width : 4 * local_width]
+    prefix_whole = merged_whole[:, 4 * local_width :]
     piece_count = piece_rows.shape[0]
     columns = normed
     projected = jnp.dot(
@@ -87,7 +101,6 @@
     )
     running = attend(initial, queries, keys, values, offset[:, None] >= offset[None, :])
     my_group = group_ids[0]
-    prefix_whole = lax.all_gather(prefix_pool, "wide", axis=0, tiled=True)
     prefix_pages = prefix_whole.reshape(-1, PAGE, 2, heads_here, HEAD_DIM)
     chosen = lax.dynamic_slice_in_dim(group_pages, my_group * PPAGES, PPAGES)
     key_rows = jnp.take(prefix_pages, chosen, axis=0).reshape(
@@ -125,29 +138,40 @@
     columns = all_heads
     branch_out = jnp.dot(
         columns,
-        lax.all_gather(out_weight, "wide", axis=0, tiled=True),
+        out_rows,
         preferred_element_type=jnp.float32,
     )
     return (branch_out.astype(jnp.bfloat16), new_pages)
 
 
+def split_mesh(mesh):
+    grid = mesh.devices
+    try:
+        along_x = len({device.coords[0] for device in grid[:, 0]})
+    except (AttributeError, TypeError):
+        along_x = 4
+    shape = (along_x, grid.shape[0] // along_x, grid.shape[1])
+    return Mesh(grid.reshape(shape), ("wx", "wz", "narrow"))
+
+
 def solution(mesh):
+    W = ("wx", "wz")
     placed = (
-        P("wide", "narrow"),
+        P(W, "narrow"),
         P(),
-        P("wide", None, "narrow"),
-        P("wide", "narrow"),
-        P("wide", None, None, "narrow"),
-        P("wide", None, "narrow"),
-        P("wide", None),
-        P("wide"),
-        P("wide"),
+        P(W, None, "narrow"),
+        P(W, "narrow"),
+        P(W, None, None, "narrow"),
+        P(W, None, "narrow"),
+        P(W, None),
+        P(W),
+        P(W),
         P(),
     )
     return jax.shard_map(
         local,
-        mesh=mesh,
+        mesh=split_mesh(mesh),
         in_specs=placed,
-        out_specs=(P("wide", "narrow"), P("wide", None, "narrow")),
+        out_specs=(P(W, "narrow"), P(W, None, "narrow")),
         check_vma=False,
     )

time: 525 us -> 283 us (0.54)
  waiting for transfers between devices: 436 us -> 179 us
  blocking collectives: 0 us -> 11.5 us
    all_gather x3 -> x1, waiting for transfers between devices: 357 us -> 80.5 us  [local(): by_xz = lax.all_gather(by_x, 'wz', axis=0, tiled=False)]
    all_gather x1, waiting for transfers between devices: 44.6 us -> 68.3 us  [local(): all_heads = lax.all_gather(head_values, 'narrow', axis=1, tiled=True)]
    all_gather x0 -> x1, blocking collectives: none -> 11.5 us  [local(): by_x = lax.all_gather(merged, 'wx', axis=0, tiled=False)]
  transfers between devices with their start and end apart: 5 -> 3, of which waited for: 5 -> 3; matrix products, arithmetic and copies ran while one was open for 13% -> 5% of each run, Pallas kernels for 0% -> 0%
where the time goes in v1:
time: 283 us; the launch traced here: 282 us
  waiting for transfers between devices  179 us (63%)
  local copies, waits for them, and re-layouts  29.8 us (11%)
  other arithmetic  23.7 us (8%)
  matrix products  22.6 us (8%)
  between operations  15.4 us (5%)
  blocking collectives  11.5 us (4%)
    all_gather x1, waiting for transfers between devices, local(): by_xz = lax.all_gather(by_x, 'wz', axis=0, tiled=False)  80.5 us
    all_gather x1, waiting for transfers between devices, local(): all_heads = lax.all_gather(head_values, 'narrow', axis=1, tiled=True)  68.3 us
    all_gather x1, waiting for transfers between devices, local(): gathered = lax.all_gather(tokens, 'narrow', axis=1, tiled=True)  29.4 us
    all_gather x1, blocking collectives, local(): by_x = lax.all_gather(merged, 'wx', axis=0, tiled=False)  11.5 us
    reshape x2, local copies, waits for them, and re-layouts, local(): prefix_pages = prefix_whole.reshape(-1, PAGE, 2, heads_here, HEAD_DIM)  9.59 us
    gather x6, local copies, waits for them, and re-layouts, cache_block(): jnp.take(cache_pool, page_ids, axis=0)  9.05 us
    dot_general x4, matrix products, attend(): jnp.einsum('hqk,khd->qhd', expo.astype(jnp.bfloat16), values, preferred_e...  8 us
    dot_general x4, matrix products, attend(): jnp.einsum('qhd,khd->hqk', queries, keys, preferred_element_type=jnp.floa...  7.41 us
  transfers between devices with their start and end apart: 3, of which 3 were waited for; matrix products, arithmetic and copies ran while one was open for 5% of the time, Pallas kernels for 0%

profile of v1, /device:TPU:1, one launch (start us, length us, event | category | flops | bytes accessed | tf_op | source)
XLA Modules:
  0.0 282.5 jit_solution(11927093459664081095)
XLA Ops:
  10.2 11.5 %all-gather = bf16[128,1536]{1,0:T(8,128)(2,1)} all-gather(bf16[32,1536]{1,0:T(8,128)(2,1)S(1)} %pad_maximum_fusion.2), channel_id=2, replica_groups=mesh['wx'=4,'wz'=16,'narrow'=8] {'wx'}, dimensions={0}, use_global_device_ids=true | all-gather | bytes 491520 | tf_op jit(solution)/shard_map/all_gather | solution.py:74
  25.3 29.4 %all-gather.6.cloned.1.call-done = bf16[768,2048]{1,0:T(8,128)(2,1)} async-done(((bf16[768,256]{1,0:T(8,128)(2,1)}), bf16[768,2048]{1,0:T(8,128)(2,1)}) %all-gather.6.cloned.1.call-update) | async-done | bytes 3145744 | tf_op jit(solution)/shard_map/all_gather | solution.py:59
  54.6 2.4 convert_reduce_fusion
  57.0 2.8 %fusion.27 = f32[768]{0:T(1024)S(1)} fusion(bf16[768,2048]{1,0:T(8,128)(2,1)} %all-gather.6.cloned.1.call-done, f32[768]{0:T(1024)S(1)} %broadcast_multiply_fusion), kind=kLoop, calls=%fused_computation.40 | loop fusion | flops 6290688 | bytes 3151872 | tf_op jit(solution)/shard_map/reduce_sum | solution.py:63
  59.9 80.5 %all-gather.10.cloned.1.call-done = bf16[64,32,1536]{2,1,0:T(8,128)(2,1)} async-done(((bf16[4,32,1536]{2,1,0:T(8,128)(2,1)}), bf16[64,32,1536]{2,1,0:T(8,128)(2,1)}) %all-gather.10.cloned.1.call-update) | async-done | bytes 6291472 | tf_op jit(solution)/shard_map/all_gather | solution.py:75
  140.4 3.7 %copy.42 = bf16[4,16,32,1536]{3,2,1,0:T(8,128)(2,1)S(1)} copy(bf16[4,16,32,1536]{3,2,0,1:T(8,128)(2,1)} %bitcast.117) | data formatting | bytes 12582912 | tf_op jit(solution)/shard_map/transpose | solution.py:76
  144.1 3.2 %fusion.33 = f32[768,768]{0,1:T(8,128)S(1)} fusion(bf16[768,2048]{1,0:T(8,128)(2,1)S(1)} %copy-done, bf16[2048,1536]{1,0:T(8,128)(2,1)S(1)} %bitcast.114, f32[2048]{0:T(1024)S(1)} %copy-done.11, f32[768]{0:T(1024)S(1)} %add_rsqrt_fusion, f32[768]{0:T(1024)S(1)} %broadcast_multiply_fusion), kind=kOutput, calls=%fused_computation.45 | convolution fusion | flops 2423783424 | bytes 8667136 | tf_op jit(solution)/shard_map/dot_general | solution.py:82
  150.1 3.8 %reshape.142 = bf16[16,128,2,4,64]{4,3,2,1,0:T(4,128)(2,1)} reshape(bf16[2048,512]{1,0:T(8,128)(2,1)S(1)} %slice.94) | data formatting | bytes 4194304 | tf_op jit(solution)/shard_map/reshape | solution.py:104
  153.9 5.8 %copy.44 = bf16[16,128,2,4,64]{1,4,3,2,0:T(8,128)(2,1)S(1)} copy(bf16[16,128,2,4,64]{4,3,2,1,0:T(4,128)(2,1)} %reshape.142) | data formatting | bytes 4194304 | tf_op jit(solution)/shard_map/reshape | solution.py:104
  163.0 1.6 multiply_reduce_fusion
  165.6 3.1 %fusion.22 = (f32[4,768]{1,0:T(4,128)S(1)}, f32[4,768,768]{1,2,0:T(8,128)S(1)}) fusion(pred[768,768]{0,1:T(8,128)(4,1)} %iota_compare_fusion, bf16[768,4,48]{0,2,1:T(8,128)(2,1)} %slice.126, bf16[768,4,16]{0,2,1:T(8,128)(2,1)} %copy-done.6, bf16[768,4,48]{0,2,1:T(8,128)(2,1)} %slice.93, bf16[768,4,16]{0,2,1:T(8,128)(2,1)S(1)} %fusion.62), kind=kOutput, calls=%fused_computation.33 | convolution fusion | flops 310637568 | bytes 10825728 | tf_op jit(solution)/shard_map/qhd,khd->hqk/dot_general | solution.py:31
  168.8 2.3 fusion.26
  171.1 4.0 %fusion.57 = f32[768,4,64]{0,2,1:T(8,128)S(1)} fusion(f32[4,768,768]{1,2,0:T(8,128)S(1)} %get-tuple-element.118, f32[4,768]{1,0:T(4,128)S(1)} %get-tuple-element.113, pred[768,768]{0,1:T(8,128)(4,1)S(1)} %copy-done.3, f32[768,4]{0,1:T(4,128)S(1)} %get-tuple-element.112, f32[768,4]{0,1:T(4,128)S(1)} %get-tuple-element.111, f32[768,3,4,64]{0,3,2,1:T(8,128)} %bitcast.119), kind=kOutput, calls=%fused_computation.62 | convolution fusion | flops 314179584 | bytes 11243520 | tf_op jit(solution)/shard_map/hqk,khd->qhd/dot_general | solution.py:37
  176.3 21.3 %while.15 = (s32[]{:T(128)}, f32[4,768]{1,0:T(4,128)S(1)}, f32[4,768]{1,0:T(4,128)S(1)}, f32[768,4,64]{0,2,1:T(8,128)S(1)}, s32[]{:T(128)}, /*index=5*/s32[]{:T(...) while((s32[]{:T(128)}, f32[4,768]{1,0:T(4,128)S(1)}, ...), condition=%wide.region_9.10_spmd.clone, body=%wide.region_6.9_spmd.clone.sunk | while | flops 423767072 | bytes 25763612 | solution.py:131
  177.2 3.5 %gather_fusion = bf16[4,128,2,256]{3,2,1,0:T(2,128)(2,1)S(1)} fusion(bf16[24,128,2,256]{3,2,1,0:T(2,128)(2,1)} %get-tuple-element.228, s32[1024]{0:T(1024)S(1)} %pad_clamp_fusion.3), kind=kCustom, calls=%fused_computation.clone.clone.1 | custom fusion | bytes 1048592 | tf_op jit(solution)/shard_map/while/body/jit(_take)/gather | solution.py:123
  181.8 1.4 bitcast_reduce_fusion.2
  183.2 2.0 fusion.89
  185.2 1.7 fusion.90
  187.8 3.5 %gather_fusion = bf16[4,128,2,256]{3,2,1,0:T(2,128)(2,1)S(1)} fusion(bf16[24,128,2,256]{3,2,1,0:T(2,128)(2,1)} %get-tuple-element.228, s32[1024]{0:T(1024)S(1)} %pad_clamp_fusion.3), kind=kCustom, calls=%fused_computation.clone.clone.1 | custom fusion | bytes 1048592 | tf_op jit(solution)/shard_map/while/body/jit(_take)/gather | solution.py:123
  193.8 2.0 fusion.89
  195.7 1.7 fusion.90
  201.0 2.7 pad_maximum_fusion
  203.7 68.3 %all-gather.8.cloned.1.call-done = bf16[768,2048]{0,1:T(8,128)(2,1)} async-done(((bf16[768,256]{0,1:T(8,128)(2,1)}), bf16[768,2048]{0,1:T(8,128)(2,1)}) %all-gather.8.cloned.1.call-update) | async-done | bytes 3145744 | tf_op jit(solution)/shard_map/all_gather | solution.py:137
  272.0 3.9 %convolution_convert_fusion = bf16[768,256]{1,0:T(8,128)(2,1)} fusion(bf16[768,2048]{0,1:T(8,128)(2,1)} %all-gather.8.cloned.1.call-done, bf16[2048,1536]{1,0:T(8,128)(2,1)} %bitcast.116), kind=kOutput, calls=%fused_computation.63 | convolution fusion | flops 805502976 | bytes 4587520 | tf_op jit(solution)/shard_map/dot_general | solution.py:139
  (84 shorter events, 22.1 us)
Async XLA Ops:
  7.2 47.5 %all-gather.6.cloned.1.call-start = ((), (), s32[]{:S(2)}) async-start(), calls=%async_computation | async-start | bytes 3538944 | tf_op jit(solution)/shard_map/all_gather | solution.py:59
  7.9 132.5 %all-gather.10.cloned.1.call-start = ((), (), s32[]{:S(2)}) async-start(), calls=%async_computation.2 | async-start | bytes 6684672 | tf_op jit(solution)/shard_map/all_gather | solution.py:75
  21.8 250.2 %all-gather.8.cloned.1.call-start = ((), (), s32[]{:S(2)}) async-start(), calls=%async_computation.1 | async-start | bytes 3538944 | tf_op jit(solution)/shard_map/all_gather | solution.py:137
  24.1 135.6 %copy-start.7 = (f32[768,16]{0,1:T(8,128)}, f32[768,16]{0,1:T(8,128)S(1)}, u32[]{:S(2)}) copy-start(f32[768,16]{0,1:T(8,128)S(1)} %get-tuple-element.123) | copy-start | bytes 147460
  24.1 135.6 %copy-start.8 = (f32[768,16]{0,1:T(8,128)}, f32[768,16]{0,1:T(8,128)S(1)}, u32[]{:S(2)}) copy-start(f32[768,16]{0,1:T(8,128)S(1)} %get-tuple-element.124) | copy-start | bytes 147460
  140.4 3.7 %copy-start = (bf16[768,2048]{1,0:T(8,128)(2,1)S(1)}, bf16[768,2048]{1,0:T(8,128)(2,1)}, u32[]{:S(2)}) copy-start(bf16[768,2048]{1,0:T(8,128)(2,1)} %all-gather.6.cloned.1.call-done) | copy-start | bytes 9437188
  140.4 3.7 %copy-start.11 = (f32[2048]{0:T(1024)S(1)}, f32[2048]{0:T(1024)}, u32[]{:S(2)}) copy-start(f32[2048]{0:T(1024)} %param.13) | copy-start | bytes 24580
  144.0 5.9 %copy-start.1 = (bf16[4,16,32,1536]{3,2,1,0:T(8,128)(2,1)}, bf16[4,16,32,1536]{3,2,1,0:T(8,128)(2,1)S(1)}, u32[]{:S(2)}) copy-start(bf16[4,16,32,1536]{3,2,1,0:T(8,128)(2,1)S(1)} %copy.42) | copy-start | bytes 18874372
  147.3 2.6 copy-start.4
  147.5 1.7 copy-start.2
  153.9 5.8 %copy-start.9 = (f32[768,4,8]{0,2,1:T(8,128)S(1)}, f32[768,4,8]{0,2,1:T(8,128)}, u32[]{:S(2)}) copy-start(f32[768,4,8]{0,2,1:T(8,128)} %get-tuple-element.122) | copy-start | bytes 294916
  160.7 0.6 copy-start.6
  164.6 4.2 %copy-start.3 = (pred[768,768]{0,1:T(8,128)(4,1)S(1)}, pred[768,768]{0,1:T(8,128)(4,1)}, u32[]{:S(2)}) copy-start(pred[768,768]{0,1:T(8,128)(4,1)} %iota_compare_fusion) | copy-start | bytes 1769476
  175.1 1.3 copy-start.10
  176.3 24.0 %copy-start.5 = (bf16[768,4,48]{0,2,1:T(8,128)(2,1)S(1)}, bf16[768,4,48]{0,2,1:T(8,128)(2,1)}, u32[]{:S(2)}) copy-start(bf16[768,4,48]{0,2,1:T(8,128)(2,1)} %slice.93) | copy-start | bytes 884740
Sparse Core Ops, SparseCore 0:
  10.1 44.4 all-gather.5
  56.7 83.6 all-gather.9
  198.6 73.3 all-gather.7

commit v2 on v1

--- a/solution.py
+++ b/solution.py
@@ -114,21 +114,25 @@
         jnp.ones((span_rows, PPAGES * PAGE), dtype=bool),
     )
     page_list = page_table[0]
+    page_count = cache_pool.shape[0]
+    slot_of_page = (
+        jnp.zeros((page_count,), jnp.int32)
+        .at[page_list]
+        .set(jnp.arange(page_count, dtype=jnp.int32))
+    )
     block_keys = KB * PAGE
-    blocks = (length + block_keys - 1) // block_keys
     key_offset = jnp.arange(block_keys, dtype=jnp.int32)
 
     def cache_block(block_index, state_now):
-        page_ids = lax.dynamic_slice_in_dim(page_list, block_index * KB, KB)
-        key_rows = jnp.take(cache_pool, page_ids, axis=0).reshape(
+        key_rows = lax.dynamic_slice_in_dim(cache_pool, block_index * KB, KB, axis=0).reshape(
             block_keys, 2, heads_here, HEAD_DIM
         )
-        key_valid = jnp.broadcast_to(
-            (block_index * block_keys + key_offset < length)[None, :], (span_rows, block_keys)
-        )
+        slots = lax.dynamic_slice_in_dim(slot_of_page, block_index * KB, KB)
+        key_slot = jnp.repeat(slots, PAGE) * PAGE + key_offset % PAGE
+        key_valid = jnp.broadcast_to((key_slot < length)[None, :], (span_rows, block_keys))
         return attend(state_now, queries, key_rows[:, 0], key_rows[:, 1], key_valid)
 
-    running = lax.fori_loop(0, blocks, cache_block, running)
+    running = lax.fori_loop(0, page_count // KB, cache_block, running)
     head_values = (
         (running[2] / jnp.transpose(running[1])[:, :, None])
         .astype(jnp.bfloat16)

time: 283 us -> 275 us (0.972)
  waiting for transfers between devices: 179 us -> 140 us
  matrix products: 22.6 us -> 34.7 us
  other arithmetic: 23.7 us -> 35.5 us
  local copies, waits for them, and re-layouts: 29.8 us -> 35.9 us
    all_gather x1, waiting for transfers between devices: 68.3 us -> 30.6 us  [local(): all_heads = lax.all_gather(head_values, 'narrow', axis=1, tiled=True)]
    dynamic_slice x0 -> x12, local copies, waits for them, and re-layouts: none -> 13.5 us  [cache_block(): lax.dynamic_slice_in_dim(cache_pool, block_index * KB, KB, axis=0)]
    gather x6 -> x0, local copies, waits for them, and re-layouts: 9.05 us -> none  [cache_block(): jnp.take(cache_pool, page_ids, axis=0)]
    reduce_sum x4 -> x8, other arithmetic: 6.81 us -> 14.7 us  [attend(): weight_sum = weight_sum * factor + jnp.sum(expo, axis=2)]
    dot_general x4 -> x8, matrix products: 8 us -> 14.7 us  [attend(): jnp.einsum('hqk,khd->qhd', expo.astype(jnp.bfloat16), values, preferred_e...]
    dot_general x4 -> x8, matrix products: 7.41 us -> 12.8 us  [attend(): jnp.einsum('qhd,khd->hqk', queries, keys, preferred_element_type=jnp.floa...]
    lt x2 -> x6, other arithmetic: 1.34 us -> 4.31 us  [cache_block(): key_slot < length]
  transfers between devices with their start and end apart: 3 -> 3, of which waited for: 3 -> 3; matrix products, arithmetic and copies ran while one was open for 5% -> 6% of each run, Pallas kernels for 0% -> 0%
where the time goes in v2:
time: 275 us; the launch traced here: 274 us
  waiting for transfers between devices  140 us (51%)
  local copies, waits for them, and re-layouts  35.9 us (13%)
  other arithmetic  35.5 us (13%)
  matrix products  34.7 us (13%)
  between operations  15.3 us (6%)
  blocking collectives  11.5 us (4%)
    all_gather x1, waiting for transfers between devices, local(): by_xz = lax.all_gather(by_x, 'wz', axis=0, tiled=False)  80.5 us
    all_gather x1, waiting for transfers between devices, local(): all_heads = lax.all_gather(head_values, 'narrow', axis=1, tiled=True)  30.6 us
    all_gather x1, waiting for transfers between devices, local(): gathered = lax.all_gather(tokens, 'narrow', axis=1, tiled=True)  28.1 us
    dot_general x8, matrix products, attend(): jnp.einsum('hqk,khd->qhd', expo.astype(jnp.bfloat16), values, preferred_e...  14.7 us
    reduce_sum x8, other arithmetic, attend(): weight_sum = weight_sum * factor + jnp.sum(expo, axis=2)  14.7 us
    dynamic_slice x12, local copies, waits for them, and re-layouts, cache_block(): lax.dynamic_slice_in_dim(cache_pool, block_index * KB, KB, axis=0)  13.5 us
    dot_general x8, matrix products, attend(): jnp.einsum('qhd,khd->hqk', queries, keys, preferred_element_type=jnp.floa...  12.8 us
    all_gather x1, blocking collectives, local(): by_x = lax.all_gather(merged, 'wx', axis=0, tiled=False)  11.5 us
  transfers between devices with their start and end apart: 3, of which 3 were waited for; matrix products, arithmetic and copies ran while one was open for 6% of the time, Pallas kernels for 0%

profile of v2, /device:TPU:1, one launch (start us, length us, event | category | flops | bytes accessed | tf_op | source)
XLA Modules:
  0.0 273.6 jit_solution(4988635492245585786)
XLA Ops:
  10.2 11.5 %all-gather = bf16[128,1536]{1,0:T(8,128)(2,1)} all-gather(bf16[32,1536]{1,0:T(8,128)(2,1)S(1)} %pad_maximum_fusion.2), channel_id=2, replica_groups=mesh['wx'=4,'wz'=16,'narrow'=8] {'wx'}, dimensions={0}, use_global_device_ids=true | all-gather | bytes 491520 | tf_op jit(solution)/shard_map/all_gather | solution.py:74
  26.6 28.1 %all-gather.6.cloned.1.call-done = bf16[768,2048]{1,0:T(8,128)(2,1)} async-done(((bf16[768,256]{1,0:T(8,128)(2,1)}), bf16[768,2048]{1,0:T(8,128)(2,1)}) %all-gather.6.cloned.1.call-update) | async-done | bytes 3145744 | tf_op jit(solution)/shard_map/all_gather | solution.py:59
  54.6 2.4 convert_reduce_fusion
  57.0 2.8 %fusion.33 = f32[768]{0:T(1024)S(1)} fusion(bf16[768,2048]{1,0:T(8,128)(2,1)} %all-gather.6.cloned.1.call-done, f32[768]{0:T(1024)S(1)} %broadcast_multiply_fusion), kind=kLoop, calls=%fused_computation.43 | loop fusion | flops 6290688 | bytes 3151872 | tf_op jit(solution)/shard_map/reduce_sum | solution.py:63
  59.9 80.5 %all-gather.10.cloned.1.call-done = bf16[64,32,1536]{2,1,0:T(8,128)(2,1)} async-done(((bf16[4,32,1536]{2,1,0:T(8,128)(2,1)}), bf16[64,32,1536]{2,1,0:T(8,128)(2,1)}) %all-gather.10.cloned.1.call-update) | async-done | bytes 6291472 | tf_op jit(solution)/shard_map/all_gather | solution.py:75
  140.4 3.7 %copy.41 = bf16[4,16,32,1536]{3,2,1,0:T(8,128)(2,1)S(1)} copy(bf16[4,16,32,1536]{3,2,0,1:T(8,128)(2,1)} %bitcast.120) | data formatting | bytes 12582912 | tf_op jit(solution)/shard_map/transpose | solution.py:76
  144.1 3.2 %fusion.39 = f32[768,768]{0,1:T(8,128)S(1)} fusion(bf16[768,2048]{1,0:T(8,128)(2,1)S(1)} %copy-done, bf16[2048,1536]{1,0:T(8,128)(2,1)S(1)} %bitcast.117, f32[2048]{0:T(1024)S(1)} %copy-done.10, f32[768]{0:T(1024)S(1)} %add_rsqrt_fusion, f32[768]{0:T(1024)S(1)} %broadcast_multiply_fusion), kind=kOutput, calls=%fused_computation.48 | convolution fusion | flops 2423783424 | bytes 8667136 | tf_op jit(solution)/shard_map/dot_general | solution.py:82
  150.0 3.8 %reshape.182 = bf16[16,128,2,4,64]{4,3,2,1,0:T(4,128)(2,1)} reshape(bf16[2048,512]{1,0:T(8,128)(2,1)S(1)} %slice.108) | data formatting | bytes 4194304 | tf_op jit(solution)/shard_map/reshape | solution.py:104
  153.8 5.8 %copy.43 = bf16[16,128,2,4,64]{1,4,3,2,0:T(8,128)(2,1)S(1)} copy(bf16[16,128,2,4,64]{4,3,2,1,0:T(4,128)(2,1)} %reshape.182) | data formatting | bytes 4194304 | tf_op jit(solution)/shard_map/reshape | solution.py:104
  165.6 3.1 %fusion.28 = (f32[4,768]{1,0:T(4,128)S(1)}, f32[4,768,768]{1,2,0:T(8,128)S(1)}) fusion(pred[768,768]{0,1:T(8,128)(4,1)} %iota_compare_fusion, bf16[768,4,48]{0,2,1:T(8,128)(2,1)} %slice.140, bf16[768,4,16]{0,2,1:T(8,128)(2,1)} %copy-done.6, bf16[768,4,48]{0,2,1:T(8,128)(2,1)} %slice.107, bf16[768,4,16]{0,2,1:T(8,128)(2,1)S(1)} %fusion.68), kind=kOutput, calls=%fused_computation.36 | convolution fusion | flops 310637568 | bytes 10825728 | tf_op jit(solution)/shard_map/qhd,khd->hqk/dot_general | solution.py:31
  168.7 2.3 fusion.32
  171.1 4.0 %fusion.63 = f32[768,4,64]{0,2,1:T(8,128)S(1)} fusion(f32[4,768,768]{1,2,0:T(8,128)S(1)} %get-tuple-element.353, f32[4,768]{1,0:T(4,128)S(1)} %get-tuple-element.348, pred[768,768]{0,1:T(8,128)(4,1)S(1)} %copy-done.3, f32[768,4]{0,1:T(4,128)S(1)} %get-tuple-element.347, f32[768,4]{0,1:T(4,128)S(1)} %get-tuple-element.346, f32[768,3,4,64]{0,3,2,1:T(8,128)} %bitcast.122), kind=kOutput, calls=%fused_computation.65 | convolution fusion | flops 314179584 | bytes 11243520 | tf_op jit(solution)/shard_map/hqk,khd->qhd/dot_general | solution.py:37
  176.3 50.3 %while.21 = (s32[]{:T(128)}, f32[4,768]{1,0:T(4,128)S(1)}, f32[4,768]{1,0:T(4,128)S(1)}, f32[768,4,64]{0,2,1:T(8,128)S(1)}, s32[24]{0:T(128)S(1)}, /*index=5*/s3...) while((s32[]{:T(128)}, f32[4,768]{1,0:T(4,128)S(1)}, ...), condition=%wide.region_10.11_spmd.clone, body=%wide.region_7.10_spmd.clone.sunk | while | flops 423506944 | bytes 24709856 | solution.py:135
  181.2 2.0 fusion.98
  189.5 2.0 fusion.98
  191.5 1.7 fusion.99
  197.9 2.0 fusion.98
  199.8 1.7 fusion.99
  206.2 2.0 fusion.98
  214.6 2.0 fusion.98
  222.9 2.0 fusion.98
  229.9 2.7 pad_maximum_fusion
  232.6 30.6 %all-gather.8.cloned.1.call-done = bf16[768,2048]{0,1:T(8,128)(2,1)} async-done(((bf16[768,256]{0,1:T(8,128)(2,1)}), bf16[768,2048]{0,1:T(8,128)(2,1)}) %all-gather.8.cloned.1.call-update) | async-done | bytes 3145744 | tf_op jit(solution)/shard_map/all_gather | solution.py:141
  263.2 3.9 %convolution_convert_fusion = bf16[768,256]{1,0:T(8,128)(2,1)} fusion(bf16[768,2048]{0,1:T(8,128)(2,1)} %all-gather.8.cloned.1.call-done, bf16[2048,1536]{1,0:T(8,128)(2,1)} %bitcast.119), kind=kOutput, calls=%fused_computation.66 | convolution fusion | flops 805502976 | bytes 4587520 | tf_op jit(solution)/shard_map/dot_general | solution.py:143
  (123 shorter events, 54.1 us)
Async XLA Ops:
  7.2 47.5 %all-gather.6.cloned.1.call-start = ((), (), s32[]{:S(2)}) async-start(), calls=%async_computation | async-start | bytes 3538944 | tf_op jit(solution)/shard_map/all_gather | solution.py:59
  7.9 132.5 %all-gather.10.cloned.1.call-start = ((), (), s32[]{:S(2)}) async-start(), calls=%async_computation.2 | async-start | bytes 6684672 | tf_op jit(solution)/shard_map/all_gather | solution.py:75
  21.8 241.4 %all-gather.8.cloned.1.call-start = ((), (), s32[]{:S(2)}) async-start(), calls=%async_computation.1 | async-start | bytes 3538944 | tf_op jit(solution)/shard_map/all_gather | solution.py:141
  25.4 134.2 %copy-start.7 = (f32[768,16]{0,1:T(8,128)}, f32[768,16]{0,1:T(8,128)S(1)}, u32[]{:S(2)}) copy-start(f32[768,16]{0,1:T(8,128)S(1)} %get-tuple-element.358) | copy-start | bytes 147460
  25.4 134.2 %copy-start.8 = (f32[768,16]{0,1:T(8,128)}, f32[768,16]{0,1:T(8,128)S(1)}, u32[]{:S(2)}) copy-start(f32[768,16]{0,1:T(8,128)S(1)} %get-tuple-element.359) | copy-start | bytes 147460
  140.4 3.7 %copy-start = (bf16[768,2048]{1,0:T(8,128)(2,1)S(1)}, bf16[768,2048]{1,0:T(8,128)(2,1)}, u32[]{:S(2)}) copy-start(bf16[768,2048]{1,0:T(8,128)(2,1)} %all-gather.6.cloned.1.call-done) | copy-start | bytes 9437188
  140.4 3.7 %copy-start.10 = (f32[2048]{0:T(1024)S(1)}, f32[2048]{0:T(1024)}, u32[]{:S(2)}) copy-start(f32[2048]{0:T(1024)} %param.13) | copy-start | bytes 24580
  144.0 5.9 %copy-start.1 = (bf16[4,16,32,1536]{3,2,1,0:T(8,128)(2,1)}, bf16[4,16,32,1536]{3,2,1,0:T(8,128)(2,1)S(1)}, u32[]{:S(2)}) copy-start(bf16[4,16,32,1536]{3,2,1,0:T(8,128)(2,1)S(1)} %copy.41) | copy-start | bytes 18874372
  147.3 2.6 copy-start.4
  147.5 1.7 copy-start.2
  153.8 5.8 %copy-start.9 = (f32[768,4,8]{0,2,1:T(8,128)S(1)}, f32[768,4,8]{0,2,1:T(8,128)}, u32[]{:S(2)}) copy-start(f32[768,4,8]{0,2,1:T(8,128)} %get-tuple-element.357) | copy-start | bytes 294916
  160.6 0.6 copy-start.6
  164.6 4.2 %copy-start.3 = (pred[768,768]{0,1:T(8,128)(4,1)S(1)}, pred[768,768]{0,1:T(8,128)(4,1)}, u32[]{:S(2)}) copy-start(pred[768,768]{0,1:T(8,128)(4,1)} %iota_compare_fusion) | copy-start | bytes 1769476
  176.3 52.9 %copy-start.5 = (bf16[768,4,48]{0,2,1:T(8,128)(2,1)S(1)}, bf16[768,4,48]{0,2,1:T(8,128)(2,1)}, u32[]{:S(2)}) copy-start(bf16[768,4,48]{0,2,1:T(8,128)(2,1)} %slice.107) | copy-start | bytes 884740
Sparse Core Ops, SparseCore 0:
  10.1 44.4 all-gather.5
  56.7 83.6 all-gather.9
  227.6 35.5 all-gather.7

commit v3 on v2

--- a/solution.py
+++ b/solution.py
@@ -41,6 +41,13 @@
     return (new_max, weight_sum, weighted)
 
 
+def gather_columns(part):
+    count = lax.axis_size("narrow")
+    copies = jnp.broadcast_to(part[None], (count,) + part.shape)
+    received = lax.all_to_all(copies, "narrow", 0, 0, tiled=False)
+    return jnp.transpose(received, (1, 0, 2)).reshape(part.shape[0], count * part.shape[1])
+
+
 def local(
     tokens,
     norm_gain,
@@ -56,7 +63,7 @@
     span_rows = tokens.shape[0]
     local_width = qkv_weight.shape[2]
     heads_here = local_width // HEAD_DIM
-    gathered = lax.all_gather(tokens, "narrow", axis=1, tiled=True)
+    gathered = gather_columns(tokens)
     widened = gathered.astype(jnp.float32)
     row_mean = jnp.mean(widened, axis=1, keepdims=True)
     centered = widened - row_mean

time: 275 us -> 254 us (0.924)
  waiting for transfers between devices: 140 us -> 94 us
  starting transfers between devices: 0.12 us -> 12.9 us
  local copies, waits for them, and re-layouts: 35.9 us -> 47.3 us
    all_gather x1, waiting for transfers between devices: 80.5 us -> 29.9 us  [local(): by_xz = lax.all_gather(by_x, 'wz', axis=0, tiled=False)]
    all_to_all x0 -> x1, waiting for transfers between devices: none -> 33.5 us  [gather_columns(): received = lax.all_to_all(copies, 'narrow', 0, 0, tiled=False)]
    all_gather x1 -> x0, waiting for transfers between devices: 28.1 us -> none  [local(): gathered = lax.all_gather(tokens, 'narrow', axis=1, tiled=True)]
    all_to_all x0 -> x1, starting transfers between devices: none -> 12.9 us  [gather_columns(): received = lax.all_to_all(copies, 'narrow', 0, 0, tiled=False)]
    another operation x1 -> x2, other arithmetic: 0.96 us -> 4.26 us
    all_to_all x0 -> x1, local copies, waits for them, and re-layouts: none -> 3.18 us  [gather_columns(): received = lax.all_to_all(copies, 'narrow', 0, 0, tiled=False)]
    dot_general x0 -> x2, local copies, waits for them, and re-layouts: none -> 3.12 us  [local(): jnp.dot(columns, piece_rows.reshape(piece_count, 3 * local_width), prefer...]
    broadcast_in_dim x0 -> x1, local copies, waits for them, and re-layouts: none -> 2.83 us  [gather_columns(): copies = jnp.broadcast_to(part[None], (count,) + part.shape)]
  transfers between devices with their start and end apart: 3 -> 3, of which waited for: 3 -> 3; matrix products, arithmetic and copies ran while one was open for 6% -> 7% of each run, Pallas kernels for 0% -> 0%
where the time goes in v3:
time: 254 us; the launch traced here: 253 us
  waiting for transfers between devices  94 us (37%)
  local copies, waits for them, and re-layouts  47.3 us (19%)
  matrix products  36.9 us (15%)
  other arithmetic  34.3 us (14%)
  between operations  15.7 us (6%)
  starting transfers between devices  12.9 us (5%)
  blocking collectives  11.5 us (5%)
    all_to_all x1, waiting for transfers between devices, gather_columns(): received = lax.all_to_all(copies, 'narrow', 0, 0, tiled=False)  33.5 us
    all_gather x1, waiting for transfers between devices, local(): all_heads = lax.all_gather(head_values, 'narrow', axis=1, tiled=True)  30.6 us
    all_gather x1, waiting for transfers between devices, local(): by_xz = lax.all_gather(by_x, 'wz', axis=0, tiled=False)  29.9 us
    dot_general x8, matrix products, attend(): jnp.einsum('hqk,khd->qhd', expo.astype(jnp.bfloat16), values, preferred_e...  14.7 us
    reduce_sum x8, other arithmetic, attend(): weight_sum = weight_sum * factor + jnp.sum(expo, axis=2)  14.7 us
    dynamic_slice x12, local copies, waits for them, and re-layouts, cache_block(): lax.dynamic_slice_in_dim(cache_pool, block_index * KB, KB, axis=0)  13.5 us
    all_to_all x1, starting transfers between devices, gather_columns(): received = lax.all_to_all(copies, 'narrow', 0, 0, tiled=False)  12.9 us
    dot_general x8, matrix products, attend(): jnp.einsum('qhd,khd->hqk', queries, keys, preferred_element_type=jnp.floa...  12.6 us
  transfers between devices with their start and end apart: 3, of which 3 were waited for; matrix products, arithmetic and copies ran while one was open for 7% of the time, Pallas kernels for 0%

profile of v3, /device:TPU:1, one launch (start us, length us, event | category | flops | bytes accessed | tf_op | source)
XLA Modules:
  0.0 253.2 jit_solution(14023914117752866079)
XLA Ops:
  9.5 11.5 %all-gather = bf16[128,1536]{1,0:T(8,128)(2,1)} all-gather(bf16[32,1536]{1,0:T(8,128)(2,1)S(1)} %pad_maximum_fusion.2), channel_id=2, replica_groups=mesh['wx'=4,'wz'=16,'narrow'=8] {'wx'}, dimensions={0}, use_global_device_ids=true | all-gather | bytes 491520 | tf_op jit(solution)/shard_map/all_gather | solution.py:81
  21.1 2.8 %broadcast_in_dim.167 = bf16[8,768,256]{2,1,0:T(8,128)(2,1)} broadcast(bf16[768,256]{1,0:T(8,128)(2,1)} %param.12), dimensions={1,2} | broadcast | bytes 3538944 | tf_op jit(solution)/shard_map/broadcast_in_dim | solution.py:46
  23.9 12.9 %all-to-all-start = ((bf16[8,768,256]{2,1,0:T(8,128)(2,1)}), bf16[8,768,256]{2,1,0:T(8,128)(2,1)}, u32[]{:S(2)}, u32[]{:S(2)}) async-start(bf16[8,768,256]{2,1,0:T(8,128)(2,1)} %broadcast_in_dim.167), calls=%async_computation | async-start | bytes 6291456 | tf_op jit(solution)/shard_map/all_to_all | solution.py:47
  40.9 33.5 %all-to-all-done = bf16[8,768,256]{2,1,0:T(8,128)(2,1)} async-done(((bf16[8,768,256]{2,1,0:T(8,128)(2,1)}), bf16[8,768,256]{2,1,0:T(8,128)(2,1)}, u32[]{:S(2)}, u32[]{:S(2)}) %all-to-all-start) | async-done | bytes 3145760 | tf_op jit(solution)/shard_map/all_to_all | solution.py:47
  74.4 3.2 %copy.53 = bf16[8,768,256]{1,2,0:T(8,128)(2,1)S(1)} copy(bf16[8,768,256]{2,1,0:T(8,128)(2,1)} %all-to-all-done) | data formatting | bytes 6291456 | tf_op jit(solution)/shard_map/all_to_all | solution.py:47
  79.0 2.7 %fusion.35 = bf16[8,768,256]{1,2,0:T(8,128)(2,1)} fusion(bf16[8,768,256]{1,2,0:T(8,128)(2,1)S(1)} %copy.53, f32[8,256]{1,0:T(8,128)S(1)} %mul.195, f32[768]{0:T(1024)S(1)} %add_rsqrt_fusion, f32[768]{0:T(1024)S(1)} %broadcast_multiply_fusion), kind=kLoop, calls=%fused_computation.45 | loop fusion | flops 7864320 | bytes 6305792 | tf_op jit(solution)/shard_map/convert.3
  81.6 29.9 %all-gather.7.cloned.1.call-done = bf16[64,32,1536]{2,1,0:T(8,128)(2,1)} async-done(((bf16[4,32,1536]{2,1,0:T(8,128)(2,1)}), bf16[64,32,1536]{2,1,0:T(8,128)(2,1)}) %all-gather.7.cloned.1.call-update) | async-done | bytes 6291472 | tf_op jit(solution)/shard_map/all_gather | solution.py:82
  111.5 3.5 %copy.55 = bf16[4,16,32,1536]{3,2,1,0:T(8,128)(2,1)S(1)} copy(bf16[4,16,32,1536]{3,2,0,1:T(8,128)(2,1)} %bitcast.128) | data formatting | bytes 12582912 | tf_op jit(solution)/shard_map/transpose | solution.py:83
  115.0 2.6 %copy-done = bf16[4,16,32,1536]{3,2,1,0:T(8,128)(2,1)} copy-done((bf16[4,16,32,1536]{3,2,1,0:T(8,128)(2,1)}, bf16[4,16,32,1536]{3,2,1,0:T(8,128)(2,1)S(1)}, u32[]{:S(2)}) %copy-start) | copy-done | bytes 6291480
  117.9 2.9 %copy.56 = bf16[768,2048]{1,0:T(8,128)(2,1)} copy(bf16[768,2048]{0,1:T(8,128)(2,1)S(1)} %slice_bitcast_fusion.4) | data formatting | bytes 6291456 | tf_op jit(solution)/shard_map/dot_general | solution.py:89
  120.8 5.6 %fusion.79 = f32[768,3,4,64]{0,3,2,1:T(8,128)S(1)} fusion(bf16[768,2048,1,1]{0,1,3,2:T(8,128)(2,1)} %bitcast.129, bf16[3,4,64,2048]{3,2,1,0:T(8,128)(2,1)} %bitcast.130), kind=kOutput, calls=%fused_computation.117 | convolution fusion | flops 2415919104 | bytes 8650752 | tf_op jit(solution)/shard_map/dot_general | solution.py:89
  129.9 3.6 %reshape.204 = bf16[16,128,2,4,64]{4,3,2,1,0:T(4,128)(2,1)} reshape(bf16[2048,512]{1,0:T(8,128)(2,1)S(1)} %slice.108) | data formatting | bytes 4194304 | tf_op jit(solution)/shard_map/reshape | solution.py:111
  133.5 5.9 %copy.59 = bf16[16,128,2,4,64]{1,4,3,2,0:T(8,128)(2,1)S(1)} copy(bf16[16,128,2,4,64]{4,3,2,1,0:T(4,128)(2,1)} %reshape.204) | data formatting | bytes 4194304 | tf_op jit(solution)/shard_map/reshape | solution.py:111
  144.9 3.0 %fusion.28 = (f32[4,768]{1,0:T(4,128)S(1)}, f32[4,768,768]{1,2,0:T(8,128)S(1)}) fusion(pred[768,768]{0,1:T(8,128)(4,1)} %iota_compare_fusion, bf16[768,4,48]{0,2,1:T(8,128)(2,1)S(1)} %slice.139, bf16[768,4,16]{0,2,1:T(8,128)(2,1)} %fusion.64, bf16[768,4,48]{0,2,1:T(8,128)(2,1)S(1)} %slice.107, bf16[768,4,16]{0,2,1:T(8,128)(2,1)} %fusion.62), kind=kOutput, calls=%fused_computation.36 | convolution fusion | flops 310637568 | bytes 10825728 | tf_op jit(solution)/shard_map/qhd,khd->hqk/dot_general | solution.py:31
  148.0 2.3 fusion.32
  150.4 3.9 %fusion.57 = f32[768,4,64]{0,2,1:T(8,128)S(1)} fusion(f32[4,768,768]{1,2,0:T(8,128)S(1)} %get-tuple-element.361, f32[4,768]{1,0:T(4,128)S(1)} %get-tuple-element.356, pred[768,768]{0,1:T(8,128)(4,1)S(1)} %copy-done.2, f32[768,4]{0,1:T(4,128)S(1)} %get-tuple-element.355, f32[768,4]{0,1:T(4,128)S(1)} %get-tuple-element.354, f32[768,3,4,64]{0,3,2,1:T(8,128)} %copy-done.3), kind=kOutput, calls=%fused_computation.61 | convolution fusion | flops 314179584 | bytes 11243520 | tf_op jit(solution)/shard_map/hqk,khd->qhd/dot_general | solution.py:37
  155.6 50.3 %while.21 = (s32[]{:T(128)}, f32[4,768]{1,0:T(4,128)S(1)}, f32[4,768]{1,0:T(4,128)S(1)}, f32[768,4,64]{0,2,1:T(8,128)S(1)}, s32[24]{0:T(128)S(1)}, /*index=5*/s3...) while((s32[]{:T(128)}, f32[4,768]{1,0:T(4,128)S(1)}, ...), condition=%wide.region_10.11_spmd.clone, body=%wide.region_7.10_spmd.clone.sunk | while | flops 423506944 | bytes 24709856 | solution.py:142
  162.2 2.0 fusion.95
  187.2 2.0 fusion.95
  195.6 2.0 fusion.95
  203.9 2.0 fusion.95
  209.2 2.7 %pad_maximum_fusion = bf16[768,2,256]{2,1,0:T(2,128)(2,1)} fusion(bf16[768,1,256]{2,1,0:T(2,128)(2,1)S(1)} %copy.65, bf16[768,1,256]{2,1,0:T(2,128)(2,1)S(1)} %copy.64), kind=kLoop, calls=%fused_computation.68 | loop fusion | flops 1572864 | bytes 1572864 | tf_op jit(solution)/shard_map/stack | solution.py:101
  211.9 30.6 %all-gather.5.cloned.1.call-done = bf16[768,2048]{0,1:T(8,128)(2,1)} async-done(((bf16[768,256]{0,1:T(8,128)(2,1)}), bf16[768,2048]{0,1:T(8,128)(2,1)}) %all-gather.5.cloned.1.call-update) | async-done | bytes 3145744 | tf_op jit(solution)/shard_map/all_gather | solution.py:148
  242.5 3.9 %convolution_convert_fusion = bf16[768,256]{1,0:T(8,128)(2,1)} fusion(bf16[768,2048]{0,1:T(8,128)(2,1)} %all-gather.5.cloned.1.call-done, bf16[2048,1536]{1,0:T(8,128)(2,1)} %bitcast.127), kind=kOutput, calls=%fused_computation.62 | convolution fusion | flops 805502976 | bytes 4587520 | tf_op jit(solution)/shard_map/dot_general | solution.py:150
  (124 shorter events, 62.0 us)
Async XLA Ops:
  7.2 29.6 %copy-start.6 = (f32[2048]{0:T(1024)S(1)}, f32[2048]{0:T(1024)}, u32[]{:S(2)}) copy-start(f32[2048]{0:T(1024)} %param.13) | copy-start | bytes 24580
  7.2 30.9 %copy-start.8 = (s32[1,24]{1,0:T(1,128)S(1)}, s32[1,24]{1,0:T(1,128)}, u32[]{:S(2)}) copy-start(s32[1,24]{1,0:T(1,128)} %param.18) | copy-start | bytes 292
  7.2 31.6 %copy-start.7 = (s32[16]{0:T(128)S(1)}, s32[16]{0:T(128)}, u32[]{:S(2)}) copy-start(s32[16]{0:T(128)} %param.21) | copy-start | bytes 196
  7.2 104.3 %all-gather.7.cloned.1.call-start = ((), (), s32[]{:S(2)}) async-start(), calls=%async_computation.2 | async-start | bytes 6684672 | tf_op jit(solution)/shard_map/all_gather | solution.py:82
  23.9 50.5 %all-to-all-start = ((bf16[8,768,256]{2,1,0:T(8,128)(2,1)}), bf16[8,768,256]{2,1,0:T(8,128)(2,1)}, u32[]{:S(2)}, u32[]{:S(2)}) async-start(bf16[8,768,256]{2,1,0:T(8,128)(2,1)} %broadcast_in_dim.167), calls=%async_computation | async-start | bytes 6291456 | tf_op jit(solution)/shard_map/all_to_all | solution.py:47
  36.8 205.7 %all-gather.5.cloned.1.call-start = ((), (), s32[]{:S(2)}) async-start(), calls=%async_computation.1 | async-start | bytes 3538944 | tf_op jit(solution)/shard_map/all_gather | solution.py:148
  115.0 2.6 %copy-start = (bf16[4,16,32,1536]{3,2,1,0:T(8,128)(2,1)}, bf16[4,16,32,1536]{3,2,1,0:T(8,128)(2,1)S(1)}, u32[]{:S(2)}) copy-start(bf16[4,16,32,1536]{3,2,1,0:T(8,128)(2,1)S(1)} %copy.55) | copy-start | bytes 18874372
  126.4 1.8 copy-start.3
  126.5 1.0 copy-start.1
  144.9 3.1 %copy-start.4 = (bf16[768,4,16]{0,2,1:T(8,128)(2,1)S(1)}, bf16[768,4,16]{0,2,1:T(8,128)(2,1)}, u32[]{:S(2)}) copy-start(bf16[768,4,16]{0,2,1:T(8,128)(2,1)} %fusion.64) | copy-start | bytes 294916
  144.9 3.1 %copy-start.2 = (pred[768,768]{0,1:T(8,128)(4,1)S(1)}, pred[768,768]{0,1:T(8,128)(4,1)}, u32[]{:S(2)}) copy-start(pred[768,768]{0,1:T(8,128)(4,1)} %iota_compare_fusion) | copy-start | bytes 1769476
  155.6 52.3 %copy-start.5 = (bf16[768,4,16]{0,2,1:T(8,128)(2,1)S(1)}, bf16[768,4,16]{0,2,1:T(8,128)(2,1)}, u32[]{:S(2)}) copy-start(bf16[768,4,16]{0,2,1:T(8,128)(2,1)} %fusion.62) | copy-start | bytes 294916
Sparse Core Ops, SparseCore 0:
  21.2 90.2 all-gather.6
  206.9 35.5 all-gather.4

commit v4 on v3

--- a/solution.py
+++ b/solution.py
@@ -79,13 +79,16 @@
         axis=1,
     )
     by_x = lax.all_gather(merged, "wx", axis=0, tiled=False)
-    by_xz = lax.all_gather(by_x, "wz", axis=0, tiled=False)
-    merged_whole = jnp.transpose(by_xz, (1, 0, 2, 3)).reshape(-1, merged.shape[1])
-    piece_rows = merged_whole[:, : 3 * local_width]
-    out_rows = merged_whole[:, 3 * local_width : 4 * local_width]
-    prefix_whole = merged_whole[:, 4 * local_width :]
-    piece_count = piece_rows.shape[0]
-    columns = normed
+    stacked = lax.all_gather(by_x, "wz", axis=0, tiled=False)
+    along_z, along_x = stacked.shape[0], stacked.shape[1]
+    piece_count = along_z * along_x * shard_rows
+    piece_rows = stacked[..., : 3 * local_width].reshape(piece_count, 3 * local_width)
+    out_rows = jnp.transpose(
+        stacked[..., 3 * local_width : 4 * local_width], (1, 0, 2, 3)
+    ).reshape(piece_count, local_width)
+    columns = jnp.transpose(
+        normed.reshape(span_rows, along_x, along_z, shard_rows), (0, 2, 1, 3)
+    ).reshape(span_rows, piece_count)
     projected = jnp.dot(
         columns,
         piece_rows.reshape(piece_count, 3 * local_width),
@@ -108,9 +111,10 @@
     )
     running = attend(initial, queries, keys, values, offset[:, None] >= offset[None, :])
     my_group = group_ids[0]
-    prefix_pages = prefix_whole.reshape(-1, PAGE, 2, heads_here, HEAD_DIM)
     chosen = lax.dynamic_slice_in_dim(group_pages, my_group * PPAGES, PPAGES)
-    key_rows = jnp.take(prefix_pages, chosen, axis=0).reshape(
+    chunks = PAGE // shard_rows
+    chunk_ids = (chosen[:, None] * chunks + jnp.arange(chunks, dtype=jnp.int32)[None, :]).reshape(-1)
+    key_rows = stacked[chunk_ids % along_z, chunk_ids // along_z][..., 4 * local_width :].reshape(
         PPAGES * PAGE, 2, heads_here, HEAD_DIM
     )
     running = attend(

time: 254 us -> 261 us (1.028)
  matrix products: 36.9 us -> 41.5 us
    reshape x2 -> x1, local copies, waits for them, and re-layouts: 9.54 us -> 0.27 us  [local(): stacked[chunk_ids % along_z, chunk_ids // along_z][..., 4 * local_width:]]
    while x6 -> x30, local copies, waits for them, and re-layouts: 0.02 us -> 5.08 us
    another operation x2 -> x1, other arithmetic: 4.26 us -> 0.03 us
    reduce_sum x8, other arithmetic: 14.7 us -> 18.5 us  [attend(): weight_sum = weight_sum * factor + jnp.sum(expo, axis=2)]
    dot_general x8, matrix products: 12.6 us -> 16.4 us  [attend(): jnp.einsum('qhd,khd->hqk', queries, keys, preferred_element_type=jnp.floa...]
    all_gather x1, waiting for transfers between devices: 29.9 us -> 33.1 us  [local(): stacked = lax.all_gather(by_x, 'wz', axis=0, tiled=False)]
    all_to_all x1 -> x0, local copies, waits for them, and re-layouts: 3.18 us -> none  [gather_columns(): received = lax.all_to_all(copies, 'narrow', 0, 0, tiled=False)]
    gather x1, local copies, waits for them, and re-layouts: 0.6 us -> 3.38 us  [local(): stacked[chunk_ids % along_z, chunk_ids // along_z][..., 4 * local_width:]]
  transfers between devices with their start and end apart: 3 -> 3, of which waited for: 3 -> 3; matrix products, arithmetic and copies ran while one was open for 7% -> 6% of each run, Pallas kernels for 0% -> 0%
where the time goes in v4:
time: 261 us; the launch traced here: 260 us
  waiting for transfers between devices  96.2 us (37%)
  local copies, waits for them, and re-layouts  46 us (18%)
  matrix products  41.5 us (16%)
  other arithmetic  36.1 us (14%)
  between operations  15.7 us (6%)
  starting transfers between devices  12.2 us (5%)
  blocking collectives  11.5 us (4%)
    all_to_all x1, waiting for transfers between devices, gather_columns(): received = lax.all_to_all(copies, 'narrow', 0, 0, tiled=False)  33.9 us
    all_gather x1, waiting for transfers between devices, local(): stacked = lax.all_gather(by_x, 'wz', axis=0, tiled=False)  33.1 us
    all_gather x1, waiting for transfers between devices, local(): all_heads = lax.all_gather(head_values, 'narrow', axis=1, tiled=True)  29.1 us
    reduce_sum x8, other arithmetic, attend(): weight_sum = weight_sum * factor + jnp.sum(expo, axis=2)  18.5 us
    dot_general x8, matrix products, attend(): jnp.einsum('qhd,khd->hqk', queries, keys, preferred_element_type=jnp.floa...  16.4 us
    dot_general x8, matrix products, attend(): jnp.einsum('hqk,khd->qhd', expo.astype(jnp.bfloat16), values, preferred_e...  15.8 us
    dynamic_slice x12, local copies, waits for them, and re-layouts, cache_block(): lax.dynamic_slice_in_dim(cache_pool, block_index * KB, KB, axis=0)  13.5 us
    all_to_all x1, starting transfers between devices, gather_columns(): received = lax.all_to_all(copies, 'narrow', 0, 0, tiled=False)  12.1 us
  transfers between devices with their start and end apart: 3, of which 3 were waited for; matrix products, arithmetic and copies ran while one was open for 6% of the time, Pallas kernels for 0%

profile of v4, /device:TPU:1, one launch (start us, length us, event | category | flops | bytes accessed | tf_op | source)
XLA Modules:
  0.0 259.7 jit_solution(8740612170411432903)
XLA Ops:
  9.5 11.5 %all-gather = bf16[128,1536]{1,0:T(8,128)(2,1)} all-gather(bf16[32,1536]{1,0:T(8,128)(2,1)S(1)} %pad_maximum_fusion.2), channel_id=2, replica_groups=mesh['wx'=4,'wz'=16,'narrow'=8] {'wx'}, dimensions={0}, use_global_device_ids=true | all-gather | bytes 491520 | tf_op jit(solution)/shard_map/all_gather | solution.py:81
  22.3 1.9 broadcast_in_dim.155
  24.1 12.1 %all-to-all-start = ((bf16[8,768,256]{1,2,0:T(8,128)(2,1)}), bf16[8,768,256]{1,2,0:T(8,128)(2,1)S(1)}, u32[]{:S(2)}, u32[]{:S(2)}) async-start(bf16[8,768,256]{1,2,0:T(8,128)(2,1)} %broadcast_in_dim.155), calls=%async_computation | async-start | bytes 6291456 | tf_op jit(solution)/shard_map/all_to_all | solution.py:47
  39.8 33.9 %all-to-all-done = bf16[8,768,256]{1,2,0:T(8,128)(2,1)S(1)} async-done(((bf16[8,768,256]{1,2,0:T(8,128)(2,1)}), bf16[8,768,256]{1,2,0:T(8,128)(2,1)S(1)}, u32[]{:S(2)}, u32[]{:S(2)}) %all-to-all-start) | async-done | bytes 3145760 | tf_op jit(solution)/shard_map/all_to_all | solution.py:47
  76.5 1.9 copy.36
  78.4 33.1 %all-gather.7.cloned.1.call-done = bf16[64,32,1536]{2,1,0:T(8,128)(2,1)} async-done(((bf16[4,32,1536]{2,1,0:T(8,128)(2,1)}), bf16[64,32,1536]{2,1,0:T(8,128)(2,1)}) %all-gather.7.cloned.1.call-update) | async-done | bytes 6291472 | tf_op jit(solution)/shard_map/all_gather | solution.py:82
  111.5 2.2 slice.97
  113.7 3.0 %copy.38 = bf16[768,2048]{1,0:T(8,128)(2,1)} copy(bf16[768,2048]{0,1:T(8,128)(2,1)S(1)} %bitcast.127) | data formatting | bytes 6291456 | tf_op jit(solution)/shard_map/dot_general | solution.py:92
  116.7 5.6 %fusion.83 = f32[768,3,4,64]{0,3,2,1:T(8,128)S(1)} fusion(bf16[768,2048,1,1]{0,1,3,2:T(8,128)(2,1)} %bitcast.131, bf16[3,4,64,2048]{3,2,1,0:T(8,128)(2,1)} %bitcast.132), kind=kOutput, calls=%fused_computation.124 | convolution fusion | flops 2415919104 | bytes 8650752 | tf_op jit(solution)/shard_map/dot_general | solution.py:92
  125.4 3.4 %gather_fusion = bf16[8,32,1536]{2,1,0:T(8,128)(2,1)S(1)} fusion(bf16[16,4,32,1536]{3,2,1,0:T(8,128)(2,1)} %bitcast.129, s32[8]{0:T(128)S(1)} %fusion.72), kind=kCustom, calls=%fused_computation | custom fusion | bytes 1572928 | tf_op jit(solution)/shard_map/gather | solution.py:117
  133.6 6.7 %fusion.28 = (f32[4,768]{1,0:T(4,128)S(1)}, f32[4,768,768]{1,2,0:T(8,128)}) fusion(pred[768,768]{0,1:T(8,128)(4,1)} %iota_compare_fusion, bf16[768,4,48]{0,2,1:T(8,128)(2,1)} %copy-done.4, bf16[768,4,16]{0,2,1:T(8,128)(2,1)S(1)} %fusion.59, bf16[768,4,48]{0,2,1:T(8,128)(2,1)} %slice.107, bf16[768,4,16]{0,2,1:T(8,128)(2,1)S(1)} %fusion.57), kind=kOutput, calls=%fused_computation.36 | convolution fusion | flops 310637568 | bytes 10825728 | tf_op jit(solution)/shard_map/qhd,khd->hqk/dot_general | solution.py:31
  143.3 6.2 %fusion.30 = f32[4,768]{1,0:T(4,128)S(1)} fusion(f32[4,768,768]{1,2,0:T(8,128)} %get-tuple-element.345, f32[4,768]{1,0:T(4,128)} %get-tuple-element.340, pred[768,768]{0,1:T(8,128)(4,1)} %iota_compare_fusion), kind=kLoop, calls=%fused_computation.38 | loop fusion | flops 11793408 | bytes 10051584 | tf_op jit(solution)/shard_map/reduce_sum | solution.py:36
  149.9 4.0 %fusion.53 = f32[768,4,64]{0,2,1:T(8,128)S(1)} fusion(f32[4,768,768]{1,2,0:T(8,128)S(1)} %copy-done, f32[4,768]{1,0:T(4,128)S(1)} %copy-done.17, pred[768,768]{0,1:T(8,128)(4,1)S(1)} %copy-done.5, f32[768,4]{0,1:T(4,128)} %get-tuple-element.339, f32[768,4]{0,1:T(4,128)S(1)} %copy-done.18, f32[768,3,4,64]{0,3,2,1:T(8,128)} %copy-done.6), kind=kOutput, calls=%fused_computation.57 | convolution fusion | flops 314179584 | bytes 11243520 | tf_op jit(solution)/shard_map/hqk,khd->qhd/dot_general | solution.py:37
  156.3 55.1 %while.21 = (s32[]{:T(128)}, f32[4,768]{1,0:T(4,128)S(1)}, f32[4,768]{1,0:T(4,128)S(1)}, f32[768,4,64]{0,2,1:T(8,128)}, s32[24]{0:T(128)S(1)}, /*index=5*/s32[]{...) while((s32[]{:T(128)}, f32[4,768]{1,0:T(4,128)S(1)}, ...), condition=%wide.region_10.11_spmd.clone, body=%wide.region_7.10_spmd.clone.sunk | while | flops 423506944 | bytes 31001368 | solution.py:146
  160.9 2.0 fusion.99
  170.1 2.0 fusion.99
  179.3 2.0 fusion.99
  188.5 2.0 fusion.99
  197.7 2.0 fusion.99
  206.9 2.0 fusion.99
  211.4 2.0 divide_convert_fusion
  217.4 2.7 %pad_maximum_fusion = bf16[768,2,256]{2,1,0:T(2,128)(2,1)} fusion(bf16[768,1,256]{2,1,0:T(2,128)(2,1)S(1)} %copy.47, bf16[768,1,256]{2,1,0:T(2,128)(2,1)S(1)} %copy.46), kind=kLoop, calls=%fused_computation.64 | loop fusion | flops 1572864 | bytes 1572864 | tf_op jit(solution)/shard_map/stack | solution.py:104
  220.0 29.1 %all-gather.5.cloned.1.call-done = bf16[768,2048]{0,1:T(8,128)(2,1)} async-done(((bf16[768,256]{0,1:T(8,128)(2,1)}), bf16[768,2048]{0,1:T(8,128)(2,1)}) %all-gather.5.cloned.1.call-update) | async-done | bytes 3145744 | tf_op jit(solution)/shard_map/all_gather | solution.py:152
  249.2 3.7 %convolution_convert_fusion = bf16[768,256]{1,0:T(8,128)(2,1)} fusion(bf16[768,2048]{0,1:T(8,128)(2,1)} %all-gather.5.cloned.1.call-done, bf16[2048,256]{1,0:T(8,128)(2,1)S(1)} %bitcast.137), kind=kOutput, calls=%fused_computation.58 | convolution fusion | flops 805502976 | bytes 4587520 | tf_op jit(solution)/shard_map/dot_general | solution.py:154
  (175 shorter events, 68.8 us)
Async XLA Ops:
  7.2 30.4 %copy-start.20 = (s32[16]{0:T(128)S(1)}, s32[16]{0:T(128)}, u32[]{:S(2)}) copy-start(s32[16]{0:T(128)} %param.21) | copy-start | bytes 196
  7.2 30.6 %copy-start.19 = (f32[2048]{0:T(1024)S(1)}, f32[2048]{0:T(1024)}, u32[]{:S(2)}) copy-start(f32[2048]{0:T(1024)} %param.13) | copy-start | bytes 24580
  7.2 30.7 %copy-start.21 = (s32[1,24]{1,0:T(1,128)S(1)}, s32[1,24]{1,0:T(1,128)}, u32[]{:S(2)}) copy-start(s32[1,24]{1,0:T(1,128)} %param.18) | copy-start | bytes 292
  7.2 104.3 %all-gather.7.cloned.1.call-start = ((), (), s32[]{:S(2)}) async-start(), calls=%async_computation.2 | async-start | bytes 6684672 | tf_op jit(solution)/shard_map/all_gather | solution.py:82
  24.1 49.6 %all-to-all-start = ((bf16[8,768,256]{1,2,0:T(8,128)(2,1)}), bf16[8,768,256]{1,2,0:T(8,128)(2,1)S(1)}, u32[]{:S(2)}, u32[]{:S(2)}) async-start(bf16[8,768,256]{1,2,0:T(8,128)(2,1)} %broadcast_in_dim.155), calls=%async_computation | async-start | bytes 6291456 | tf_op jit(solution)/shard_map/all_to_all | solution.py:47
  36.2 212.9 %all-gather.5.cloned.1.call-start = ((), (), s32[]{:S(2)}) async-start(), calls=%async_computation.1 | async-start | bytes 3538944 | tf_op jit(solution)/shard_map/all_gather | solution.py:152
  38.7 92.0 %copy-start.9 = (f32[768,16]{0,1:T(8,128)}, f32[768,16]{0,1:T(8,128)S(1)}, u32[]{:S(2)}) copy-start(f32[768,16]{0,1:T(8,128)S(1)} %get-tuple-element.350) | copy-start | bytes 147460
  38.8 92.0 %copy-start.10 = (f32[768,16]{0,1:T(8,128)}, f32[768,16]{0,1:T(8,128)S(1)}, u32[]{:S(2)}) copy-start(f32[768,16]{0,1:T(8,128)S(1)} %get-tuple-element.351) | copy-start | bytes 147460
  123.7 7.1 %copy-start.4 = (bf16[768,4,48]{0,2,1:T(8,128)(2,1)}, bf16[768,4,48]{0,2,1:T(8,128)(2,1)S(1)}, u32[]{:S(2)}) copy-start(bf16[768,4,48]{0,2,1:T(8,128)(2,1)S(1)} %slice.133) | copy-start | bytes 884740
  132.5 8.4 %copy-start.13 = (f32[4,768]{1,0:T(4,128)}, f32[4,768]{1,0:T(4,128)S(1)}, u32[]{:S(2)}) copy-start(f32[4,768]{1,0:T(4,128)S(1)} %get-tuple-element.346) | copy-start | bytes 36868
  133.6 6.7 %copy-start.11 = (bf16[768,4,16]{0,2,1:T(8,128)(2,1)}, bf16[768,4,16]{0,2,1:T(8,128)(2,1)S(1)}, u32[]{:S(2)}) copy-start(bf16[768,4,16]{0,2,1:T(8,128)(2,1)S(1)} %fusion.57) | copy-start | bytes 294916
  143.3 6.5 %copy-start = (f32[4,768,768]{1,2,0:T(8,128)S(1)}, f32[4,768,768]{1,2,0:T(8,128)}, u32[]{:S(2)}) copy-start(f32[4,768,768]{1,2,0:T(8,128)} %get-tuple-element.345) | copy-start | bytes 28311556
  143.3 6.6 %copy-start.5 = (pred[768,768]{0,1:T(8,128)(4,1)S(1)}, pred[768,768]{0,1:T(8,128)(4,1)}, u32[]{:S(2)}) copy-start(pred[768,768]{0,1:T(8,128)(4,1)} %iota_compare_fusion) | copy-start | bytes 1769476
  143.3 6.6 %copy-start.17 = (f32[4,768]{1,0:T(4,128)S(1)}, f32[4,768]{1,0:T(4,128)}, u32[]{:S(2)}) copy-start(f32[4,768]{1,0:T(4,128)} %get-tuple-element.340) | copy-start | bytes 36868
  143.3 6.6 %copy-start.18 = (f32[768,4]{0,1:T(4,128)S(1)}, f32[768,4]{0,1:T(4,128)}, u32[]{:S(2)}) copy-start(f32[768,4]{0,1:T(4,128)} %get-tuple-element.338) | copy-start | bytes 36868
  149.9 4.5 %copy-start.8 = (bf16[256,1,4,64]{0,3,2,1:T(8,128)(2,1)S(1)}, bf16[256,1,4,64]{0,3,2,1:T(8,128)(2,1)}, u32[]{:S(2)}) copy-start(bf16[256,1,4,64]{0,3,2,1:T(8,128)(2,1)} %copy.55) | copy-start | bytes 393220
  159.6 3.4 %copy-start.1 = (f32[768,4,64]{0,2,1:T(8,128)S(1)}, f32[768,4,64]{0,2,1:T(8,128)}, u32[]{:S(2)}) copy-start(f32[768,4,64]{0,2,1:T(8,128)} %get-tuple-element.424) | copy-start | bytes 2359300 | tf_op jit(solution)/shard_map/while
  168.7 3.4 %copy-start.1 = (f32[768,4,64]{0,2,1:T(8,128)S(1)}, f32[768,4,64]{0,2,1:T(8,128)}, u32[]{:S(2)}) copy-start(f32[768,4,64]{0,2,1:T(8,128)} %get-tuple-element.424) | copy-start | bytes 2359300 | tf_op jit(solution)/shard_map/while
  177.9 3.4 %copy-start.1 = (f32[768,4,64]{0,2,1:T(8,128)S(1)}, f32[768,4,64]{0,2,1:T(8,128)}, u32[]{:S(2)}) copy-start(f32[768,4,64]{0,2,1:T(8,128)} %get-tuple-element.424) | copy-start | bytes 2359300 | tf_op jit(solution)/shard_map/while
  187.1 3.4 %copy-start.1 = (f32[768,4,64]{0,2,1:T(8,128)S(1)}, f32[768,4,64]{0,2,1:T(8,128)}, u32[]{:S(2)}) copy-start(f32[768,4,64]{0,2,1:T(8,128)} %get-tuple-element.424) | copy-start | bytes 2359300 | tf_op jit(solution)/shard_map/while
  196.3 3.4 %copy-start.1 = (f32[768,4,64]{0,2,1:T(8,128)S(1)}, f32[768,4,64]{0,2,1:T(8,128)}, u32[]{:S(2)}) copy-start(f32[768,4,64]{0,2,1:T(8,128)} %get-tuple-element.424) | copy-start | bytes 2359300 | tf_op jit(solution)/shard_map/while
  205.5 3.4 %copy-start.1 = (f32[768,4,64]{0,2,1:T(8,128)S(1)}, f32[768,4,64]{0,2,1:T(8,128)}, u32[]{:S(2)}) copy-start(f32[768,4,64]{0,2,1:T(8,128)} %get-tuple-element.424) | copy-start | bytes 2359300 | tf_op jit(solution)/shard_map/while
  211.4 5.2 %copy-start.7 = (bf16[768,4,48]{0,2,1:T(8,128)(2,1)S(1)}, bf16[768,4,48]{0,2,1:T(8,128)(2,1)}, u32[]{:S(2)}) copy-start(bf16[768,4,48]{0,2,1:T(8,128)(2,1)} %slice.107) | copy-start | bytes 884740
  211.4 5.2 %copy-start.12 = (bf16[768,4,16]{0,2,1:T(8,128)(2,1)S(1)}, bf16[768,4,16]{0,2,1:T(8,128)(2,1)}, u32[]{:S(2)}) copy-start(bf16[768,4,16]{0,2,1:T(8,128)(2,1)} %copy-done.11) | copy-start | bytes 294916
  (11 other events, 13.6 us)
Sparse Core Ops, SparseCore 0:
  21.2 90.2 all-gather.6
  213.6 35.5 all-gather.4

commit v5 on v3

--- a/solution.py
+++ b/solution.py
@@ -1,6 +1,8 @@
 import jax
 import jax.numpy as jnp
 from jax import lax
+from jax.experimental import pallas as pl
+from jax.experimental.pallas import tpu as pltpu
 from jax.sharding import Mesh, PartitionSpec as P
 
 HEAD_DIM = 64
@@ -39,6 +41,70 @@
     )
     weighted = weighted * jnp.transpose(factor)[:, :, None] + update
     return (new_max, weight_sum, weighted)
+
+
+def cache_attention(queries_hm, keys_hm, values_hm, key_valid, block_keys):
+    heads, rows, depth = queries_hm.shape
+    total_keys = keys_hm.shape[1]
+    steps = total_keys // block_keys
+
+    def body(q_ref, k_ref, v_ref, valid_ref, max_out, sum_out, acc_out, max_s, sum_s, acc_s):
+        step = pl.program_id(1)
+
+        @pl.when(step == 0)
+        def _():
+            max_s[...] = jnp.full(max_s.shape, NEGATIVE, jnp.float32)
+            sum_s[...] = jnp.zeros(sum_s.shape, jnp.float32)
+            acc_s[...] = jnp.zeros(acc_s.shape, jnp.float32)
+
+        q = q_ref[0]
+        k = k_ref[0]
+        v = v_ref[0]
+        valid = valid_ref[...] > 0
+        scores = lax.dot_general(q, k, (((1,), (1,)), ((), ())), preferred_element_type=jnp.float32) * 0.125
+        scores = jnp.where(valid, scores, NEGATIVE)
+        old_max = max_s[...]
+        new_max = jnp.maximum(old_max, jnp.max(scores, axis=1, keepdims=True))
+        expo = jnp.where(valid, jnp.exp(scores - new_max), 0.0)
+        factor = jnp.exp(old_max - new_max)
+        sum_s[...] = sum_s[...] * factor + jnp.sum(expo, axis=1, keepdims=True)
+        acc_s[...] = acc_s[...] * factor + lax.dot_general(
+            expo.astype(jnp.bfloat16), v, (((1,), (0,)), ((), ())), preferred_element_type=jnp.float32
+        )
+        max_s[...] = new_max
+
+        @pl.when(step == steps - 1)
+        def _():
+            max_out[0] = max_s[...]
+            sum_out[0] = sum_s[...]
+            acc_out[0] = acc_s[...]
+
+    return pl.pallas_call(
+        body,
+        grid=(heads, steps),
+        in_specs=[
+            pl.BlockSpec((1, rows, depth), lambda h, s: (h, 0, 0)),
+            pl.BlockSpec((1, block_keys, depth), lambda h, s: (h, s, 0)),
+            pl.BlockSpec((1, block_keys, depth), lambda h, s: (h, s, 0)),
+            pl.BlockSpec((1, block_keys), lambda h, s: (0, s)),
+        ],
+        out_specs=[
+            pl.BlockSpec((1, rows, 1), lambda h, s: (h, 0, 0)),
+            pl.BlockSpec((1, rows, 1), lambda h, s: (h, 0, 0)),
+            pl.BlockSpec((1, rows, depth), lambda h, s: (h, 0, 0)),
+        ],
+        out_shape=[
+            jax.ShapeDtypeStruct((heads, rows, 1), jnp.float32),
+            jax.ShapeDtypeStruct((heads, rows, 1), jnp.float32),
+            jax.ShapeDtypeStruct((heads, rows, depth), jnp.float32),
+        ],
+        scratch_shapes=[
+            pltpu.VMEM((rows, 1), jnp.float32),
+            pltpu.VMEM((rows, 1), jnp.float32),
+            pltpu.VMEM((rows, depth), jnp.float32),
+        ],
+        compiler_params=pltpu.CompilerParams(dimension_semantics=("parallel", "arbitrary")),
+    )(queries_hm, keys_hm, values_hm, key_valid)
 
 
 def gather_columns(part):
@@ -128,18 +194,27 @@
         .set(jnp.arange(page_count, dtype=jnp.int32))
     )
     block_keys = KB * PAGE
-    key_offset = jnp.arange(block_keys, dtype=jnp.int32)
-
-    def cache_block(block_index, state_now):
-        key_rows = lax.dynamic_slice_in_dim(cache_pool, block_index * KB, KB, axis=0).reshape(
-            block_keys, 2, heads_here, HEAD_DIM
-        )
-        slots = lax.dynamic_slice_in_dim(slot_of_page, block_index * KB, KB)
-        key_slot = jnp.repeat(slots, PAGE) * PAGE + key_offset % PAGE
-        key_valid = jnp.broadcast_to((key_slot < length)[None, :], (span_rows, block_keys))
-        return attend(state_now, queries, key_rows[:, 0], key_rows[:, 1], key_valid)
-
-    running = lax.fori_loop(0, page_count // KB, cache_block, running)
+    key_slot = (slot_of_page[:, None] * PAGE + jnp.arange(PAGE, dtype=jnp.int32)[None, :]).reshape(1, -1)
+    key_valid = (key_slot < length).astype(jnp.int32)
+    pool_rows = cache_pool.reshape(page_count * PAGE, 2, heads_here, HEAD_DIM)
+    cache_max, cache_sum, cache_acc = cache_attention(
+        jnp.transpose(queries, (1, 0, 2)),
+        jnp.transpose(pool_rows[:, 0], (1, 0, 2)),
+        jnp.transpose(pool_rows[:, 1], (1, 0, 2)),
+        key_valid,
+        block_keys,
+    )
+    row_max, weight_sum, weighted = running
+    cache_max = cache_max[..., 0]
+    both_max = jnp.maximum(row_max, cache_max)
+    keep = jnp.exp(row_max - both_max)
+    take = jnp.exp(cache_max - both_max)
+    running = (
+        both_max,
+        weight_sum * keep + cache_sum[..., 0] * take,
+        weighted * jnp.transpose(keep)[:, :, None]
+        + jnp.transpose(cache_acc, (1, 0, 2)) * jnp.transpose(take)[:, :, None],
+    )
     head_values = (
         (running[2] / jnp.transpose(running[1])[:, :, None])
         .astype(jnp.bfloat16)

time: 254 us -> 307 us (1.21)
  Pallas kernels: 0 us -> 48.6 us
  local copies, waits for them, and re-layouts: 47.3 us -> 78.3 us
  waiting for transfers between devices: 94 us -> 79.6 us
  matrix products: 36.9 us -> 27.6 us
    pallas_call x0 -> x1, Pallas kernels: none -> 48.6 us  [cache_attention(): pl.pallas_call(body, grid=(heads, steps), in_specs=[pl.BlockSpec((1, rows...]
    all_to_all x1, waiting for transfers between devices: 33.5 us -> 17.6 us  [gather_columns(): received = lax.all_to_all(copies, 'narrow', 0, 0, tiled=False)]
    dynamic_slice x12 -> x0, local copies, waits for them, and re-layouts: 13.5 us -> none  [cache_block(): lax.dynamic_slice_in_dim(cache_pool, block_index * KB, KB, axis=0)]
    slice x0 -> x4, local copies, waits for them, and re-layouts: none -> 10.8 us  [the longest x2 4.97 us: rotary(): rotated_in[..., :half_rot]]
    reduce_sum x8 -> x2, other arithmetic: 14.7 us -> 6.69 us  [attend(): weight_sum = weight_sum * factor + jnp.sum(expo, axis=2)]
    dot_general x8 -> x2, matrix products: 14.7 us -> 8.81 us  [attend(): jnp.einsum('hqk,khd->qhd', expo.astype(jnp.bfloat16), values, preferred_e...]
    reshape x6 -> x1, local copies, waits for them, and re-layouts: 1.19 us -> 6.18 us  [local(): pool_rows = cache_pool.reshape(page_count * PAGE, 2, heads_here, HEAD_DIM)]
    neg x0 -> x2, local copies, waits for them, and re-layouts: none -> 4.95 us  [rotary(): -rotated_in[..., half_rot:]]
  transfers between devices with their start and end apart: 3 -> 3, of which waited for: 3 -> 3; matrix products, arithmetic and copies ran while one was open for 7% -> 10% of each run, Pallas kernels for 0% -> 0%
where the time goes in v5:
time: 307 us; the launch traced here: 306 us
  waiting for transfers between devices  79.6 us (26%)
  local copies, waits for them, and re-layouts  78.3 us (26%)
  Pallas kernels  48.6 us (16%)
  other arithmetic  31.5 us (10%)
  matrix products  27.6 us (9%)
  between operations  15.7 us (5%)
  starting transfers between devices  13.2 us (4%)
  blocking collectives  11.5 us (4%)
    pallas_call x1, Pallas kernels, cache_attention(): pl.pallas_call(body, grid=(heads, steps), in_specs=[pl.BlockSpec((1, rows...  48.6 us
    all_gather x1, waiting for transfers between devices, local(): all_heads = lax.all_gather(head_values, 'narrow', axis=1, tiled=True)  32.4 us
    all_gather x1, waiting for transfers between devices, local(): by_xz = lax.all_gather(by_x, 'wz', axis=0, tiled=False)  29.5 us
    all_to_all x1, waiting for transfers between devices, gather_columns(): received = lax.all_to_all(copies, 'narrow', 0, 0, tiled=False)  17.6 us
    reshape x2, local copies, waits for them, and re-layouts, local(): prefix_pages = prefix_whole.reshape(-1, PAGE, 2, heads_here, HEAD_DIM)  14.5 us
    all_to_all x1, starting transfers between devices, gather_columns(): received = lax.all_to_all(copies, 'narrow', 0, 0, tiled=False)  13.2 us
    all_gather x1, blocking collectives, local(): by_x = lax.all_gather(merged, 'wx', axis=0, tiled=False)  11.5 us
    dot_general x2, matrix products, attend(): jnp.einsum('qhd,khd->hqk', queries, keys, preferred_element_type=jnp.floa...  9.44 us
  transfers between devices with their start and end apart: 3, of which 3 were waited for; matrix products, arithmetic and copies ran while one was open for 10% of the time, Pallas kernels for 0%

profile of v5, /device:TPU:1, one launch (start us, length us, event | category | flops | bytes accessed | tf_op | source)
XLA Modules:
  0.0 306.1 jit_solution(9726745691077318860)
XLA Ops:
  9.5 11.5 %all-gather = bf16[128,1536]{1,0:T(8,128)(2,1)} all-gather(bf16[32,1536]{1,0:T(8,128)(2,1)S(1)} %pad_maximum_fusion.2), channel_id=2, replica_groups=mesh['wx'=4,'wz'=16,'narrow'=8] {'wx'}, dimensions={0}, use_global_device_ids=true | all-gather | bytes 491520 | tf_op jit(solution)/shard_map/all_gather | solution.py:147
  21.1 2.9 broadcast_in_dim.92
  23.9 13.2 %all-to-all-start = ((bf16[8,768,256]{2,1,0:T(8,128)(2,1)}), bf16[8,768,256]{2,1,0:T(8,128)(2,1)}, u32[]{:S(2)}, u32[]{:S(2)}) async-start(bf16[8,768,256]{2,1,0:T(8,128)(2,1)} %broadcast_in_dim.92), calls=%async_computation | async-start | bytes 6291456 | tf_op jit(solution)/shard_map/all_to_all | solution.py:113
  39.6 6.2 %reshape.223 = bf16[3072,2,4,64]{3,2,1,0:T(4,128)(2,1)} reshape(bf16[24,128,2,256]{3,2,1,0:T(2,128)(2,1)S(1)} %copy-done.8) | data formatting | bytes 6291456 | tf_op jit(solution)/shard_map/reshape | solution.py:199
  49.0 4.6 %fusion.49 = (bf16[3072,1,4,64]{3,2,1,0:T(4,128)(2,1)S(1)}, bf16[3072,1,4,64]{3,2,1,0:T(4,128)(2,1)S(1)}) fusion(bf16[3072,2,4,64]{3,2,1,0:T(4,128)(2,1)} %reshape.223), kind=kLoop, calls=%fused_computation.96 | loop fusion | bytes 6291456 | tf_op jit(solution)/shard_map/slice | solution.py:203
  53.6 3.5 %copy_bitcast_fusion = (bf16[4,3072,64]{2,1,0:T(8,128)(2,1)}, bf16[4,3072,64]{2,1,0:T(8,128)(2,1)}) fusion(bf16[3072,1,4,64]{3,2,1,0:T(4,128)(2,1)S(1)} %get-tuple-element.22, bf16[3072,1,4,64]{3,2,1,0:T(4,128)(2,1)S(1)} %get-tuple-element.23), kind=kLoop, calls=%fused_computation.17 | loop fusion | bytes 6291456 | tf_op jit(solution)/shard_map/transpose | solution.py:203
  57.0 17.6 %all-to-all-done = bf16[8,768,256]{2,1,0:T(8,128)(2,1)} async-done(((bf16[8,768,256]{2,1,0:T(8,128)(2,1)}), bf16[8,768,256]{2,1,0:T(8,128)(2,1)}, u32[]{:S(2)}, u32[]{:S(2)}) %all-to-all-start) | async-done | bytes 3145760 | tf_op jit(solution)/shard_map/all_to_all | solution.py:113
  74.7 3.2 %copy.126 = bf16[8,768,256]{1,2,0:T(8,128)(2,1)S(1)} copy(bf16[8,768,256]{2,1,0:T(8,128)(2,1)} %all-to-all-done) | data formatting | bytes 6291456 | tf_op jit(solution)/shard_map/all_to_all | solution.py:113
  79.3 2.6 fusion.7
  81.9 29.5 %all-gather.7.cloned.1.call-done = bf16[64,32,1536]{2,1,0:T(8,128)(2,1)} async-done(((bf16[4,32,1536]{2,1,0:T(8,128)(2,1)}), bf16[64,32,1536]{2,1,0:T(8,128)(2,1)}) %all-gather.7.cloned.1.call-update) | async-done | bytes 6291472 | tf_op jit(solution)/shard_map/all_gather | solution.py:148
  111.5 3.5 %copy.128 = bf16[4,16,32,1536]{3,2,1,0:T(8,128)(2,1)S(1)} copy(bf16[4,16,32,1536]{3,2,0,1:T(8,128)(2,1)} %bitcast.107) | data formatting | bytes 12582912 | tf_op jit(solution)/shard_map/transpose | solution.py:149
  115.0 2.7 copy-done.2
  117.9 3.0 copy.129
  120.9 5.5 %fusion.52 = f32[768,3,4,64]{0,3,2,1:T(8,128)S(1)} fusion(bf16[768,2048,1,1]{0,1,3,2:T(8,128)(2,1)} %bitcast.108, bf16[3,4,64,2048]{3,2,1,0:T(8,128)(2,1)} %bitcast.109), kind=kOutput, calls=%fused_computation.99 | convolution fusion | flops 2415919104 | bytes 8650752 | tf_op jit(solution)/shard_map/dot_general | solution.py:155
  131.9 3.1 slice.91
  154.2 7.5 %reshape.222 = bf16[16,128,2,4,64]{4,3,2,1,0:T(4,128)(2,1)} reshape(bf16[2048,512]{1,0:T(8,128)(2,1)} %slice.91) | data formatting | bytes 4194304 | tf_op jit(solution)/shard_map/reshape | solution.py:177
  161.7 7.0 %copy.148 = bf16[16,128,2,4,64]{1,4,3,2,0:T(8,128)(2,1)} copy(bf16[16,128,2,4,64]{4,3,2,1,0:T(4,128)(2,1)} %reshape.222) | data formatting | bytes 4194304 | tf_op jit(solution)/shard_map/reshape | solution.py:177
  174.8 3.7 %multiply_reduce_fusion = (f32[4,768]{1,0:T(4,128)S(1)}, f32[4,768,256]{1,2,0:T(8,128)}) fusion(bf16[256,2,4,64]{0,3,2,1:T(8,128)(2,1)S(1)} %bitcast_select_fusion, bf16[768,4,48]{2,0,1:T(8,128)(2,1)S(1)} %copy-done.4, bf16[768,4,16]{2,0,1:T(8,128)(2,1)} %copy-done.5), kind=kOutput, calls=%fused_computation.20 | convolution fusion | flops 103019520 | bytes 4173824 | tf_op jit(solution)/shard_map/qhd,khd->hqk/dot_general | solution.py:33
  182.6 48.6 %shard_map.113 = (f32[4,768,1]{2,1,0:T(8,128)}, f32[4,768,1]{2,1,0:T(8,128)}, f32[4,768,64]{2,1,0:T(8,128)}) custom-call(bf16[4,768,64]{2,1,0:T(8,128)(2,1)} %fusion.46.q_ref, bf16[4,3072,64]{2,1,0:T(8,128)(2,1)} %get-tuple-element.46.k_ref, bf16[4,3072,64]{2,1,0:T(8,128)(2,1)} %get-tuple-element.45.v_ref, s32[1,3072]{1,0:T(1,128)} %bitcast.117), custom_call_target="tpu_custom_call" | custom-call | tf_op jit(solution)/shard_map/pallas_call | solution.py:82
  235.1 5.8 %fusion = (f32[4,768]{1,0:T(4,128)S(1)}, f32[4,768,768]{1,2,0:T(8,128)}) fusion(pred[768,768]{0,1:T(8,128)(4,1)S(1)} %copy-done.7, bf16[768,4,64]{2,0,1:T(8,128)(2,1)S(1)} %maximum_convert_fusion, bf16[768,4,48]{2,0,1:T(8,128)(2,1)S(1)} %copy-done.4, bf16[768,4,16]{2,0,1:T(8,128)(2,1)S(1)} %copy-done.6), kind=kOutput, calls=%fused_computation.4 | convolution fusion | flops 309851136 | bytes 10825728 | tf_op jit(solution)/shard_map/qhd,khd->hqk/dot_general | solution.py:33
  245.4 6.1 %fusion.3 = f32[4,768]{1,0:T(4,128)S(1)} fusion(f32[4,768,768]{1,2,0:T(8,128)} %get-tuple-element.42, f32[4,768]{1,0:T(4,128)S(1)} %get-tuple-element.36, pred[768,768]{0,1:T(8,128)(4,1)S(1)} %copy-done.7), kind=kLoop, calls=%fused_computation.9 | loop fusion | flops 11793408 | bytes 10051584 | tf_op jit(solution)/shard_map/reduce_sum | solution.py:38
  251.7 6.8 %fusion.20 = bf16[768,4,64]{2,0,1:T(8,128)(2,1)S(1)} fusion(f32[4,768,64]{2,1,0:T(8,128)} %get-tuple-element.6, f32[4,64,768]{1,2,0:T(8,128)} %fusion.13, f32[4,768,768]{1,2,0:T(8,128)S(1)} %copy-done, f32[4,768]{1,0:T(4,128)S(1)} %get-tuple-element.36, pred[768,768]{0,1:T(8,128)(4,1)S(1)} %copy-done.7, f32[768,4]{0,1:T(4,128)S(1)} %get-tuple-element.33, ...), kind=kOutput, calls=%fused_computation.37 | convolution fusion | flops 315359232 | bytes 14032896 | tf_op jit(solution)/shard_map/hqk,khd->qhd/dot_general | solution.py:39
  262.9 32.4 %all-gather.5.cloned.1.call-done = bf16[768,2048]{0,1:T(8,128)(2,1)} async-done(((bf16[768,256]{0,1:T(8,128)(2,1)}), bf16[768,2048]{0,1:T(8,128)(2,1)}) %all-gather.5.cloned.1.call-update) | async-done | bytes 3145744 | tf_op jit(solution)/shard_map/all_gather | solution.py:223
  295.3 3.9 %convolution_convert_fusion = bf16[768,256]{1,0:T(8,128)(2,1)} fusion(bf16[768,2048]{0,1:T(8,128)(2,1)} %all-gather.5.cloned.1.call-done, bf16[2048,1536]{1,0:T(8,128)(2,1)} %bitcast.106), kind=kOutput, calls=%fused_computation.44 | convolution fusion | flops 805502976 | bytes 4587520 | tf_op jit(solution)/shard_map/dot_general | solution.py:225
  (90 shorter events, 56.1 us)
Async XLA Ops:
  7.2 104.3 %all-gather.7.cloned.1.call-start = ((), (), s32[]{:S(2)}) async-start(), calls=%async_computation.2 | async-start | bytes 6684672 | tf_op jit(solution)/shard_map/all_gather | solution.py:148
  23.9 14.7 %copy-start.13 = (f32[2048]{0:T(1024)S(1)}, f32[2048]{0:T(1024)}, u32[]{:S(2)}) copy-start(f32[2048]{0:T(1024)} %param.11) | copy-start | bytes 24580
  23.9 15.6 %copy-start.8 = (bf16[24,128,2,256]{3,2,1,0:T(2,128)(2,1)S(1)}, bf16[24,128,2,256]{3,2,1,0:T(2,128)(2,1)}, u32[]{:S(2)}) copy-start(bf16[24,128,2,256]{3,2,1,0:T(2,128)(2,1)} %param.14) | copy-start | bytes 9437188
  23.9 50.8 %all-to-all-start = ((bf16[8,768,256]{2,1,0:T(8,128)(2,1)}), bf16[8,768,256]{2,1,0:T(8,128)(2,1)}, u32[]{:S(2)}, u32[]{:S(2)}) async-start(bf16[8,768,256]{2,1,0:T(8,128)(2,1)} %broadcast_in_dim.92), calls=%async_computation | async-start | bytes 6291456 | tf_op jit(solution)/shard_map/all_to_all | solution.py:113
  37.1 258.2 %all-gather.5.cloned.1.call-start = ((), (), s32[]{:S(2)}) async-start(), calls=%async_computation.1 | async-start | bytes 3538944 | tf_op jit(solution)/shard_map/all_gather | solution.py:223
  39.6 6.9 %copy-start.15 = (s32[1,24]{1,0:T(1,128)S(1)}, s32[1,24]{1,0:T(1,128)}, u32[]{:S(2)}) copy-start(s32[1,24]{1,0:T(1,128)} %param.16) | copy-start | bytes 292
  39.6 7.5 %copy-start.14 = (s32[16]{0:T(128)S(1)}, s32[16]{0:T(128)}, u32[]{:S(2)}) copy-start(s32[16]{0:T(128)} %param.19) | copy-start | bytes 196
  115.0 2.7 copy-start.2
  126.3 1.7 copy-start.9
  168.7 2.5 copy-start.3
  170.3 0.9 copy-start.5
  171.2 3.6 %copy-start.4 = (bf16[768,4,48]{2,0,1:T(8,128)(2,1)S(1)}, bf16[768,4,48]{2,0,1:T(8,128)(2,1)}, u32[]{:S(2)}) copy-start(bf16[768,4,48]{2,0,1:T(8,128)(2,1)} %slice.116) | copy-start | bytes 884740
  172.5 6.0 %copy-start.12 = (f32[768,4,16]{0,2,1:T(8,128)S(1)}, f32[768,4,16]{0,2,1:T(8,128)}, u32[]{:S(2)}) copy-start(f32[768,4,16]{0,2,1:T(8,128)} %get-tuple-element.30) | copy-start | bytes 589828
  174.8 5.3 %copy-start.10 = (bf16[256,2,4,64]{0,3,2,1:T(8,128)(2,1)}, bf16[256,2,4,64]{0,3,2,1:T(8,128)(2,1)S(1)}, u32[]{:S(2)}) copy-start(bf16[256,2,4,64]{0,3,2,1:T(8,128)(2,1)S(1)} %bitcast_select_fusion) | copy-start | bytes 786436
  231.2 3.8 %copy-start.6 = (bf16[768,4,16]{2,0,1:T(8,128)(2,1)S(1)}, bf16[768,4,16]{2,0,1:T(8,128)(2,1)}, u32[]{:S(2)}) copy-start(bf16[768,4,16]{2,0,1:T(8,128)(2,1)} %copy-done.5) | copy-start | bytes 294916
  231.3 3.8 %copy-start.7 = (pred[768,768]{0,1:T(8,128)(4,1)S(1)}, pred[768,768]{0,1:T(8,128)(4,1)}, u32[]{:S(2)}) copy-start(pred[768,768]{0,1:T(8,128)(4,1)} %iota_compare_fusion) | copy-start | bytes 1769476
  235.1 5.8 %copy-start.1 = (f32[4,768,256]{1,2,0:T(8,128)S(1)}, f32[4,768,256]{1,2,0:T(8,128)}, u32[]{:S(2)}) copy-start(f32[4,768,256]{1,2,0:T(8,128)} %get-tuple-element.40) | copy-start | bytes 9437188
  235.1 5.8 %copy-start.11 = (bf16[256,2,4,64]{0,3,2,1:T(8,128)(2,1)S(1)}, bf16[256,2,4,64]{0,3,2,1:T(8,128)(2,1)}, u32[]{:S(2)}) copy-start(bf16[256,2,4,64]{0,3,2,1:T(8,128)(2,1)} %copy-done.10) | copy-start | bytes 786436
  245.4 6.4 %copy-start = (f32[4,768,768]{1,2,0:T(8,128)S(1)}, f32[4,768,768]{1,2,0:T(8,128)}, u32[]{:S(2)}) copy-start(f32[4,768,768]{1,2,0:T(8,128)} %get-tuple-element.42) | copy-start | bytes 28311556
Sparse Core Ops, SparseCore 0:
  21.2 90.2 all-gather.6
  259.7 35.5 all-gather.4

commit v6 on v3

--- a/solution.py
+++ b/solution.py
@@ -28,16 +28,16 @@
 
 def attend(running, queries, keys, values, key_valid):
     row_max, weight_sum, weighted = running
-    scores = jnp.einsum("qhd,khd->hqk", queries, keys, preferred_element_type=jnp.float32) * 0.125
+    scores = jnp.einsum("hqd,hkd->hqk", queries, keys, preferred_element_type=jnp.float32) * 0.125
     scores = jnp.where(key_valid[None], scores, NEGATIVE)
     new_max = jnp.maximum(row_max, jnp.max(scores, axis=2))
     expo = jnp.where(key_valid[None], jnp.exp(scores - new_max[:, :, None]), 0.0)
     factor = jnp.exp(row_max - new_max)
     weight_sum = weight_sum * factor + jnp.sum(expo, axis=2)
     update = jnp.einsum(
-        "hqk,khd->qhd", expo.astype(jnp.bfloat16), values, preferred_element_type=jnp.float32
+        "hqk,hkd->hqd", expo.astype(jnp.bfloat16), values, preferred_element_type=jnp.float32
     )
-    weighted = weighted * jnp.transpose(factor)[:, :, None] + update
+    weighted = weighted * factor[:, :, None] + update
     return (new_max, weight_sum, weighted)
 
 
@@ -104,9 +104,13 @@
     initial = (
         jnp.full((heads_here, span_rows), NEGATIVE, jnp.float32),
         jnp.zeros((heads_here, span_rows), jnp.float32),
-        jnp.zeros((span_rows, heads_here, HEAD_DIM), jnp.float32),
+        jnp.zeros((heads_here, span_rows, HEAD_DIM), jnp.float32),
     )
-    running = attend(initial, queries, keys, values, offset[:, None] >= offset[None, :])
+    head_major = lambda rows: jnp.transpose(rows, (1, 0, 2))
+    queries_hm = head_major(queries)
+    running = attend(
+        initial, queries_hm, head_major(keys), head_major(values), offset[:, None] >= offset[None, :]
+    )
     my_group = group_ids[0]
     prefix_pages = prefix_whole.reshape(-1, PAGE, 2, heads_here, HEAD_DIM)
     chosen = lax.dynamic_slice_in_dim(group_pages, my_group * PPAGES, PPAGES)
@@ -115,9 +119,9 @@
     )
     running = attend(
         running,
-        queries,
-        key_rows[:, 0],
-        key_rows[:, 1],
+        queries_hm,
+        head_major(key_rows[:, 0]),
+        head_major(key_rows[:, 1]),
         jnp.ones((span_rows, PPAGES * PAGE), dtype=bool),
     )
     page_list = page_table[0]
@@ -130,18 +134,21 @@
     block_keys = KB * PAGE
     key_offset = jnp.arange(block_keys, dtype=jnp.int32)
 
+    pool_rows = cache_pool.reshape(page_count * PAGE, 2, heads_here, HEAD_DIM)
+    pool_keys = head_major(pool_rows[:, 0])
+    pool_values = head_major(pool_rows[:, 1])
+
     def cache_block(block_index, state_now):
-        key_rows = lax.dynamic_slice_in_dim(cache_pool, block_index * KB, KB, axis=0).reshape(
-            block_keys, 2, heads_here, HEAD_DIM
-        )
+        block_keys_hm = lax.dynamic_slice_in_dim(pool_keys, block_index * block_keys, block_keys, axis=1)
+        block_values_hm = lax.dynamic_slice_in_dim(pool_values, block_index * block_keys, block_keys, axis=1)
         slots = lax.dynamic_slice_in_dim(slot_of_page, block_index * KB, KB)
         key_slot = jnp.repeat(slots, PAGE) * PAGE + key_offset % PAGE
         key_valid = jnp.broadcast_to((key_slot < length)[None, :], (span_rows, block_keys))
-        return attend(state_now, queries, key_rows[:, 0], key_rows[:, 1], key_valid)
+        return attend(state_now, queries_hm, block_keys_hm, block_values_hm, key_valid)
 
     running = lax.fori_loop(0, page_count // KB, cache_block, running)
     head_values = (
-        (running[2] / jnp.transpose(running[1])[:, :, None])
+        jnp.transpose(running[2] / running[1][:, :, None], (1, 0, 2))
         .astype(jnp.bfloat16)
         .reshape(span_rows, local_width)
     )

time: 254 us -> 256 us (level)
  waiting for transfers between devices: 94 us -> 80.1 us
  matrix products: 36.9 us -> 44.7 us
  local copies, waits for them, and re-layouts: 47.3 us -> 51 us
  other arithmetic: 34.3 us -> 37.6 us
    dynamic_slice x12 -> x0, local copies, waits for them, and re-layouts: 13.5 us -> none  [cache_block(): lax.dynamic_slice_in_dim(cache_pool, block_index * KB, KB, axis=0)]
    all_to_all x1, waiting for transfers between devices: 33.5 us -> 22.1 us  [gather_columns(): received = lax.all_to_all(copies, 'narrow', 0, 0, tiled=False)]
    dot_general x16, matrix products: 27.4 us -> 35.2 us  [the longest x8 19.2 us: attend(): jnp.einsum('hqk,hkd->hqd', expo.astype(jnp.bfloat16), values, preferred_e...]
    unnamed x19 -> x30, local copies, waits for them, and re-layouts: 4.03 us -> 10.4 us
    mul x6, other arithmetic: 0.47 us -> 4.53 us  [cache_block(): key_slot = jnp.repeat(slots, PAGE) * PAGE + key_offset % PAGE]
    while x6 -> x30, local copies, waits for them, and re-layouts: 0.02 us -> 3.62 us
    reshape x6 -> x1, local copies, waits for them, and re-layouts: 1.19 us -> 4.16 us  [local(): pool_rows = cache_pool.reshape(page_count * PAGE, 2, heads_here, HEAD_DIM)]
  transfers between devices with their start and end apart: 3 -> 3, of which waited for: 3 -> 3; matrix products, arithmetic and copies ran while one was open for 7% -> 12% of each run, Pallas kernels for 0% -> 0%
where the time goes in v6:
time: 256 us; the launch traced here: 255 us
  waiting for transfers between devices  80.1 us (31%)
  local copies, waits for them, and re-layouts  51 us (20%)
  matrix products  44.7 us (17%)
  other arithmetic  37.6 us (15%)
  between operations  15.7 us (6%)
  starting transfers between devices  13.2 us (5%)
  blocking collectives  11.5 us (4%)
    all_gather x1, waiting for transfers between devices, local(): by_xz = lax.all_gather(by_x, 'wz', axis=0, tiled=False)  29.5 us
    all_gather x1, waiting for transfers between devices, local(): all_heads = lax.all_gather(head_values, 'narrow', axis=1, tiled=True)  28.4 us
    all_to_all x1, waiting for transfers between devices, gather_columns(): received = lax.all_to_all(copies, 'narrow', 0, 0, tiled=False)  22.1 us
    dot_general x8, matrix products, attend(): jnp.einsum('hqk,hkd->hqd', expo.astype(jnp.bfloat16), values, preferred_e...  19.2 us
    dot_general x8, matrix products, attend(): jnp.einsum('hqd,hkd->hqk', queries, keys, preferred_element_type=jnp.floa...  16 us
    reduce_sum x8, other arithmetic, attend(): weight_sum = weight_sum * factor + jnp.sum(expo, axis=2)  14.7 us
    all_to_all x1, starting transfers between devices, gather_columns(): received = lax.all_to_all(copies, 'narrow', 0, 0, tiled=False)  13.2 us
    all_gather x1, blocking collectives, local(): by_x = lax.all_gather(merged, 'wx', axis=0, tiled=False)  11.5 us
  transfers between devices with their start and end apart: 3, of which 3 were waited for; matrix products, arithmetic and copies ran while one was open for 12% of the time, Pallas kernels for 0%

profile of v6, /device:TPU:1, one launch (start us, length us, event | category | flops | bytes accessed | tf_op | source)
XLA Modules:
  0.0 254.5 jit_solution(8455690350495356324)
XLA Ops:
  9.5 11.5 %all-gather = bf16[128,1536]{1,0:T(8,128)(2,1)} all-gather(bf16[32,1536]{1,0:T(8,128)(2,1)S(1)} %pad_maximum_fusion.1), channel_id=2, replica_groups=mesh['wx'=4,'wz'=16,'narrow'=8] {'wx'}, dimensions={0}, use_global_device_ids=true | all-gather | bytes 491520 | tf_op jit(solution)/shard_map/all_gather | solution.py:81
  21.1 2.8 %broadcast_in_dim.163 = bf16[8,768,256]{2,1,0:T(8,128)(2,1)} broadcast(bf16[768,256]{1,0:T(8,128)(2,1)} %param.12), dimensions={1,2} | broadcast | bytes 3538944 | tf_op jit(solution)/shard_map/broadcast_in_dim | solution.py:46
  23.9 13.2 %all-to-all-start = ((bf16[8,768,256]{2,1,0:T(8,128)(2,1)}), bf16[8,768,256]{2,1,0:T(8,128)(2,1)}, u32[]{:S(2)}, u32[]{:S(2)}) async-start(bf16[8,768,256]{2,1,0:T(8,128)(2,1)} %broadcast_in_dim.163), calls=%async_computation | async-start | bytes 6291456 | tf_op jit(solution)/shard_map/all_to_all | solution.py:47
  38.4 5.3 %copy.63 = bf16[24,128,2,256]{1,0,3,2:T(8,128)(2,1)} copy(bf16[24,128,2,256]{3,2,1,0:T(2,128)(2,1)S(1)} %copy-done.2) | data formatting | bytes 6291456 | tf_op args[4]
  43.7 4.2 %reshape.182 = bf16[3072,2,4,64]{0,3,2,1:T(8,128)(2,1)S(1)} reshape(bf16[24,128,2,256]{1,0,3,2:T(8,128)(2,1)} %copy.63) | data formatting | bytes 6291456 | tf_op jit(solution)/shard_map/reshape | solution.py:137
  52.6 22.1 %all-to-all-done = bf16[8,768,256]{2,1,0:T(8,128)(2,1)} async-done(((bf16[8,768,256]{2,1,0:T(8,128)(2,1)}), bf16[8,768,256]{2,1,0:T(8,128)(2,1)}, u32[]{:S(2)}, u32[]{:S(2)}) %all-to-all-start) | async-done | bytes 3145760 | tf_op jit(solution)/shard_map/all_to_all | solution.py:47
  74.6 3.2 %copy.53 = bf16[8,768,256]{1,2,0:T(8,128)(2,1)S(1)} copy(bf16[8,768,256]{2,1,0:T(8,128)(2,1)} %all-to-all-done) | data formatting | bytes 6291456 | tf_op jit(solution)/shard_map/all_to_all | solution.py:47
  79.3 2.7 %fusion.35 = bf16[8,768,256]{1,2,0:T(8,128)(2,1)} fusion(bf16[8,768,256]{1,2,0:T(8,128)(2,1)S(1)} %copy.53, f32[8,256]{1,0:T(8,128)S(1)} %mul.206, f32[768]{0:T(1024)S(1)} %add_rsqrt_fusion, f32[768]{0:T(1024)S(1)} %broadcast_multiply_fusion), kind=kLoop, calls=%fused_computation.44 | loop fusion | flops 7864320 | bytes 6305792 | tf_op jit(solution)/shard_map/convert.3
  81.9 29.5 %all-gather.7.cloned.1.call-done = bf16[64,32,1536]{2,1,0:T(8,128)(2,1)} async-done(((bf16[4,32,1536]{2,1,0:T(8,128)(2,1)}), bf16[64,32,1536]{2,1,0:T(8,128)(2,1)}) %all-gather.7.cloned.1.call-update) | async-done | bytes 6291472 | tf_op jit(solution)/shard_map/all_gather | solution.py:82
  111.5 3.5 %copy.55 = bf16[4,16,32,1536]{3,2,1,0:T(8,128)(2,1)S(1)} copy(bf16[4,16,32,1536]{3,2,0,1:T(8,128)(2,1)} %bitcast.115) | data formatting | bytes 12582912 | tf_op jit(solution)/shard_map/transpose | solution.py:83
  119.1 2.9 %copy.56 = bf16[768,2048]{1,0:T(8,128)(2,1)} copy(bf16[768,2048]{0,1:T(8,128)(2,1)S(1)} %slice_bitcast_fusion) | data formatting | bytes 6291456 | tf_op jit(solution)/shard_map/dot_general | solution.py:89
  122.0 5.6 %fusion.71 = f32[768,3,4,64]{0,3,2,1:T(8,128)S(1)} fusion(bf16[768,2048,1,1]{0,1,3,2:T(8,128)(2,1)} %bitcast.116, bf16[3,4,64,2048]{3,2,1,0:T(8,128)(2,1)} %bitcast.117), kind=kOutput, calls=%fused_computation.114 | convolution fusion | flops 2415919104 | bytes 8650752 | tf_op jit(solution)/shard_map/dot_general | solution.py:89
  130.6 3.6 %reshape.204 = bf16[16,128,2,4,64]{4,3,2,1,0:T(4,128)(2,1)} reshape(bf16[2048,512]{1,0:T(8,128)(2,1)S(1)} %copy-done.1) | data formatting | bytes 4194304 | tf_op jit(solution)/shard_map/reshape | solution.py:115
  134.1 5.9 %copy.59 = bf16[16,128,2,4,64]{1,4,3,2,0:T(8,128)(2,1)S(1)} copy(bf16[16,128,2,4,64]{4,3,2,1,0:T(4,128)(2,1)} %reshape.204) | data formatting | bytes 4194304 | tf_op jit(solution)/shard_map/reshape | solution.py:115
  148.6 2.8 %fusion.51 = f32[4,768,64]{1,2,0:T(8,128)S(1)} fusion(f32[4,768,768]{1,2,0:T(8,128)S(1)} %get-tuple-element.354, f32[4,768]{1,0:T(4,128)S(1)} %get-tuple-element.350, pred[768,768]{0,1:T(8,128)(4,1)S(1)} %copy-done.4, f32[4,768]{1,0:T(4,128)S(1)} %get-tuple-element.335, f32[4,768]{1,0:T(4,128)S(1)} %get-tuple-element.348, f32[768,3,4,64]{0,3,2,1:T(8,128)S(1)} %copy-done.6), kind=kOutput, calls=%fused_computation.60 | convolution fusion | flops 314179584 | bytes 11243520 | tf_op jit(solution)/shard_map/hqk,hkd->hqd/dot_general | solution.py:37
  152.1 54.4 %while.21 = (s32[]{:T(128)}, f32[4,768]{1,0:T(4,128)S(1)}, f32[4,768]{1,0:T(4,128)}, f32[4,768,64]{1,2,0:T(8,128)S(1)}, s32[24]{0:T(128)}, /*index=5*/s32[]{:T(1...) while((s32[]{:T(128)}, f32[4,768]{1,0:T(4,128)S(1)}, ...), condition=%wide.region_10.11_spmd.clone, body=%wide.region_7.10_spmd.clone.sunk | while | flops 423503872 | bytes 21662560 | solution.py:149
  158.7 2.6 %fusion.88 = f32[4,768,64]{1,2,0:T(8,128)S(1)} fusion(f32[4,512,768]{2,1,0:T(8,128)S(1)} %get-tuple-element.421, f32[4,768]{1,0:T(4,128)S(1)} %max.28, pred[512]{0:T(512)(128)(4,1)S(1)} %fusion.86, f32[4,768,64]{1,2,0:T(8,128)S(1)} %get-tuple-element.442, f32[4,768]{1,0:T(4,128)S(1)} %get-tuple-element.423, ...), kind=kOutput, calls=%fused_computation.14.clone.1 | convolution fusion | flops 209584128 | bytes 8152068 | tf_op jit(solution)/shard_map/while/body/eval_jaxpr/hqk,hkd->hqd/dot_general | solution.py:37
  167.7 2.6 %fusion.88 = f32[4,768,64]{1,2,0:T(8,128)S(1)} fusion(f32[4,512,768]{2,1,0:T(8,128)S(1)} %get-tuple-element.421, f32[4,768]{1,0:T(4,128)S(1)} %max.28, pred[512]{0:T(512)(128)(4,1)S(1)} %fusion.86, f32[4,768,64]{1,2,0:T(8,128)S(1)} %get-tuple-element.442, f32[4,768]{1,0:T(4,128)S(1)} %get-tuple-element.423, ...), kind=kOutput, calls=%fused_computation.14.clone.1 | convolution fusion | flops 209584128 | bytes 8152068 | tf_op jit(solution)/shard_map/while/body/eval_jaxpr/hqk,hkd->hqd/dot_general | solution.py:37
  176.7 2.6 %fusion.88 = f32[4,768,64]{1,2,0:T(8,128)S(1)} fusion(f32[4,512,768]{2,1,0:T(8,128)S(1)} %get-tuple-element.421, f32[4,768]{1,0:T(4,128)S(1)} %max.28, pred[512]{0:T(512)(128)(4,1)S(1)} %fusion.86, f32[4,768,64]{1,2,0:T(8,128)S(1)} %get-tuple-element.442, f32[4,768]{1,0:T(4,128)S(1)} %get-tuple-element.423, ...), kind=kOutput, calls=%fused_computation.14.clone.1 | convolution fusion | flops 209584128 | bytes 8152068 | tf_op jit(solution)/shard_map/while/body/eval_jaxpr/hqk,hkd->hqd/dot_general | solution.py:37
  185.8 2.6 %fusion.88 = f32[4,768,64]{1,2,0:T(8,128)S(1)} fusion(f32[4,512,768]{2,1,0:T(8,128)S(1)} %get-tuple-element.421, f32[4,768]{1,0:T(4,128)S(1)} %max.28, pred[512]{0:T(512)(128)(4,1)S(1)} %fusion.86, f32[4,768,64]{1,2,0:T(8,128)S(1)} %get-tuple-element.442, f32[4,768]{1,0:T(4,128)S(1)} %get-tuple-element.423, ...), kind=kOutput, calls=%fused_computation.14.clone.1 | convolution fusion | flops 209584128 | bytes 8152068 | tf_op jit(solution)/shard_map/while/body/eval_jaxpr/hqk,hkd->hqd/dot_general | solution.py:37
  194.8 2.6 %fusion.88 = f32[4,768,64]{1,2,0:T(8,128)S(1)} fusion(f32[4,512,768]{2,1,0:T(8,128)S(1)} %get-tuple-element.421, f32[4,768]{1,0:T(4,128)S(1)} %max.28, pred[512]{0:T(512)(128)(4,1)S(1)} %fusion.86, f32[4,768,64]{1,2,0:T(8,128)S(1)} %get-tuple-element.442, f32[4,768]{1,0:T(4,128)S(1)} %get-tuple-element.423, ...), kind=kOutput, calls=%fused_computation.14.clone.1 | convolution fusion | flops 209584128 | bytes 8152068 | tf_op jit(solution)/shard_map/while/body/eval_jaxpr/hqk,hkd->hqd/dot_general | solution.py:37
  212.7 2.7 %pad_maximum_fusion = bf16[768,2,256]{2,1,0:T(2,128)(2,1)} fusion(bf16[768,1,256]{2,1,0:T(2,128)(2,1)S(1)} %copy.65, bf16[768,1,256]{2,1,0:T(2,128)(2,1)S(1)} %copy.64), kind=kLoop, calls=%fused_computation.67 | loop fusion | flops 1572864 | bytes 1572864 | tf_op jit(solution)/shard_map/stack | solution.py:101
  215.3 28.4 %all-gather.5.cloned.1.call-done = bf16[768,2048]{0,1:T(8,128)(2,1)} async-done(((bf16[768,256]{0,1:T(8,128)(2,1)}), bf16[768,2048]{0,1:T(8,128)(2,1)}) %all-gather.5.cloned.1.call-update) | async-done | bytes 3145744 | tf_op jit(solution)/shard_map/all_gather | solution.py:155
  243.7 3.9 %convolution_convert_fusion = bf16[768,256]{1,0:T(8,128)(2,1)} fusion(bf16[768,2048]{0,1:T(8,128)(2,1)} %all-gather.5.cloned.1.call-done, bf16[2048,1536]{1,0:T(8,128)(2,1)} %bitcast.114), kind=kOutput, calls=%fused_computation.61 | convolution fusion | flops 805502976 | bytes 4587520 | tf_op jit(solution)/shard_map/dot_general | solution.py:157
  (142 shorter events, 71.2 us)
Async XLA Ops:
  7.2 104.3 %all-gather.7.cloned.1.call-start = ((), (), s32[]{:S(2)}) async-start(), calls=%async_computation.2 | async-start | bytes 6684672 | tf_op jit(solution)/shard_map/all_gather | solution.py:82
  23.9 13.2 %copy-start.13 = (f32[2048]{0:T(1024)S(1)}, f32[2048]{0:T(1024)}, u32[]{:S(2)}) copy-start(f32[2048]{0:T(1024)} %param.13) | copy-start | bytes 24580
  23.9 14.5 %copy-start.2 = (bf16[24,128,2,256]{3,2,1,0:T(2,128)(2,1)S(1)}, bf16[24,128,2,256]{3,2,1,0:T(2,128)(2,1)}, u32[]{:S(2)}) copy-start(bf16[24,128,2,256]{3,2,1,0:T(2,128)(2,1)} %param.16) | copy-start | bytes 9437188
  23.9 50.7 %all-to-all-start = ((bf16[8,768,256]{2,1,0:T(8,128)(2,1)}), bf16[8,768,256]{2,1,0:T(8,128)(2,1)}, u32[]{:S(2)}, u32[]{:S(2)}) async-start(bf16[8,768,256]{2,1,0:T(8,128)(2,1)} %broadcast_in_dim.163), calls=%async_computation | async-start | bytes 6291456 | tf_op jit(solution)/shard_map/all_to_all | solution.py:47
  37.1 206.7 %all-gather.5.cloned.1.call-start = ((), (), s32[]{:S(2)}) async-start(), calls=%async_computation.1 | async-start | bytes 3538944 | tf_op jit(solution)/shard_map/all_gather | solution.py:155
  43.7 4.2 %copy-start.15 = (s32[1,24]{1,0:T(1,128)S(1)}, s32[1,24]{1,0:T(1,128)}, u32[]{:S(2)}) copy-start(s32[1,24]{1,0:T(1,128)} %param.18) | copy-start | bytes 292
  43.7 5.4 %copy-start.14 = (s32[16]{0:T(128)S(1)}, s32[16]{0:T(128)}, u32[]{:S(2)}) copy-start(s32[16]{0:T(128)} %param.21) | copy-start | bytes 196
  115.0 2.7 %copy-start = (bf16[4,16,32,1536]{3,2,1,0:T(8,128)(2,1)}, bf16[4,16,32,1536]{3,2,1,0:T(8,128)(2,1)S(1)}, u32[]{:S(2)}) copy-start(bf16[4,16,32,1536]{3,2,1,0:T(8,128)(2,1)S(1)} %copy.55) | copy-start | bytes 18874372
  127.6 1.8 copy-start.5
  127.6 3.0 %copy-start.1 = (bf16[2048,512]{1,0:T(8,128)(2,1)S(1)}, bf16[2048,512]{1,0:T(8,128)(2,1)}, u32[]{:S(2)}) copy-start(bf16[2048,512]{1,0:T(8,128)(2,1)} %slice.90) | copy-start | bytes 6291460
  127.7 0.9 copy-start.3
  140.7 1.9 copy-start.11
  140.7 1.9 copy-start.12
  140.7 2.0 copy-start.4
  140.7 2.0 copy-start.7
  142.7 1.8 copy-start.10
  146.9 1.7 copy-start.6
  156.1 2.0 copy-start.8
  165.1 2.0 copy-start.8
  167.1 0.6 copy-start.9
  174.1 2.0 copy-start.8
  183.2 2.0 copy-start.8
  192.2 2.0 copy-start.8
  201.2 2.0 copy-start.8
  (5 other events, 3.0 us)
Sparse Core Ops, SparseCore 0:
  21.2 90.2 all-gather.6
  208.1 35.5 all-gather.4

commit v7 on v3

--- a/solution.py
+++ b/solution.py
@@ -6,7 +6,7 @@
 HEAD_DIM = 64
 ROT = 16
 PAGE = 128
-KB = 4
+KB = 8
 PPAGES = 2
 
 
@@ -78,7 +78,10 @@
         ],
         axis=1,
     )
-    by_x = lax.all_gather(merged, "wx", axis=0, tiled=False)
+    along_x = lax.axis_size("wx")
+    by_x = lax.all_to_all(
+        jnp.broadcast_to(merged[None], (along_x,) + merged.shape), "wx", 0, 0, tiled=False
+    )
     by_xz = lax.all_gather(by_x, "wz", axis=0, tiled=False)
     merged_whole = jnp.transpose(by_xz, (1, 0, 2, 3)).reshape(-1, merged.shape[1])
     piece_rows = merged_whole[:, : 3 * local_width]

time: 254 us -> 245 us (0.965)
  local copies, waits for them, and re-layouts: 47.3 us -> 44.5 us
    all_gather x1 -> x0, blocking collectives: 11.5 us -> none  [local(): by_x = lax.all_gather(merged, 'wx', axis=0, tiled=False)]
    all_to_all x0 -> x1, blocking collectives: none -> 11 us  [local(): lax.all_to_all(jnp.broadcast_to(merged[None], (along_x,) + merged.shape),...]
    dynamic_slice x12 -> x6, local copies, waits for them, and re-layouts: 13.5 us -> 10.3 us  [cache_block(): lax.dynamic_slice_in_dim(cache_pool, block_index * KB, KB, axis=0)]
    dot_general x8 -> x5, matrix products: 14.7 us -> 13.7 us  [attend(): jnp.einsum('hqk,khd->qhd', expo.astype(jnp.bfloat16), values, preferred_e...]
    reduce_sum x8 -> x5, other arithmetic: 14.7 us -> 14.9 us  [attend(): weight_sum = weight_sum * factor + jnp.sum(expo, axis=2)]
    dot_general x8 -> x5, matrix products: 12.6 us -> 12.5 us  [attend(): jnp.einsum('qhd,khd->hqk', queries, keys, preferred_element_type=jnp.floa...]
  transfers between devices with their start and end apart: 3 -> 3, of which waited for: 3 -> 3; matrix products, arithmetic and copies ran while one was open for 7% -> 8% of each run, Pallas kernels for 0% -> 0%
where the time goes in v7:
time: 245 us; the launch traced here: 244 us
  waiting for transfers between devices  92.7 us (38%)
  local copies, waits for them, and re-layouts  44.5 us (18%)
  matrix products  35.8 us (15%)
  other arithmetic  33 us (13%)
  between operations  15.7 us (6%)
  blocking collectives  11 us (4%)
  starting transfers between devices  10.7 us (4%)
    all_to_all x1, waiting for transfers between devices, gather_columns(): received = lax.all_to_all(copies, 'narrow', 0, 0, tiled=False)  33.5 us
    all_gather x1, waiting for transfers between devices, local(): all_heads = lax.all_gather(head_values, 'narrow', axis=1, tiled=True)  29.6 us
    all_gather x1, waiting for transfers between devices, local(): by_xz = lax.all_gather(by_x, 'wz', axis=0, tiled=False)  29.6 us
    reduce_sum x5, other arithmetic, attend(): weight_sum = weight_sum * factor + jnp.sum(expo, axis=2)  14.9 us
    dot_general x5, matrix products, attend(): jnp.einsum('hqk,khd->qhd', expo.astype(jnp.bfloat16), values, preferred_e...  13.7 us
    dot_general x5, matrix products, attend(): jnp.einsum('qhd,khd->hqk', queries, keys, preferred_element_type=jnp.floa...  12.5 us
    all_to_all x1, blocking collectives, local(): lax.all_to_all(jnp.broadcast_to(merged[None], (along_x,) + merged.shape),...  11 us
    all_to_all x1, starting transfers between devices, gather_columns(): received = lax.all_to_all(copies, 'narrow', 0, 0, tiled=False)  10.7 us
  transfers between devices with their start and end apart: 3, of which 3 were waited for; matrix products, arithmetic and copies ran while one was open for 8% of the time, Pallas kernels for 0%

profile of v7, /device:TPU:1, one launch (start us, length us, event | category | flops | bytes accessed | tf_op | source)
XLA Modules:
  0.0 243.8 jit_solution(13240682312993087615)
XLA Ops:
  9.6 11.0 %all_to_all.10 = bf16[4,32,1536]{2,1,0:T(8,128)(2,1)} all-to-all(bf16[4,32,1536]{2,1,0:T(8,128)(2,1)S(1)} %broadcast_in_dim.174), channel_id=1, replica_groups=mesh['wx'=4,'wz'=16,'narrow'=8] {'wx'}, dimensions={0} | all-to-all | bytes 786432 | tf_op jit(solution)/shard_map/all_to_all | solution.py:82
  20.6 2.8 %broadcast_in_dim.173 = bf16[8,768,256]{2,1,0:T(8,128)(2,1)} broadcast(bf16[768,256]{1,0:T(8,128)(2,1)} %param.12), dimensions={1,2} | broadcast | bytes 3538944 | tf_op jit(solution)/shard_map/broadcast_in_dim | solution.py:46
  23.4 10.7 %all-to-all-start = ((bf16[8,768,256]{2,1,0:T(8,128)(2,1)}), bf16[8,768,256]{2,1,0:T(8,128)(2,1)}, u32[]{:S(2)}, u32[]{:S(2)}) async-start(bf16[8,768,256]{2,1,0:T(8,128)(2,1)} %broadcast_in_dim.173), calls=%async_computation | async-start | bytes 6291456 | tf_op jit(solution)/shard_map/all_to_all | solution.py:47
  38.1 33.5 %all-to-all-done = bf16[8,768,256]{2,1,0:T(8,128)(2,1)} async-done(((bf16[8,768,256]{2,1,0:T(8,128)(2,1)}), bf16[8,768,256]{2,1,0:T(8,128)(2,1)}, u32[]{:S(2)}, u32[]{:S(2)}) %all-to-all-start) | async-done | bytes 3145760 | tf_op jit(solution)/shard_map/all_to_all | solution.py:47
  71.6 3.2 %copy.53 = bf16[8,768,256]{1,2,0:T(8,128)(2,1)S(1)} copy(bf16[8,768,256]{2,1,0:T(8,128)(2,1)} %all-to-all-done) | data formatting | bytes 6291456 | tf_op jit(solution)/shard_map/all_to_all | solution.py:47
  78.9 29.6 %all-gather.6.cloned.1.call-done = bf16[64,32,1536]{2,1,0:T(8,128)(2,1)} async-done(((bf16[4,32,1536]{2,1,0:T(8,128)(2,1)}), bf16[64,32,1536]{2,1,0:T(8,128)(2,1)}) %all-gather.6.cloned.1.call-update) | async-done | bytes 6291472 | tf_op jit(solution)/shard_map/all_gather | solution.py:85
  108.5 3.5 %copy.55 = bf16[4,16,32,1536]{3,2,1,0:T(8,128)(2,1)S(1)} copy(bf16[4,16,32,1536]{3,2,0,1:T(8,128)(2,1)} %bitcast.129) | data formatting | bytes 12582912 | tf_op jit(solution)/shard_map/transpose | solution.py:86
  114.9 3.0 %copy.56 = bf16[768,2048]{1,0:T(8,128)(2,1)} copy(bf16[768,2048]{0,1:T(8,128)(2,1)S(1)} %slice_bitcast_fusion.4) | data formatting | bytes 6291456 | tf_op jit(solution)/shard_map/dot_general | solution.py:92
  117.8 5.6 %fusion.79 = f32[768,3,4,64]{0,3,2,1:T(8,128)S(1)} fusion(bf16[768,2048,1,1]{0,1,3,2:T(8,128)(2,1)} %bitcast.130, bf16[3,4,64,2048]{3,2,1,0:T(8,128)(2,1)} %bitcast.131), kind=kOutput, calls=%fused_computation.117 | convolution fusion | flops 2415919104 | bytes 8650752 | tf_op jit(solution)/shard_map/dot_general | solution.py:92
  126.9 3.6 %reshape.204 = bf16[16,128,2,4,64]{4,3,2,1,0:T(4,128)(2,1)} reshape(bf16[2048,512]{1,0:T(8,128)(2,1)S(1)} %slice.108) | data formatting | bytes 4194304 | tf_op jit(solution)/shard_map/reshape | solution.py:114
  130.5 5.9 %copy.59 = bf16[16,128,2,4,64]{1,4,3,2,0:T(8,128)(2,1)S(1)} copy(bf16[16,128,2,4,64]{4,3,2,1,0:T(4,128)(2,1)} %reshape.204) | data formatting | bytes 4194304 | tf_op jit(solution)/shard_map/reshape | solution.py:114
  142.0 3.0 %fusion.28 = (f32[4,768]{1,0:T(4,128)S(1)}, f32[4,768,768]{1,2,0:T(8,128)S(1)}) fusion(pred[768,768]{0,1:T(8,128)(4,1)} %iota_compare_fusion, bf16[768,4,48]{0,2,1:T(8,128)(2,1)S(1)} %slice.139, bf16[768,4,16]{0,2,1:T(8,128)(2,1)} %fusion.64, bf16[768,4,48]{0,2,1:T(8,128)(2,1)S(1)} %slice.107, bf16[768,4,16]{0,2,1:T(8,128)(2,1)} %fusion.62), kind=kOutput, calls=%fused_computation.36 | convolution fusion | flops 310637568 | bytes 10825728 | tf_op jit(solution)/shard_map/qhd,khd->hqk/dot_general | solution.py:31
  147.5 3.9 %fusion.57 = f32[768,4,64]{0,2,1:T(8,128)S(1)} fusion(f32[4,768,768]{1,2,0:T(8,128)S(1)} %get-tuple-element.361, f32[4,768]{1,0:T(4,128)S(1)} %get-tuple-element.356, pred[768,768]{0,1:T(8,128)(4,1)S(1)} %copy-done.2, f32[768,4]{0,1:T(4,128)S(1)} %get-tuple-element.355, f32[768,4]{0,1:T(4,128)S(1)} %get-tuple-element.354, f32[768,3,4,64]{0,3,2,1:T(8,128)} %copy-done.3), kind=kOutput, calls=%fused_computation.61 | convolution fusion | flops 314179584 | bytes 11243520 | tf_op jit(solution)/shard_map/hqk,khd->qhd/dot_general | solution.py:37
  152.7 43.8 %while.21 = (s32[]{:T(128)}, f32[4,768]{1,0:T(4,128)S(1)}, f32[4,768]{1,0:T(4,128)S(1)}, f32[768,4,64]{0,2,1:T(8,128)S(1)}, s32[24]{0:T(128)S(1)}, /*index=5*/s3...) while((s32[]{:T(128)}, f32[4,768]{1,0:T(4,128)S(1)}, ...), condition=%wide.region_10.11_spmd.clone, body=%wide.region_7.10_spmd.clone.sunk | while | flops 846611456 | bytes 47256848 | solution.py:145
  160.4 3.0 %fusion.96 = f32[768,4,64]{0,2,1:T(8,128)S(1)} fusion(f32[4,1024,768]{2,1,0:T(8,128)S(1)} %get-tuple-element.423, f32[4,768]{1,0:T(4,128)S(1)} %get-tuple-element.450, pred[1024]{0:T(1024)(128)(4,1)S(1)} %fusion.93, f32[768,4,64]{0,2,1:T(8,128)S(1)} %get-tuple-element.440, bf16[1024,2,4,64]{0,3,2,1:T(8,128)(2,1)S(1)} %reshape.208, ...), kind=kOutput, calls=%fused_computation.15.clone.1 | convolution fusion | flops 418775040 | bytes 14706688 | tf_op jit(solution)/shard_map/while/body/eval_jaxpr/hqk,khd->qhd/dot_general | solution.py:37
  163.4 4.0 %fusion.95 = f32[4,768]{1,0:T(4,128)S(1)} fusion(f32[4,1024,768]{2,1,0:T(8,128)S(1)} %get-tuple-element.423, f32[4,768]{1,0:T(4,128)S(1)} %get-tuple-element.450, pred[1024]{0:T(1024)(128)(4,1)S(1)} %fusion.93), kind=kLoop, calls=%fused_computation.10.clone.1 | loop fusion | flops 15725568 | bytes 12608512 | tf_op jit(solution)/shard_map/while/body/eval_jaxpr/reduce_sum | solution.py:36
  174.9 3.0 %fusion.96 = f32[768,4,64]{0,2,1:T(8,128)S(1)} fusion(f32[4,1024,768]{2,1,0:T(8,128)S(1)} %get-tuple-element.423, f32[4,768]{1,0:T(4,128)S(1)} %get-tuple-element.450, pred[1024]{0:T(1024)(128)(4,1)S(1)} %fusion.93, f32[768,4,64]{0,2,1:T(8,128)S(1)} %get-tuple-element.440, bf16[1024,2,4,64]{0,3,2,1:T(8,128)(2,1)S(1)} %reshape.208, ...), kind=kOutput, calls=%fused_computation.15.clone.1 | convolution fusion | flops 418775040 | bytes 14706688 | tf_op jit(solution)/shard_map/while/body/eval_jaxpr/hqk,khd->qhd/dot_general | solution.py:37
  177.9 4.0 %fusion.95 = f32[4,768]{1,0:T(4,128)S(1)} fusion(f32[4,1024,768]{2,1,0:T(8,128)S(1)} %get-tuple-element.423, f32[4,768]{1,0:T(4,128)S(1)} %get-tuple-element.450, pred[1024]{0:T(1024)(128)(4,1)S(1)} %fusion.93), kind=kLoop, calls=%fused_computation.10.clone.1 | loop fusion | flops 15725568 | bytes 12608512 | tf_op jit(solution)/shard_map/while/body/eval_jaxpr/reduce_sum | solution.py:36
  186.7 2.7 %bitcast_reduce_fusion.2 = (f32[4,768]{1,0:T(4,128)S(1)}, f32[4,1024,768]{2,1,0:T(8,128)S(1)}) fusion(pred[1024]{0:T(1024)(128)(4,1)S(1)} %fusion.93, bf16[768,4,64]{0,2,1:T(8,128)(2,1)S(1)} %get-tuple-element.456, bf16[1024,2,4,64]{0,3,2,1:T(8,128)(2,1)S(1)} %reshape.208), kind=kOutput, calls=%fused_computation.5.clone.1 | convolution fusion | flops 412087296 | bytes 13513728 | tf_op jit(solution)/shard_map/while/body/eval_jaxpr/qhd,khd->hqk/dot_general | solution.py:31
  189.4 3.0 %fusion.96 = f32[768,4,64]{0,2,1:T(8,128)S(1)} fusion(f32[4,1024,768]{2,1,0:T(8,128)S(1)} %get-tuple-element.423, f32[4,768]{1,0:T(4,128)S(1)} %get-tuple-element.450, pred[1024]{0:T(1024)(128)(4,1)S(1)} %fusion.93, f32[768,4,64]{0,2,1:T(8,128)S(1)} %get-tuple-element.440, bf16[1024,2,4,64]{0,3,2,1:T(8,128)(2,1)S(1)} %reshape.208, ...), kind=kOutput, calls=%fused_computation.15.clone.1 | convolution fusion | flops 418775040 | bytes 14706688 | tf_op jit(solution)/shard_map/while/body/eval_jaxpr/hqk,khd->qhd/dot_general | solution.py:37
  192.4 4.0 %fusion.95 = f32[4,768]{1,0:T(4,128)S(1)} fusion(f32[4,1024,768]{2,1,0:T(8,128)S(1)} %get-tuple-element.423, f32[4,768]{1,0:T(4,128)S(1)} %get-tuple-element.450, pred[1024]{0:T(1024)(128)(4,1)S(1)} %fusion.93), kind=kLoop, calls=%fused_computation.10.clone.1 | loop fusion | flops 15725568 | bytes 12608512 | tf_op jit(solution)/shard_map/while/body/eval_jaxpr/reduce_sum | solution.py:36
  200.8 2.7 %pad_maximum_fusion = bf16[768,2,256]{2,1,0:T(2,128)(2,1)} fusion(bf16[768,1,256]{2,1,0:T(2,128)(2,1)S(1)} %copy.65, bf16[768,1,256]{2,1,0:T(2,128)(2,1)S(1)} %copy.64), kind=kLoop, calls=%fused_computation.68 | loop fusion | flops 1572864 | bytes 1572864 | tf_op jit(solution)/shard_map/stack | solution.py:104
  203.4 29.6 %all-gather.4.cloned.1.call-done = bf16[768,2048]{0,1:T(8,128)(2,1)} async-done(((bf16[768,256]{0,1:T(8,128)(2,1)}), bf16[768,2048]{0,1:T(8,128)(2,1)}) %all-gather.4.cloned.1.call-update) | async-done | bytes 3145744 | tf_op jit(solution)/shard_map/all_gather | solution.py:151
  233.0 3.9 %convolution_convert_fusion = bf16[768,256]{1,0:T(8,128)(2,1)} fusion(bf16[768,2048]{0,1:T(8,128)(2,1)} %all-gather.4.cloned.1.call-done, bf16[2048,1536]{1,0:T(8,128)(2,1)} %bitcast.128), kind=kOutput, calls=%fused_computation.62 | convolution fusion | flops 805502976 | bytes 4587520 | tf_op jit(solution)/shard_map/dot_general | solution.py:153
  (94 shorter events, 48.4 us)
Async XLA Ops:
  7.2 26.9 %copy-start.7 = (f32[2048]{0:T(1024)S(1)}, f32[2048]{0:T(1024)}, u32[]{:S(2)}) copy-start(f32[2048]{0:T(1024)} %param.13) | copy-start | bytes 24580
  7.2 28.2 %copy-start.9 = (s32[1,24]{1,0:T(1,128)S(1)}, s32[1,24]{1,0:T(1,128)}, u32[]{:S(2)}) copy-start(s32[1,24]{1,0:T(1,128)} %param.18) | copy-start | bytes 292
  7.2 28.9 %copy-start.8 = (s32[16]{0:T(128)S(1)}, s32[16]{0:T(128)}, u32[]{:S(2)}) copy-start(s32[16]{0:T(128)} %param.21) | copy-start | bytes 196
  7.2 101.3 %all-gather.6.cloned.1.call-start = ((), (), s32[]{:S(2)}) async-start(), calls=%async_computation.3 | async-start | bytes 6684672 | tf_op jit(solution)/shard_map/all_gather | solution.py:85
  23.4 48.2 %all-to-all-start = ((bf16[8,768,256]{2,1,0:T(8,128)(2,1)}), bf16[8,768,256]{2,1,0:T(8,128)(2,1)}, u32[]{:S(2)}, u32[]{:S(2)}) async-start(bf16[8,768,256]{2,1,0:T(8,128)(2,1)} %broadcast_in_dim.173), calls=%async_computation | async-start | bytes 6291456 | tf_op jit(solution)/shard_map/all_to_all | solution.py:47
  34.1 199.0 %all-gather.4.cloned.1.call-start = ((), (), s32[]{:S(2)}) async-start(), calls=%async_computation.2 | async-start | bytes 3538944 | tf_op jit(solution)/shard_map/all_gather | solution.py:151
  112.0 2.7 %copy-start = (bf16[4,16,32,1536]{3,2,1,0:T(8,128)(2,1)}, bf16[4,16,32,1536]{3,2,1,0:T(8,128)(2,1)S(1)}, u32[]{:S(2)}) copy-start(bf16[4,16,32,1536]{3,2,1,0:T(8,128)(2,1)S(1)} %copy.55) | copy-start | bytes 18874372
  123.4 1.8 copy-start.3
  123.5 1.0 copy-start.1
  123.6 18.4 %copy-start.4 = (bf16[768,4,48]{0,2,1:T(8,128)(2,1)}, bf16[768,4,48]{0,2,1:T(8,128)(2,1)S(1)}, u32[]{:S(2)}) copy-start(bf16[768,4,48]{0,2,1:T(8,128)(2,1)S(1)} %slice.107) | copy-start | bytes 884740
  142.0 3.1 %copy-start.5 = (bf16[768,4,16]{0,2,1:T(8,128)(2,1)S(1)}, bf16[768,4,16]{0,2,1:T(8,128)(2,1)}, u32[]{:S(2)}) copy-start(bf16[768,4,16]{0,2,1:T(8,128)(2,1)} %fusion.64) | copy-start | bytes 294916
  142.0 3.1 %copy-start.2 = (pred[768,768]{0,1:T(8,128)(4,1)S(1)}, pred[768,768]{0,1:T(8,128)(4,1)}, u32[]{:S(2)}) copy-start(pred[768,768]{0,1:T(8,128)(4,1)} %iota_compare_fusion) | copy-start | bytes 1769476
  152.7 45.8 %copy-start.6 = (bf16[768,4,16]{0,2,1:T(8,128)(2,1)S(1)}, bf16[768,4,16]{0,2,1:T(8,128)(2,1)}, u32[]{:S(2)}) copy-start(bf16[768,4,16]{0,2,1:T(8,128)(2,1)} %fusion.62) | copy-start | bytes 294916
Sparse Core Ops, SparseCore 0:
  20.7 87.7 all-gather.5
  197.4 35.5 all-gather.3

commit v8 on v7

--- a/solution.py
+++ b/solution.py
@@ -111,11 +111,11 @@
     )
     running = attend(initial, queries, keys, values, offset[:, None] >= offset[None, :])
     my_group = group_ids[0]
-    prefix_pages = prefix_whole.reshape(-1, PAGE, 2, heads_here, HEAD_DIM)
     chosen = lax.dynamic_slice_in_dim(group_pages, my_group * PPAGES, PPAGES)
-    key_rows = jnp.take(prefix_pages, chosen, axis=0).reshape(
-        PPAGES * PAGE, 2, heads_here, HEAD_DIM
-    )
+    key_rows = jnp.concatenate(
+        [lax.dynamic_slice_in_dim(prefix_whole, chosen[k] * PAGE, PAGE, axis=0) for k in range(PPAGES)],
+        axis=0,
+    ).reshape(PPAGES * PAGE, 2, heads_here, HEAD_DIM)
     running = attend(
         running,
         queries,

time: 245 us -> 232 us (0.947)
  local copies, waits for them, and re-layouts: 44.5 us -> 35.6 us
    reshape x2 -> x0, local copies, waits for them, and re-layouts: 9.53 us -> none  [local(): prefix_pages = prefix_whole.reshape(-1, PAGE, 2, heads_here, HEAD_DIM)]
where the time goes in v8:
time: 232 us; the launch traced here: 231 us
  waiting for transfers between devices  90.9 us (39%)
  local copies, waits for them, and re-layouts  35.6 us (15%)
  matrix products  33.6 us (14%)
  other arithmetic  31.3 us (13%)
  between operations  17 us (7%)
  blocking collectives  11 us (5%)
  starting transfers between devices  10.7 us (5%)
    all_to_all x1, waiting for transfers between devices, gather_columns(): received = lax.all_to_all(copies, 'narrow', 0, 0, tiled=False)  31.7 us
    all_gather x1, waiting for transfers between devices, local(): by_xz = lax.all_gather(by_x, 'wz', axis=0, tiled=False)  29.6 us
    all_gather x1, waiting for transfers between devices, local(): all_heads = lax.all_gather(head_values, 'narrow', axis=1, tiled=True)  29.6 us
    reduce_sum x5, other arithmetic, attend(): weight_sum = weight_sum * factor + jnp.sum(expo, axis=2)  14.9 us
    dot_general x5, matrix products, attend(): jnp.einsum('hqk,khd->qhd', expo.astype(jnp.bfloat16), values, preferred_e...  13.7 us
    all_to_all x1, blocking collectives, local(): lax.all_to_all(jnp.broadcast_to(merged[None], (along_x,) + merged.shape),...  11 us
    all_to_all x1, starting transfers between devices, gather_columns(): received = lax.all_to_all(copies, 'narrow', 0, 0, tiled=False)  10.7 us
    dot_general x5, matrix products, attend(): jnp.einsum('qhd,khd->hqk', queries, keys, preferred_element_type=jnp.floa...  10.4 us
  transfers between devices with their start and end apart: 3, of which 3 were waited for; matrix products, arithmetic and copies ran while one was open for 8% of the time, Pallas kernels for 0%

profile of v8, /device:TPU:1, one launch (start us, length us, event | category | flops | bytes accessed | tf_op | source)
XLA Modules:
  0.0 230.6 jit_solution(7096636370363122591)
XLA Ops:
  9.6 11.0 %all_to_all.10 = bf16[4,32,1536]{2,1,0:T(8,128)(2,1)} all-to-all(bf16[4,32,1536]{2,1,0:T(8,128)(2,1)S(1)} %broadcast_in_dim.158), channel_id=1, replica_groups=mesh['wx'=4,'wz'=16,'narrow'=8] {'wx'}, dimensions={0} | all-to-all | bytes 786432 | tf_op jit(solution)/shard_map/all_to_all | solution.py:82
  20.6 2.8 %broadcast_in_dim.157 = bf16[8,768,256]{2,1,0:T(8,128)(2,1)} broadcast(bf16[768,256]{1,0:T(8,128)(2,1)} %param.12), dimensions={1,2} | broadcast | bytes 3538944 | tf_op jit(solution)/shard_map/broadcast_in_dim | solution.py:46
  23.4 10.7 %all-to-all-start = ((bf16[8,768,256]{2,1,0:T(8,128)(2,1)}), bf16[8,768,256]{2,1,0:T(8,128)(2,1)}, u32[]{:S(2)}, u32[]{:S(2)}) async-start(bf16[8,768,256]{2,1,0:T(8,128)(2,1)} %broadcast_in_dim.157), calls=%async_computation | async-start | bytes 6291456 | tf_op jit(solution)/shard_map/all_to_all | solution.py:47
  39.9 31.7 %all-to-all-done = bf16[8,768,256]{2,1,0:T(8,128)(2,1)} async-done(((bf16[8,768,256]{2,1,0:T(8,128)(2,1)}), bf16[8,768,256]{2,1,0:T(8,128)(2,1)}, u32[]{:S(2)}, u32[]{:S(2)}) %all-to-all-start) | async-done | bytes 3145760 | tf_op jit(solution)/shard_map/all_to_all | solution.py:47
  71.6 3.2 %copy.39 = bf16[8,768,256]{1,2,0:T(8,128)(2,1)S(1)} copy(bf16[8,768,256]{2,1,0:T(8,128)(2,1)} %all-to-all-done) | data formatting | bytes 6291456 | tf_op jit(solution)/shard_map/all_to_all | solution.py:47
  76.2 2.6 %fusion.35 = bf16[8,768,256]{1,2,0:T(8,128)(2,1)} fusion(bf16[8,768,256]{1,2,0:T(8,128)(2,1)S(1)} %copy.39, f32[8,256]{1,0:T(8,128)S(1)} %mul.207, f32[768]{0:T(1024)S(1)} %add_rsqrt_fusion, f32[768]{0:T(1024)S(1)} %broadcast_multiply_fusion), kind=kLoop, calls=%fused_computation.44 | loop fusion | flops 7864320 | bytes 6305792 | tf_op jit(solution)/shard_map/convert.3
  78.9 29.6 %all-gather.6.cloned.1.call-done = bf16[64,32,1536]{2,1,0:T(8,128)(2,1)} async-done(((bf16[4,32,1536]{2,1,0:T(8,128)(2,1)}), bf16[64,32,1536]{2,1,0:T(8,128)(2,1)}) %all-gather.6.cloned.1.call-update) | async-done | bytes 6291472 | tf_op jit(solution)/shard_map/all_gather | solution.py:85
  108.5 3.5 %copy.41 = bf16[4,16,32,1536]{3,2,1,0:T(8,128)(2,1)S(1)} copy(bf16[4,16,32,1536]{3,2,0,1:T(8,128)(2,1)} %bitcast.126) | data formatting | bytes 12582912 | tf_op jit(solution)/shard_map/transpose | solution.py:86
  115.5 3.0 %copy.42 = bf16[768,2048]{1,0:T(8,128)(2,1)} copy(bf16[768,2048]{0,1:T(8,128)(2,1)S(1)} %slice_bitcast_fusion.4) | data formatting | bytes 6291456 | tf_op jit(solution)/shard_map/dot_general | solution.py:92
  118.4 5.6 %fusion.80 = f32[768,3,4,64]{0,3,2,1:T(8,128)S(1)} fusion(bf16[768,2048,1,1]{0,1,3,2:T(8,128)(2,1)} %bitcast.127, bf16[3,4,64,2048]{3,2,1,0:T(8,128)(2,1)} %bitcast.128), kind=kOutput, calls=%fused_computation.115 | convolution fusion | flops 2415919104 | bytes 8650752 | tf_op jit(solution)/shard_map/dot_general | solution.py:92
  134.3 3.9 %fusion.57 = f32[768,4,64]{0,2,1:T(8,128)S(1)} fusion(f32[4,768,768]{1,2,0:T(8,128)S(1)} %get-tuple-element.355, f32[4,768]{1,0:T(4,128)S(1)} %get-tuple-element.348, pred[768,768]{0,1:T(8,128)(4,1)S(1)} %copy-done.1, f32[768,4]{0,1:T(4,128)S(1)} %get-tuple-element.347, f32[768,4]{0,1:T(4,128)S(1)} %get-tuple-element.346, f32[768,3,4,64]{0,3,2,1:T(8,128)} %copy-done.2), kind=kOutput, calls=%fused_computation.60 | convolution fusion | flops 314179584 | bytes 11243520 | tf_op jit(solution)/shard_map/hqk,khd->qhd/dot_general | solution.py:37
  139.5 43.8 %while.21 = (s32[]{:T(128)}, f32[4,768]{1,0:T(4,128)S(1)}, f32[4,768]{1,0:T(4,128)S(1)}, f32[768,4,64]{0,2,1:T(8,128)S(1)}, s32[24]{0:T(128)S(1)}, /*index=5*/s3...) while((s32[]{:T(128)}, f32[4,768]{1,0:T(4,128)S(1)}, ...), condition=%wide.region_10.11_spmd.clone, body=%wide.region_7.10_spmd.clone.sunk | while | flops 846611456 | bytes 47256848 | solution.py:145
  144.5 2.7 %bitcast_reduce_fusion.2 = (f32[4,768]{1,0:T(4,128)S(1)}, f32[4,1024,768]{2,1,0:T(8,128)S(1)}) fusion(pred[1024]{0:T(1024)(128)(4,1)S(1)} %fusion.93, bf16[768,4,64]{0,2,1:T(8,128)(2,1)S(1)} %get-tuple-element.450, bf16[1024,2,4,64]{0,3,2,1:T(8,128)(2,1)S(1)} %reshape.194), kind=kOutput, calls=%fused_computation.4.clone.1 | convolution fusion | flops 412087296 | bytes 13513728 | tf_op jit(solution)/shard_map/while/body/eval_jaxpr/qhd,khd->hqk/dot_general | solution.py:31
  147.2 3.0 %fusion.96 = f32[768,4,64]{0,2,1:T(8,128)S(1)} fusion(f32[4,1024,768]{2,1,0:T(8,128)S(1)} %get-tuple-element.417, f32[4,768]{1,0:T(4,128)S(1)} %get-tuple-element.444, pred[1024]{0:T(1024)(128)(4,1)S(1)} %fusion.93, f32[768,4,64]{0,2,1:T(8,128)S(1)} %get-tuple-element.434, bf16[1024,2,4,64]{0,3,2,1:T(8,128)(2,1)S(1)} %reshape.194, ...), kind=kOutput, calls=%fused_computation.14.clone.1 | convolution fusion | flops 418775040 | bytes 14706688 | tf_op jit(solution)/shard_map/while/body/eval_jaxpr/hqk,khd->qhd/dot_general | solution.py:37
  150.2 4.0 %fusion.95 = f32[4,768]{1,0:T(4,128)S(1)} fusion(f32[4,1024,768]{2,1,0:T(8,128)S(1)} %get-tuple-element.417, f32[4,768]{1,0:T(4,128)S(1)} %get-tuple-element.444, pred[1024]{0:T(1024)(128)(4,1)S(1)} %fusion.93), kind=kLoop, calls=%fused_computation.9.clone.1 | loop fusion | flops 15725568 | bytes 12608512 | tf_op jit(solution)/shard_map/while/body/eval_jaxpr/reduce_sum | solution.py:36
  159.0 2.7 %bitcast_reduce_fusion.2 = (f32[4,768]{1,0:T(4,128)S(1)}, f32[4,1024,768]{2,1,0:T(8,128)S(1)}) fusion(pred[1024]{0:T(1024)(128)(4,1)S(1)} %fusion.93, bf16[768,4,64]{0,2,1:T(8,128)(2,1)S(1)} %get-tuple-element.450, bf16[1024,2,4,64]{0,3,2,1:T(8,128)(2,1)S(1)} %reshape.194), kind=kOutput, calls=%fused_computation.4.clone.1 | convolution fusion | flops 412087296 | bytes 13513728 | tf_op jit(solution)/shard_map/while/body/eval_jaxpr/qhd,khd->hqk/dot_general | solution.py:31
  161.7 3.0 %fusion.96 = f32[768,4,64]{0,2,1:T(8,128)S(1)} fusion(f32[4,1024,768]{2,1,0:T(8,128)S(1)} %get-tuple-element.417, f32[4,768]{1,0:T(4,128)S(1)} %get-tuple-element.444, pred[1024]{0:T(1024)(128)(4,1)S(1)} %fusion.93, f32[768,4,64]{0,2,1:T(8,128)S(1)} %get-tuple-element.434, bf16[1024,2,4,64]{0,3,2,1:T(8,128)(2,1)S(1)} %reshape.194, ...), kind=kOutput, calls=%fused_computation.14.clone.1 | convolution fusion | flops 418775040 | bytes 14706688 | tf_op jit(solution)/shard_map/while/body/eval_jaxpr/hqk,khd->qhd/dot_general | solution.py:37
  164.7 4.0 %fusion.95 = f32[4,768]{1,0:T(4,128)S(1)} fusion(f32[4,1024,768]{2,1,0:T(8,128)S(1)} %get-tuple-element.417, f32[4,768]{1,0:T(4,128)S(1)} %get-tuple-element.444, pred[1024]{0:T(1024)(128)(4,1)S(1)} %fusion.93), kind=kLoop, calls=%fused_computation.9.clone.1 | loop fusion | flops 15725568 | bytes 12608512 | tf_op jit(solution)/shard_map/while/body/eval_jaxpr/reduce_sum | solution.py:36
  173.5 2.7 %bitcast_reduce_fusion.2 = (f32[4,768]{1,0:T(4,128)S(1)}, f32[4,1024,768]{2,1,0:T(8,128)S(1)}) fusion(pred[1024]{0:T(1024)(128)(4,1)S(1)} %fusion.93, bf16[768,4,64]{0,2,1:T(8,128)(2,1)S(1)} %get-tuple-element.450, bf16[1024,2,4,64]{0,3,2,1:T(8,128)(2,1)S(1)} %reshape.194), kind=kOutput, calls=%fused_computation.4.clone.1 | convolution fusion | flops 412087296 | bytes 13513728 | tf_op jit(solution)/shard_map/while/body/eval_jaxpr/qhd,khd->hqk/dot_general | solution.py:31
  176.2 3.0 %fusion.96 = f32[768,4,64]{0,2,1:T(8,128)S(1)} fusion(f32[4,1024,768]{2,1,0:T(8,128)S(1)} %get-tuple-element.417, f32[4,768]{1,0:T(4,128)S(1)} %get-tuple-element.444, pred[1024]{0:T(1024)(128)(4,1)S(1)} %fusion.93, f32[768,4,64]{0,2,1:T(8,128)S(1)} %get-tuple-element.434, bf16[1024,2,4,64]{0,3,2,1:T(8,128)(2,1)S(1)} %reshape.194, ...), kind=kOutput, calls=%fused_computation.14.clone.1 | convolution fusion | flops 418775040 | bytes 14706688 | tf_op jit(solution)/shard_map/while/body/eval_jaxpr/hqk,khd->qhd/dot_general | solution.py:37
  179.3 4.0 %fusion.95 = f32[4,768]{1,0:T(4,128)S(1)} fusion(f32[4,1024,768]{2,1,0:T(8,128)S(1)} %get-tuple-element.417, f32[4,768]{1,0:T(4,128)S(1)} %get-tuple-element.444, pred[1024]{0:T(1024)(128)(4,1)S(1)} %fusion.93), kind=kLoop, calls=%fused_computation.9.clone.1 | loop fusion | flops 15725568 | bytes 12608512 | tf_op jit(solution)/shard_map/while/body/eval_jaxpr/reduce_sum | solution.py:36
  187.6 2.7 %pad_maximum_fusion = bf16[768,2,256]{2,1,0:T(2,128)(2,1)} fusion(bf16[768,1,256]{2,1,0:T(2,128)(2,1)S(1)} %copy.49, bf16[768,1,256]{2,1,0:T(2,128)(2,1)S(1)} %copy.48), kind=kLoop, calls=%fused_computation.67 | loop fusion | flops 1572864 | bytes 1572864 | tf_op jit(solution)/shard_map/stack | solution.py:104
  190.3 29.6 %all-gather.4.cloned.1.call-done = bf16[768,2048]{0,1:T(8,128)(2,1)} async-done(((bf16[768,256]{0,1:T(8,128)(2,1)}), bf16[768,2048]{0,1:T(8,128)(2,1)}) %all-gather.4.cloned.1.call-update) | async-done | bytes 3145744 | tf_op jit(solution)/shard_map/all_gather | solution.py:151
  219.8 3.9 %convolution_convert_fusion = bf16[768,256]{1,0:T(8,128)(2,1)} fusion(bf16[768,2048]{0,1:T(8,128)(2,1)} %all-gather.4.cloned.1.call-done, bf16[2048,1536]{1,0:T(8,128)(2,1)} %bitcast.125), kind=kOutput, calls=%fused_computation.61 | convolution fusion | flops 805502976 | bytes 4587520 | tf_op jit(solution)/shard_map/dot_general | solution.py:153
  (90 shorter events, 40.3 us)
Async XLA Ops:
  7.2 27.6 %copy-start.7 = (s32[16]{0:T(128)S(1)}, s32[16]{0:T(128)}, u32[]{:S(2)}) copy-start(s32[16]{0:T(128)} %param.21) | copy-start | bytes 196
  7.2 30.2 %copy-start.6 = (f32[2048]{0:T(1024)S(1)}, f32[2048]{0:T(1024)}, u32[]{:S(2)}) copy-start(f32[2048]{0:T(1024)} %param.13) | copy-start | bytes 24580
  7.2 30.2 %copy-start.8 = (s32[1,24]{1,0:T(1,128)S(1)}, s32[1,24]{1,0:T(1,128)}, u32[]{:S(2)}) copy-start(s32[1,24]{1,0:T(1,128)} %param.18) | copy-start | bytes 292
  7.2 101.3 %all-gather.6.cloned.1.call-start = ((), (), s32[]{:S(2)}) async-start(), calls=%async_computation.3 | async-start | bytes 6684672 | tf_op jit(solution)/shard_map/all_gather | solution.py:85
  23.4 48.2 %all-to-all-start = ((bf16[8,768,256]{2,1,0:T(8,128)(2,1)}), bf16[8,768,256]{2,1,0:T(8,128)(2,1)}, u32[]{:S(2)}, u32[]{:S(2)}) async-start(bf16[8,768,256]{2,1,0:T(8,128)(2,1)} %broadcast_in_dim.157), calls=%async_computation | async-start | bytes 6291456 | tf_op jit(solution)/shard_map/all_to_all | solution.py:47
  34.1 185.8 %all-gather.4.cloned.1.call-start = ((), (), s32[]{:S(2)}) async-start(), calls=%async_computation.2 | async-start | bytes 3538944 | tf_op jit(solution)/shard_map/all_gather | solution.py:151
  112.0 3.3 %copy-start = (bf16[4,16,32,1536]{3,2,1,0:T(8,128)(2,1)}, bf16[4,16,32,1536]{3,2,1,0:T(8,128)(2,1)S(1)}, u32[]{:S(2)}) copy-start(bf16[4,16,32,1536]{3,2,1,0:T(8,128)(2,1)S(1)} %copy.41) | copy-start | bytes 18874372
  124.0 1.4 copy-start.2
  124.0 6.0 %copy-start.1 = (pred[768,768]{0,1:T(8,128)(4,1)S(1)}, pred[768,768]{0,1:T(8,128)(4,1)}, u32[]{:S(2)}) copy-start(pred[768,768]{0,1:T(8,128)(4,1)} %iota_compare_fusion) | copy-start | bytes 1769476
  125.5 6.4 %copy-start.3 = (bf16[768,4,48]{0,2,1:T(8,128)(2,1)}, bf16[768,4,48]{0,2,1:T(8,128)(2,1)S(1)}, u32[]{:S(2)}) copy-start(bf16[768,4,48]{0,2,1:T(8,128)(2,1)S(1)} %slice.113) | copy-start | bytes 884740
  130.1 4.2 %copy-start.4 = (bf16[768,4,16]{0,2,1:T(8,128)(2,1)}, bf16[768,4,16]{0,2,1:T(8,128)(2,1)S(1)}, u32[]{:S(2)}) copy-start(bf16[768,4,16]{0,2,1:T(8,128)(2,1)S(1)} %fusion.62) | copy-start | bytes 294916
  139.5 46.4 %copy-start.5 = (bf16[768,4,16]{0,2,1:T(8,128)(2,1)S(1)}, bf16[768,4,16]{0,2,1:T(8,128)(2,1)}, u32[]{:S(2)}) copy-start(bf16[768,4,16]{0,2,1:T(8,128)(2,1)} %copy-done.4) | copy-start | bytes 294916
Sparse Core Ops, SparseCore 0:
  20.7 87.7 all-gather.5
  184.3 35.5 all-gather.3

commit v9 on v8

--- a/solution.py
+++ b/solution.py
@@ -6,7 +6,7 @@
 HEAD_DIM = 64
 ROT = 16
 PAGE = 128
-KB = 8
+KB = 12
 PPAGES = 2
 
 

time: 232 us -> 240 us (1.034)
  local copies, waits for them, and re-layouts: 35.6 us -> 42.8 us
  matrix products: 33.6 us -> 36.1 us
    dynamic_slice x6 -> x4, local copies, waits for them, and re-layouts: 10.3 us -> 14.8 us  [cache_block(): lax.dynamic_slice_in_dim(cache_pool, block_index * KB, KB, axis=0)]
    dot_general x5 -> x4, matrix products: 10.4 us -> 13.1 us  [attend(): jnp.einsum('qhd,khd->hqk', queries, keys, preferred_element_type=jnp.floa...]
    reshape x3 -> x2, local copies, waits for them, and re-layouts: 1.48 us -> 3.89 us  [cache_block(): lax.dynamic_slice_in_dim(cache_pool, block_index * KB, KB, axis=0)]
    reduce_sum x5 -> x4, other arithmetic: 14.9 us -> 15.1 us  [attend(): weight_sum = weight_sum * factor + jnp.sum(expo, axis=2)]
    dot_general x5 -> x4, matrix products: 13.7 us -> 13.5 us  [attend(): jnp.einsum('hqk,khd->qhd', expo.astype(jnp.bfloat16), values, preferred_e...]
where the time goes in v9:
time: 240 us; the launch traced here: 239 us
  waiting for transfers between devices  90.7 us (38%)
  local copies, waits for them, and re-layouts  42.8 us (18%)
  matrix products  36.1 us (15%)
  other arithmetic  30.7 us (13%)
  between operations  17 us (7%)
  blocking collectives  11 us (5%)
  starting transfers between devices  10.7 us (4%)
    all_to_all x1, waiting for transfers between devices, gather_columns(): received = lax.all_to_all(copies, 'narrow', 0, 0, tiled=False)  31.7 us
    all_gather x1, waiting for transfers between devices, local(): by_xz = lax.all_gather(by_x, 'wz', axis=0, tiled=False)  29.6 us
    all_gather x1, waiting for transfers between devices, local(): all_heads = lax.all_gather(head_values, 'narrow', axis=1, tiled=True)  29.3 us
    reduce_sum x4, other arithmetic, attend(): weight_sum = weight_sum * factor + jnp.sum(expo, axis=2)  15.1 us
    dynamic_slice x4, local copies, waits for them, and re-layouts, cache_block(): lax.dynamic_slice_in_dim(cache_pool, block_index * KB, KB, axis=0)  14.8 us
    dot_general x4, matrix products, attend(): jnp.einsum('hqk,khd->qhd', expo.astype(jnp.bfloat16), values, preferred_e...  13.5 us
    dot_general x4, matrix products, attend(): jnp.einsum('qhd,khd->hqk', queries, keys, preferred_element_type=jnp.floa...  13.1 us
    all_to_all x1, blocking collectives, local(): lax.all_to_all(jnp.broadcast_to(merged[None], (along_x,) + merged.shape),...  11 us
  transfers between devices with their start and end apart: 3, of which 3 were waited for; matrix products, arithmetic and copies ran while one was open for 8% of the time, Pallas kernels for 0%

profile of v9, /device:TPU:1, one launch (start us, length us, event | category | flops | bytes accessed | tf_op | source)
XLA Modules:
  0.0 239.3 jit_solution(18271034731433525721)
XLA Ops:
  9.6 11.0 %all_to_all.10 = bf16[4,32,1536]{2,1,0:T(8,128)(2,1)} all-to-all(bf16[4,32,1536]{2,1,0:T(8,128)(2,1)S(1)} %broadcast_in_dim.158), channel_id=1, replica_groups=mesh['wx'=4,'wz'=16,'narrow'=8] {'wx'}, dimensions={0} | all-to-all | bytes 786432 | tf_op jit(solution)/shard_map/all_to_all | solution.py:82
  20.6 2.8 %broadcast_in_dim.157 = bf16[8,768,256]{2,1,0:T(8,128)(2,1)} broadcast(bf16[768,256]{1,0:T(8,128)(2,1)} %param.12), dimensions={1,2} | broadcast | bytes 3538944 | tf_op jit(solution)/shard_map/broadcast_in_dim | solution.py:46
  23.4 10.6 %all-to-all-start = ((bf16[8,768,256]{2,1,0:T(8,128)(2,1)}), bf16[8,768,256]{2,1,0:T(8,128)(2,1)}, u32[]{:S(2)}, u32[]{:S(2)}) async-start(bf16[8,768,256]{2,1,0:T(8,128)(2,1)} %broadcast_in_dim.157), calls=%async_computation | async-start | bytes 6291456 | tf_op jit(solution)/shard_map/all_to_all | solution.py:47
  39.9 31.7 %all-to-all-done = bf16[8,768,256]{2,1,0:T(8,128)(2,1)} async-done(((bf16[8,768,256]{2,1,0:T(8,128)(2,1)}), bf16[8,768,256]{2,1,0:T(8,128)(2,1)}, u32[]{:S(2)}, u32[]{:S(2)}) %all-to-all-start) | async-done | bytes 3145760 | tf_op jit(solution)/shard_map/all_to_all | solution.py:47
  71.6 3.2 %copy.39 = bf16[8,768,256]{1,2,0:T(8,128)(2,1)S(1)} copy(bf16[8,768,256]{2,1,0:T(8,128)(2,1)} %all-to-all-done) | data formatting | bytes 6291456 | tf_op jit(solution)/shard_map/all_to_all | solution.py:47
  78.9 29.6 %all-gather.6.cloned.1.call-done = bf16[64,32,1536]{2,1,0:T(8,128)(2,1)} async-done(((bf16[4,32,1536]{2,1,0:T(8,128)(2,1)}), bf16[64,32,1536]{2,1,0:T(8,128)(2,1)}) %all-gather.6.cloned.1.call-update) | async-done | bytes 6291472 | tf_op jit(solution)/shard_map/all_gather | solution.py:85
  108.5 3.5 %copy.41 = bf16[4,16,32,1536]{3,2,1,0:T(8,128)(2,1)S(1)} copy(bf16[4,16,32,1536]{3,2,0,1:T(8,128)(2,1)} %bitcast.124) | data formatting | bytes 12582912 | tf_op jit(solution)/shard_map/transpose | solution.py:86
  115.5 2.9 %copy.42 = bf16[768,2048]{1,0:T(8,128)(2,1)} copy(bf16[768,2048]{0,1:T(8,128)(2,1)S(1)} %slice_bitcast_fusion.4) | data formatting | bytes 6291456 | tf_op jit(solution)/shard_map/dot_general | solution.py:92
  118.4 5.6 %fusion.80 = f32[768,3,4,64]{0,3,2,1:T(8,128)S(1)} fusion(bf16[768,2048,1,1]{0,1,3,2:T(8,128)(2,1)} %bitcast.125, bf16[3,4,64,2048]{3,2,1,0:T(8,128)(2,1)} %bitcast.126), kind=kOutput, calls=%fused_computation.115 | convolution fusion | flops 2415919104 | bytes 8650752 | tf_op jit(solution)/shard_map/dot_general | solution.py:92
  134.3 3.9 %fusion.57 = f32[768,4,64]{0,2,1:T(8,128)S(1)} fusion(f32[4,768,768]{1,2,0:T(8,128)S(1)} %get-tuple-element.355, f32[4,768]{1,0:T(4,128)S(1)} %get-tuple-element.348, pred[768,768]{0,1:T(8,128)(4,1)S(1)} %copy-done.2, f32[768,4]{0,1:T(4,128)S(1)} %get-tuple-element.347, f32[768,4]{0,1:T(4,128)S(1)} %get-tuple-element.346, f32[768,3,4,64]{0,3,2,1:T(8,128)} %copy-done.3), kind=kOutput, calls=%fused_computation.60 | convolution fusion | flops 314179584 | bytes 11243520 | tf_op jit(solution)/shard_map/hqk,khd->qhd/dot_general | solution.py:37
  139.5 52.5 %while.21 = (s32[]{:T(128)}, f32[4,768]{1,0:T(4,128)S(1)}, f32[4,768]{1,0:T(4,128)S(1)}, f32[768,4,64]{0,2,1:T(8,128)S(1)}, s32[24]{0:T(128)S(1)}, /*index=5*/s3...) while((s32[]{:T(128)}, f32[4,768]{1,0:T(4,128)S(1)}, ...), condition=%wide.region_10.11_spmd.clone, body=%wide.region_7.10_spmd.clone.sunk | while | flops 1269715968 | bytes 76096344 | solution.py:145
  140.5 3.9 %constant_dynamic-slice_fusion.4 = bf16[12,128,2,256]{3,2,1,0:T(2,128)(2,1)} fusion(bf16[24,128,2,256]{3,2,1,0:T(2,128)(2,1)} %get-tuple-element.449, s32[]{:T(128)S(6)} %select_n.172), kind=kLoop, calls=%fused_computation.29.clone.1 | loop fusion | bytes 3145732 | tf_op jit(solution)/shard_map/while/body/eval_jaxpr/dynamic_slice | solution.py:137
  144.4 3.5 %copy.59 = bf16[12,128,2,256]{1,0,3,2:T(8,128)(2,1)S(1)} copy(bf16[12,128,2,256]{3,2,1,0:T(2,128)(2,1)} %constant_dynamic-slice_fusion.4) | data formatting | bytes 3145728 | tf_op jit(solution)/shard_map/while/body/eval_jaxpr/dynamic_slice | solution.py:137
  149.9 5.3 %bitcast_reduce_fusion.2 = (f32[4,768]{1,0:T(4,128)S(1)}, f32[4,1536,768]{2,1,0:T(8,128)S(1)}) fusion(pred[1536]{0:T(1024)(128)(4,1)S(1)} %fusion.93, bf16[768,4,64]{0,2,1:T(8,128)(2,1)S(1)} %get-tuple-element.450, bf16[1536,2,4,64]{0,3,2,1:T(8,128)(2,1)} %reshape.194), kind=kOutput, calls=%fused_computation.4.clone.1 | convolution fusion | flops 618132480 | bytes 20067840 | tf_op jit(solution)/shard_map/while/body/eval_jaxpr/qhd,khd->hqk/dot_general | solution.py:31
  155.2 4.4 %fusion.96 = f32[768,4,64]{0,2,1:T(8,128)S(1)} fusion(f32[4,1536,768]{2,1,0:T(8,128)S(1)} %get-tuple-element.417, f32[4,768]{1,0:T(4,128)S(1)} %get-tuple-element.444, pred[1536]{0:T(1024)(128)(4,1)S(1)} %fusion.93, bf16[1536,2,4,64]{0,3,2,1:T(8,128)(2,1)S(1)} %copy-done, f32[768,4,64]{0,2,1:T(8,128)S(1)} %get-tuple-element.434, ...), kind=kOutput, calls=%fused_computation.14.clone.1 | convolution fusion | flops 627965952 | bytes 21262336 | tf_op jit(solution)/shard_map/while/body/eval_jaxpr/hqk,khd->qhd/dot_general | solution.py:37
  159.7 6.1 %fusion.95 = f32[4,768]{1,0:T(4,128)S(1)} fusion(f32[4,1536,768]{2,1,0:T(8,128)S(1)} %get-tuple-element.417, f32[4,768]{1,0:T(4,128)S(1)} %get-tuple-element.444, pred[1536]{0:T(1024)(128)(4,1)S(1)} %fusion.93), kind=kLoop, calls=%fused_computation.9.clone.1 | loop fusion | flops 23589888 | bytes 18900480 | tf_op jit(solution)/shard_map/while/body/eval_jaxpr/reduce_sum | solution.py:36
  166.6 3.9 %constant_dynamic-slice_fusion.4 = bf16[12,128,2,256]{3,2,1,0:T(2,128)(2,1)} fusion(bf16[24,128,2,256]{3,2,1,0:T(2,128)(2,1)} %get-tuple-element.449, s32[]{:T(128)S(6)} %select_n.172), kind=kLoop, calls=%fused_computation.29.clone.1 | loop fusion | bytes 3145732 | tf_op jit(solution)/shard_map/while/body/eval_jaxpr/dynamic_slice | solution.py:137
  170.5 3.5 %copy.59 = bf16[12,128,2,256]{1,0,3,2:T(8,128)(2,1)S(1)} copy(bf16[12,128,2,256]{3,2,1,0:T(2,128)(2,1)} %constant_dynamic-slice_fusion.4) | data formatting | bytes 3145728 | tf_op jit(solution)/shard_map/while/body/eval_jaxpr/dynamic_slice | solution.py:137
  176.0 5.3 %bitcast_reduce_fusion.2 = (f32[4,768]{1,0:T(4,128)S(1)}, f32[4,1536,768]{2,1,0:T(8,128)S(1)}) fusion(pred[1536]{0:T(1024)(128)(4,1)S(1)} %fusion.93, bf16[768,4,64]{0,2,1:T(8,128)(2,1)S(1)} %get-tuple-element.450, bf16[1536,2,4,64]{0,3,2,1:T(8,128)(2,1)} %reshape.194), kind=kOutput, calls=%fused_computation.4.clone.1 | convolution fusion | flops 618132480 | bytes 20067840 | tf_op jit(solution)/shard_map/while/body/eval_jaxpr/qhd,khd->hqk/dot_general | solution.py:31
  181.3 4.4 %fusion.96 = f32[768,4,64]{0,2,1:T(8,128)S(1)} fusion(f32[4,1536,768]{2,1,0:T(8,128)S(1)} %get-tuple-element.417, f32[4,768]{1,0:T(4,128)S(1)} %get-tuple-element.444, pred[1536]{0:T(1024)(128)(4,1)S(1)} %fusion.93, bf16[1536,2,4,64]{0,3,2,1:T(8,128)(2,1)S(1)} %copy-done, f32[768,4,64]{0,2,1:T(8,128)S(1)} %get-tuple-element.434, ...), kind=kOutput, calls=%fused_computation.14.clone.1 | convolution fusion | flops 627965952 | bytes 21262336 | tf_op jit(solution)/shard_map/while/body/eval_jaxpr/hqk,khd->qhd/dot_general | solution.py:37
  185.8 6.1 %fusion.95 = f32[4,768]{1,0:T(4,128)S(1)} fusion(f32[4,1536,768]{2,1,0:T(8,128)S(1)} %get-tuple-element.417, f32[4,768]{1,0:T(4,128)S(1)} %get-tuple-element.444, pred[1536]{0:T(1024)(128)(4,1)S(1)} %fusion.93), kind=kLoop, calls=%fused_computation.9.clone.1 | loop fusion | flops 23589888 | bytes 18900480 | tf_op jit(solution)/shard_map/while/body/eval_jaxpr/reduce_sum | solution.py:36
  196.5 2.7 %pad_maximum_fusion = bf16[768,2,256]{2,1,0:T(2,128)(2,1)} fusion(bf16[768,1,256]{2,1,0:T(2,128)(2,1)S(1)} %copy.49, bf16[768,1,256]{2,1,0:T(2,128)(2,1)S(1)} %copy.48), kind=kLoop, calls=%fused_computation.67 | loop fusion | flops 1572864 | bytes 1572864 | tf_op jit(solution)/shard_map/stack | solution.py:104
  199.2 29.3 %all-gather.4.cloned.1.call-done = bf16[768,2048]{0,1:T(8,128)(2,1)} async-done(((bf16[768,256]{0,1:T(8,128)(2,1)}), bf16[768,2048]{0,1:T(8,128)(2,1)}) %all-gather.4.cloned.1.call-update) | async-done | bytes 3145744 | tf_op jit(solution)/shard_map/all_gather | solution.py:151
  228.5 3.9 %convolution_convert_fusion = bf16[768,256]{1,0:T(8,128)(2,1)} fusion(bf16[768,2048]{0,1:T(8,128)(2,1)} %all-gather.4.cloned.1.call-done, bf16[2048,1536]{1,0:T(8,128)(2,1)} %bitcast.123), kind=kOutput, calls=%fused_computation.61 | convolution fusion | flops 805502976 | bytes 4587520 | tf_op jit(solution)/shard_map/dot_general | solution.py:153
  (83 shorter events, 34.5 us)
Async XLA Ops:
  7.2 27.5 %copy-start.8 = (s32[16]{0:T(128)S(1)}, s32[16]{0:T(128)}, u32[]{:S(2)}) copy-start(s32[16]{0:T(128)} %param.21) | copy-start | bytes 196
  7.2 30.1 %copy-start.7 = (f32[2048]{0:T(1024)S(1)}, f32[2048]{0:T(1024)}, u32[]{:S(2)}) copy-start(f32[2048]{0:T(1024)} %param.13) | copy-start | bytes 24580
  7.2 30.2 %copy-start.9 = (s32[1,24]{1,0:T(1,128)S(1)}, s32[1,24]{1,0:T(1,128)}, u32[]{:S(2)}) copy-start(s32[1,24]{1,0:T(1,128)} %param.18) | copy-start | bytes 292
  7.2 101.3 %all-gather.6.cloned.1.call-start = ((), (), s32[]{:S(2)}) async-start(), calls=%async_computation.3 | async-start | bytes 6684672 | tf_op jit(solution)/shard_map/all_gather | solution.py:85
  23.4 48.2 %all-to-all-start = ((bf16[8,768,256]{2,1,0:T(8,128)(2,1)}), bf16[8,768,256]{2,1,0:T(8,128)(2,1)}, u32[]{:S(2)}, u32[]{:S(2)}) async-start(bf16[8,768,256]{2,1,0:T(8,128)(2,1)} %broadcast_in_dim.157), calls=%async_computation | async-start | bytes 6291456 | tf_op jit(solution)/shard_map/all_to_all | solution.py:47
  34.0 194.4 %all-gather.4.cloned.1.call-start = ((), (), s32[]{:S(2)}) async-start(), calls=%async_computation.2 | async-start | bytes 3538944 | tf_op jit(solution)/shard_map/all_gather | solution.py:151
  112.0 3.3 %copy-start.1 = (bf16[4,16,32,1536]{3,2,1,0:T(8,128)(2,1)}, bf16[4,16,32,1536]{3,2,1,0:T(8,128)(2,1)S(1)}, u32[]{:S(2)}) copy-start(bf16[4,16,32,1536]{3,2,1,0:T(8,128)(2,1)S(1)} %copy.41) | copy-start | bytes 18874372
  124.0 1.4 copy-start.3
  124.0 6.0 %copy-start.2 = (pred[768,768]{0,1:T(8,128)(4,1)S(1)}, pred[768,768]{0,1:T(8,128)(4,1)}, u32[]{:S(2)}) copy-start(pred[768,768]{0,1:T(8,128)(4,1)} %iota_compare_fusion) | copy-start | bytes 1769476
  125.5 6.4 %copy-start.4 = (bf16[768,4,48]{0,2,1:T(8,128)(2,1)}, bf16[768,4,48]{0,2,1:T(8,128)(2,1)S(1)}, u32[]{:S(2)}) copy-start(bf16[768,4,48]{0,2,1:T(8,128)(2,1)S(1)} %slice.113) | copy-start | bytes 884740
  130.1 4.2 %copy-start.5 = (bf16[768,4,16]{0,2,1:T(8,128)(2,1)}, bf16[768,4,16]{0,2,1:T(8,128)(2,1)S(1)}, u32[]{:S(2)}) copy-start(bf16[768,4,16]{0,2,1:T(8,128)(2,1)S(1)} %fusion.62) | copy-start | bytes 294916
  139.5 55.1 %copy-start.6 = (bf16[768,4,16]{0,2,1:T(8,128)(2,1)S(1)}, bf16[768,4,16]{0,2,1:T(8,128)(2,1)}, u32[]{:S(2)}) copy-start(bf16[768,4,16]{0,2,1:T(8,128)(2,1)} %copy-done.5) | copy-start | bytes 294916
  149.9 5.4 %copy-start = (bf16[1536,2,4,64]{0,3,2,1:T(8,128)(2,1)S(1)}, bf16[1536,2,4,64]{0,3,2,1:T(8,128)(2,1)}, u32[]{:S(2)}) copy-start(bf16[1536,2,4,64]{0,3,2,1:T(8,128)(2,1)} %reshape.194) | copy-start | bytes 4718596 | tf_op jit(solution)/shard_map/while
  176.0 5.4 %copy-start = (bf16[1536,2,4,64]{0,3,2,1:T(8,128)(2,1)S(1)}, bf16[1536,2,4,64]{0,3,2,1:T(8,128)(2,1)}, u32[]{:S(2)}) copy-start(bf16[1536,2,4,64]{0,3,2,1:T(8,128)(2,1)} %reshape.194) | copy-start | bytes 4718596 | tf_op jit(solution)/shard_map/while
Sparse Core Ops, SparseCore 0:
  20.7 87.7 all-gather.5
  192.9 35.5 all-gather.3

commit v10 on v9

--- a/solution.py
+++ b/solution.py
@@ -6,7 +6,7 @@
 HEAD_DIM = 64
 ROT = 16
 PAGE = 128
-KB = 12
+KB = 6
 PPAGES = 2
 
 

time: 240 us -> 235 us (0.979)
  local copies, waits for them, and re-layouts: 42.8 us -> 38.3 us
    dynamic_slice x4 -> x8, local copies, waits for them, and re-layouts: 14.8 us -> 11.7 us  [cache_block(): lax.dynamic_slice_in_dim(cache_pool, block_index * KB, KB, axis=0)]
    dot_general x4 -> x6, matrix products: 13.1 us -> 10.3 us  [attend(): jnp.einsum('qhd,khd->hqk', queries, keys, preferred_element_type=jnp.floa...]
    dot_general x4 -> x6, matrix products: 13.5 us -> 13.9 us  [attend(): jnp.einsum('hqk,khd->qhd', expo.astype(jnp.bfloat16), values, preferred_e...]
    reduce_sum x4 -> x6, other arithmetic: 15.1 us -> 14.7 us  [attend(): weight_sum = weight_sum * factor + jnp.sum(expo, axis=2)]
where the time goes in v10:
time: 235 us; the launch traced here: 234 us
  waiting for transfers between devices  92.6 us (39%)
  local copies, waits for them, and re-layouts  38.3 us (16%)
  matrix products  33.7 us (14%)
  other arithmetic  30.3 us (13%)
  between operations  17 us (7%)
  blocking collectives  11 us (5%)
  starting transfers between devices  10.7 us (5%)
    all_to_all x1, waiting for transfers between devices, gather_columns(): received = lax.all_to_all(copies, 'narrow', 0, 0, tiled=False)  32.4 us
    all_gather x1, waiting for transfers between devices, local(): all_heads = lax.all_gather(head_values, 'narrow', axis=1, tiled=True)  30.6 us
    all_gather x1, waiting for transfers between devices, local(): by_xz = lax.all_gather(by_x, 'wz', axis=0, tiled=False)  29.6 us
    reduce_sum x6, other arithmetic, attend(): weight_sum = weight_sum * factor + jnp.sum(expo, axis=2)  14.7 us
    dot_general x6, matrix products, attend(): jnp.einsum('hqk,khd->qhd', expo.astype(jnp.bfloat16), values, preferred_e...  13.9 us
    dynamic_slice x8, local copies, waits for them, and re-layouts, cache_block(): lax.dynamic_slice_in_dim(cache_pool, block_index * KB, KB, axis=0)  11.7 us
    all_to_all x1, blocking collectives, local(): lax.all_to_all(jnp.broadcast_to(merged[None], (along_x,) + merged.shape),...  11 us
    all_to_all x1, starting transfers between devices, gather_columns(): received = lax.all_to_all(copies, 'narrow', 0, 0, tiled=False)  10.6 us
  transfers between devices with their start and end apart: 3, of which 3 were waited for; matrix products, arithmetic and copies ran while one was open for 8% of the time, Pallas kernels for 0%

profile of v10, /device:TPU:1, one launch (start us, length us, event | category | flops | bytes accessed | tf_op | source)
XLA Modules:
  0.0 234.1 jit_solution(7094145370746919015)
XLA Ops:
  9.6 11.0 %all_to_all.10 = bf16[4,32,1536]{2,1,0:T(8,128)(2,1)} all-to-all(bf16[4,32,1536]{2,1,0:T(8,128)(2,1)S(1)} %broadcast_in_dim.154), channel_id=1, replica_groups=mesh['wx'=4,'wz'=16,'narrow'=8] {'wx'}, dimensions={0} | all-to-all | bytes 786432 | tf_op jit(solution)/shard_map/all_to_all | solution.py:82
  20.6 2.8 %broadcast_in_dim.153 = bf16[8,768,256]{2,1,0:T(8,128)(2,1)} broadcast(bf16[768,256]{1,0:T(8,128)(2,1)} %param.12), dimensions={1,2} | broadcast | bytes 3538944 | tf_op jit(solution)/shard_map/broadcast_in_dim | solution.py:46
  23.4 10.6 %all-to-all-start = ((bf16[8,768,256]{2,1,0:T(8,128)(2,1)}), bf16[8,768,256]{2,1,0:T(8,128)(2,1)}, u32[]{:S(2)}, u32[]{:S(2)}) async-start(bf16[8,768,256]{2,1,0:T(8,128)(2,1)} %broadcast_in_dim.153), calls=%async_computation | async-start | bytes 6291456 | tf_op jit(solution)/shard_map/all_to_all | solution.py:47
  39.2 32.4 %all-to-all-done = bf16[8,768,256]{2,1,0:T(8,128)(2,1)} async-done(((bf16[8,768,256]{2,1,0:T(8,128)(2,1)}), bf16[8,768,256]{2,1,0:T(8,128)(2,1)}, u32[]{:S(2)}, u32[]{:S(2)}) %all-to-all-start) | async-done | bytes 3145760 | tf_op jit(solution)/shard_map/all_to_all | solution.py:47
  71.6 3.2 %copy.39 = bf16[8,768,256]{1,2,0:T(8,128)(2,1)S(1)} copy(bf16[8,768,256]{2,1,0:T(8,128)(2,1)} %all-to-all-done) | data formatting | bytes 6291456 | tf_op jit(solution)/shard_map/all_to_all | solution.py:47
  76.2 2.7 %fusion.35 = bf16[8,768,256]{1,2,0:T(8,128)(2,1)} fusion(bf16[8,768,256]{1,2,0:T(8,128)(2,1)S(1)} %copy.39, f32[8,256]{1,0:T(8,128)S(1)} %mul.204, f32[768]{0:T(1024)S(1)} %add_rsqrt_fusion, f32[768]{0:T(1024)S(1)} %broadcast_multiply_fusion), kind=kLoop, calls=%fused_computation.44 | loop fusion | flops 7864320 | bytes 6305792 | tf_op jit(solution)/shard_map/convert.3
  78.9 29.6 %all-gather.6.cloned.1.call-done = bf16[64,32,1536]{2,1,0:T(8,128)(2,1)} async-done(((bf16[4,32,1536]{2,1,0:T(8,128)(2,1)}), bf16[64,32,1536]{2,1,0:T(8,128)(2,1)}) %all-gather.6.cloned.1.call-update) | async-done | bytes 6291472 | tf_op jit(solution)/shard_map/all_gather | solution.py:85
  108.5 3.5 %copy.41 = bf16[4,16,32,1536]{3,2,1,0:T(8,128)(2,1)S(1)} copy(bf16[4,16,32,1536]{3,2,0,1:T(8,128)(2,1)} %bitcast.123) | data formatting | bytes 12582912 | tf_op jit(solution)/shard_map/transpose | solution.py:86
  112.0 2.6 %copy-done = bf16[4,16,32,1536]{3,2,1,0:T(8,128)(2,1)} copy-done((bf16[4,16,32,1536]{3,2,1,0:T(8,128)(2,1)}, bf16[4,16,32,1536]{3,2,1,0:T(8,128)(2,1)S(1)}, u32[]{:S(2)}) %copy-start) | copy-done | bytes 6291480
  114.9 2.9 %copy.42 = bf16[768,2048]{1,0:T(8,128)(2,1)} copy(bf16[768,2048]{0,1:T(8,128)(2,1)S(1)} %slice_bitcast_fusion.4) | data formatting | bytes 6291456 | tf_op jit(solution)/shard_map/dot_general | solution.py:92
  117.8 5.6 %fusion.80 = f32[768,3,4,64]{0,3,2,1:T(8,128)S(1)} fusion(bf16[768,2048,1,1]{0,1,3,2:T(8,128)(2,1)} %bitcast.124, bf16[3,4,64,2048]{3,2,1,0:T(8,128)(2,1)} %bitcast.125), kind=kOutput, calls=%fused_computation.115 | convolution fusion | flops 2415919104 | bytes 8650752 | tf_op jit(solution)/shard_map/dot_general | solution.py:92
  131.5 2.3 fusion.32
  133.9 4.0 %fusion.57 = f32[768,4,64]{0,2,1:T(8,128)S(1)} fusion(f32[4,768,768]{1,2,0:T(8,128)S(1)} %get-tuple-element.355, f32[4,768]{1,0:T(4,128)S(1)} %get-tuple-element.348, pred[768,768]{0,1:T(8,128)(4,1)S(1)} %copy-done.1, f32[768,4]{0,1:T(4,128)S(1)} %get-tuple-element.347, f32[768,4]{0,1:T(4,128)S(1)} %get-tuple-element.346, f32[768,3,4,64]{0,3,2,1:T(8,128)} %copy-done.2), kind=kOutput, calls=%fused_computation.60 | convolution fusion | flops 314179584 | bytes 11243520 | tf_op jit(solution)/shard_map/hqk,khd->qhd/dot_general | solution.py:37
  138.6 48.2 %while.21 = (s32[]{:T(128)}, f32[4,768]{1,0:T(4,128)S(1)}, f32[4,768]{1,0:T(4,128)S(1)}, f32[768,4,64]{0,2,1:T(8,128)S(1)}, s32[24]{0:T(128)S(1)}, /*index=5*/s3...) while((s32[]{:T(128)}, f32[4,768]{1,0:T(4,128)S(1)}, ...), condition=%wide.region_10.11_spmd.clone, body=%wide.region_7.10_spmd.clone.sunk | while | flops 635059200 | bytes 35984128 | solution.py:145
  145.4 3.0 %fusion.95 = f32[4,768]{1,0:T(4,128)S(1)} fusion(f32[4,768,768]{2,1,0:T(8,128)S(1)} %get-tuple-element.417, f32[4,768]{1,0:T(4,128)S(1)} %get-tuple-element.444, pred[768]{0:T(1024)(128)(4,1)S(1)} %fusion.93), kind=kLoop, calls=%fused_computation.9.clone.1 | loop fusion | flops 11793408 | bytes 9462528 | tf_op jit(solution)/shard_map/while/body/eval_jaxpr/reduce_sum | solution.py:36
  148.4 2.3 fusion.96
  157.4 3.0 %fusion.95 = f32[4,768]{1,0:T(4,128)S(1)} fusion(f32[4,768,768]{2,1,0:T(8,128)S(1)} %get-tuple-element.417, f32[4,768]{1,0:T(4,128)S(1)} %get-tuple-element.444, pred[768]{0:T(1024)(128)(4,1)S(1)} %fusion.93), kind=kLoop, calls=%fused_computation.9.clone.1 | loop fusion | flops 11793408 | bytes 9462528 | tf_op jit(solution)/shard_map/while/body/eval_jaxpr/reduce_sum | solution.py:36
  160.4 2.3 fusion.96
  169.4 3.0 %fusion.95 = f32[4,768]{1,0:T(4,128)S(1)} fusion(f32[4,768,768]{2,1,0:T(8,128)S(1)} %get-tuple-element.417, f32[4,768]{1,0:T(4,128)S(1)} %get-tuple-element.444, pred[768]{0:T(1024)(128)(4,1)S(1)} %fusion.93), kind=kLoop, calls=%fused_computation.9.clone.1 | loop fusion | flops 11793408 | bytes 9462528 | tf_op jit(solution)/shard_map/while/body/eval_jaxpr/reduce_sum | solution.py:36
  172.4 2.3 fusion.96
  181.4 3.0 %fusion.95 = f32[4,768]{1,0:T(4,128)S(1)} fusion(f32[4,768,768]{2,1,0:T(8,128)S(1)} %get-tuple-element.417, f32[4,768]{1,0:T(4,128)S(1)} %get-tuple-element.444, pred[768]{0:T(1024)(128)(4,1)S(1)} %fusion.93), kind=kLoop, calls=%fused_computation.9.clone.1 | loop fusion | flops 11793408 | bytes 9462528 | tf_op jit(solution)/shard_map/while/body/eval_jaxpr/reduce_sum | solution.py:36
  190.1 2.7 %pad_maximum_fusion = bf16[768,2,256]{2,1,0:T(2,128)(2,1)} fusion(bf16[768,1,256]{2,1,0:T(2,128)(2,1)S(1)} %copy.49, bf16[768,1,256]{2,1,0:T(2,128)(2,1)S(1)} %copy.48), kind=kLoop, calls=%fused_computation.67 | loop fusion | flops 1572864 | bytes 1572864 | tf_op jit(solution)/shard_map/stack | solution.py:104
  192.7 30.6 %all-gather.4.cloned.1.call-done = bf16[768,2048]{0,1:T(8,128)(2,1)} async-done(((bf16[768,256]{0,1:T(8,128)(2,1)}), bf16[768,2048]{0,1:T(8,128)(2,1)}) %all-gather.4.cloned.1.call-update) | async-done | bytes 3145744 | tf_op jit(solution)/shard_map/all_gather | solution.py:151
  223.3 3.9 %convolution_convert_fusion = bf16[768,256]{1,0:T(8,128)(2,1)} fusion(bf16[768,2048]{0,1:T(8,128)(2,1)} %all-gather.4.cloned.1.call-done, bf16[2048,1536]{1,0:T(8,128)(2,1)} %bitcast.122), kind=kOutput, calls=%fused_computation.61 | convolution fusion | flops 805502976 | bytes 4587520 | tf_op jit(solution)/shard_map/dot_general | solution.py:153
  (99 shorter events, 47.4 us)
Async XLA Ops:
  7.2 27.5 %copy-start.6 = (s32[16]{0:T(128)S(1)}, s32[16]{0:T(128)}, u32[]{:S(2)}) copy-start(s32[16]{0:T(128)} %param.21) | copy-start | bytes 196
  7.2 29.5 %copy-start.5 = (f32[2048]{0:T(1024)S(1)}, f32[2048]{0:T(1024)}, u32[]{:S(2)}) copy-start(f32[2048]{0:T(1024)} %param.13) | copy-start | bytes 24580
  7.2 30.2 %copy-start.7 = (s32[1,24]{1,0:T(1,128)S(1)}, s32[1,24]{1,0:T(1,128)}, u32[]{:S(2)}) copy-start(s32[1,24]{1,0:T(1,128)} %param.18) | copy-start | bytes 292
  7.2 101.3 %all-gather.6.cloned.1.call-start = ((), (), s32[]{:S(2)}) async-start(), calls=%async_computation.3 | async-start | bytes 6684672 | tf_op jit(solution)/shard_map/all_gather | solution.py:85
  23.4 48.2 %all-to-all-start = ((bf16[8,768,256]{2,1,0:T(8,128)(2,1)}), bf16[8,768,256]{2,1,0:T(8,128)(2,1)}, u32[]{:S(2)}, u32[]{:S(2)}) async-start(bf16[8,768,256]{2,1,0:T(8,128)(2,1)} %broadcast_in_dim.153), calls=%async_computation | async-start | bytes 6291456 | tf_op jit(solution)/shard_map/all_to_all | solution.py:47
  34.0 189.3 %all-gather.4.cloned.1.call-start = ((), (), s32[]{:S(2)}) async-start(), calls=%async_computation.2 | async-start | bytes 3538944 | tf_op jit(solution)/shard_map/all_gather | solution.py:151
  112.0 2.6 %copy-start = (bf16[4,16,32,1536]{3,2,1,0:T(8,128)(2,1)}, bf16[4,16,32,1536]{3,2,1,0:T(8,128)(2,1)S(1)}, u32[]{:S(2)}) copy-start(bf16[4,16,32,1536]{3,2,1,0:T(8,128)(2,1)S(1)} %copy.41) | copy-start | bytes 18874372
  123.4 2.9 %copy-start.2 = (f32[768,3,4,64]{0,3,2,1:T(8,128)}, f32[768,3,4,64]{0,3,2,1:T(8,128)S(1)}, u32[]{:S(2)}) copy-start(f32[768,3,4,64]{0,3,2,1:T(8,128)S(1)} %fusion.80) | copy-start | bytes 7077892
  123.5 5.6 %copy-start.1 = (pred[768,768]{0,1:T(8,128)(4,1)S(1)}, pred[768,768]{0,1:T(8,128)(4,1)}, u32[]{:S(2)}) copy-start(pred[768,768]{0,1:T(8,128)(4,1)} %iota_compare_fusion) | copy-start | bytes 1769476
  126.4 4.5 %copy-start.3 = (bf16[256,512]{0,1:T(8,128)(2,1)}, bf16[256,512]{0,1:T(8,128)(2,1)S(1)}, u32[]{:S(2)}) copy-start(bf16[256,512]{0,1:T(8,128)(2,1)S(1)} %copy.44) | copy-start | bytes 786436
  133.9 4.0 %copy-start.4 = (bf16[256,512]{0,1:T(8,128)(2,1)S(1)}, bf16[256,512]{0,1:T(8,128)(2,1)}, u32[]{:S(2)}) copy-start(bf16[256,512]{0,1:T(8,128)(2,1)} %copy-done.3) | copy-start | bytes 786436
Sparse Core Ops, SparseCore 0:
  20.7 87.7 all-gather.5
  187.7 35.5 all-gather.3
